TPU v7x, 32 devices: a whole 2x2x4 slice. The times are simulated.
32 devices in a mesh: req: 4 (over x, core), tok: 8 (over z, y).
Axes of the slice: x: 2, y: 2, z: 4, core: 2. Of those that a mesh axis runs over, the one named last changes fastest.
Arguments:
- queries: bfloat16 [8, 2048, 2048], P('req', 'tok'), may hold values from -16 to 16
- new_kv: bfloat16 [8, 2048, 256], P('req', 'tok'), may hold values from -6 to 6
- cache_kv: bfloat16 [8, 4096, 256], P('req', 'tok'), may hold values from -6 to 6
- residual: bfloat16 [8, 2048, 2048], P('req', 'tok'), may hold values from -24 to 24
- prefix_len: int32 [8], replicated, may hold values from 0 to 4096, as said below
- dest_map: int32 [8, 2048], P('req', 'tok'), may hold values from -1 to 4095, as said below
- w_out: bfloat16 [2048, 2048], replicated, may hold values from -0.125 to 0.125
- b_out: float32 [2048], replicated, may hold values from -4 to 4
- ln_gain: float32 [2048], replicated, may hold values from 0.1 to 1.9
- ln_bias: float32 [2048], replicated, may hold values from -4 to 4
- w_up: bfloat16 [2048, 8192], P(None, 'tok'), may hold values from -0.125 to 0.125
- b_up: float32 [8192], P('tok'), may hold values from -6 to 6
- w_down: bfloat16 [8192, 2048], P('tok'), may hold values from -0.0625 to 0.0625
- b_down: float32 [2048], replicated, may hold values from -4 to 4
Outputs:
- layer_out: bfloat16 [4096, 2048], P(('req', 'tok'))
Inputs may be any that keep to these rules, and one draw needn't show every extreme that they name: `prefix_len`: some request uses all 4096 cached positions. In each request the slots that are not -1 are its first n, with n from 128 to 2048; the n over all requests sum to 4096 and the largest is exactly 2048. These slots hold distinct rows of layer_out, every row held by exactly one of them. The live slots of one device's block of dest_map name at most 16 rows of any one device's block of layer_out.
All inputs are finite; a program needn't handle non-finite values.
Results may differ from a plain program's by a relative error of at most 0.012.
Values may be sent and summed in bfloat16 or wider, within the bound.
No kernel may reach another device: no remote copies, remote signals or barrier semaphores. Data moves between devices by JAX's collectives and lax.ppermute only.
A program may use at most 192 MiB of HBM per device.

v0:
```python
import math

import jax
import jax.numpy as jnp
from jax import lax
from jax.sharding import PartitionSpec as P

TOK_DEV = 128


neg_large = -1e30
ln_eps = 1e-05


def attend_block(
    state, block, block_start, queries_four, query_pos, own_prefix, shard_keys, shard_prefix, scale
):
    running_max, running_sum, accum = state
    count = block.shape[1]
    head_dim = queries_four.shape[-1]
    index_all = block_start + jnp.arange(count, dtype=jnp.int32)
    owner = index_all // shard_keys
    offset = index_all % shard_keys
    in_prefix = offset < shard_prefix
    prefix_pos = owner * shard_prefix + offset
    new_pos = owner * (shard_keys - shard_prefix) + offset - shard_prefix
    prefix_seen = prefix_pos[None, None, :] < own_prefix[:, None, None]
    new_seen = new_pos[None, None, :] <= query_pos[None, :, None]
    visible = jnp.where(in_prefix[None, None, :], prefix_seen, new_seen)[:, None, :, :]
    scores = (
        jnp.einsum(
            "rqhd,rkd->rhqk",
            queries_four,
            block[:, :, :head_dim],
            preferred_element_type=jnp.float32,
        )
        * scale
    )
    scores = jnp.where(visible, scores, neg_large)
    new_max = jnp.maximum(running_max, jnp.max(scores, axis=-1))
    probs = jnp.where(visible, jnp.exp(scores - new_max[..., None]), 0.0)
    factor = jnp.exp(running_max - new_max)
    new_sum = running_sum * factor + jnp.sum(probs, axis=-1)
    update = jnp.einsum(
        "rhqk,rkd->rhqd",
        probs.astype(jnp.bfloat16),
        block[:, :, head_dim:],
        preferred_element_type=jnp.float32,
    )
    return (new_max, new_sum, accum * factor[..., None] + update)


def project_rows(attended, residual_rows, w_out, b_out):
    total = (
        residual_rows.astype(jnp.float32)
        + jnp.dot(attended, w_out, preferred_element_type=jnp.float32)
        + b_out
    )
    return total.astype(jnp.bfloat16)


def per_device(
    queries,
    new_kv,
    cache_kv,
    residual,
    prefix_len,
    dest_map,
    w_out,
    b_out,
    ln_gain,
    ln_bias,
    w_up,
    b_up,
    w_down,
    b_down,
):
    group = lax.axis_index("req")
    member = lax.axis_index("tok")
    n_group = lax.axis_size("req")
    n_member = lax.axis_size("tok")
    devices = n_group * n_member
    req_dev, slot_dev, width = queries.shape
    head_dim = new_kv.shape[2] // 2
    heads = width // head_dim
    prefix_dev = cache_kv.shape[1]
    shard_keys = prefix_dev + slot_dev
    own_prefix = lax.dynamic_slice_in_dim(prefix_len, group * req_dev, req_dev)
    query_pos = member * slot_dev + jnp.arange(slot_dev, dtype=jnp.int32)
    queries_four = queries.reshape(req_dev, slot_dev, heads, head_dim)
    scale = 1.0 / math.sqrt(head_dim)
    local_keys = jnp.concatenate([cache_kv, new_kv], axis=1)

    def attend(state, block, block_start):
        return attend_block(
            state,
            block,
            block_start,
            queries_four,
            query_pos,
            own_prefix,
            shard_keys,
            prefix_dev,
            scale,
        )

    initial = (
        jnp.full((req_dev, heads, slot_dev), neg_large, jnp.float32),
        jnp.zeros((req_dev, heads, slot_dev), jnp.float32),
        jnp.zeros((req_dev, heads, slot_dev, head_dim), jnp.float32),
    )
    state = initial
    piece = lax.all_gather(local_keys, "tok", axis=1, tiled=True)
    count = piece.shape[1]
    number = count // shard_keys
    blocks = jnp.moveaxis(piece.reshape(req_dev, number, shard_keys, piece.shape[2]), 1, 0)

    def one_block(carry, item):
        block, index = item
        return (attend(carry, block, index * shard_keys), None)

    state, unused = lax.scan(one_block, state, (blocks, jnp.arange(number, dtype=jnp.int32)))
    running_max, running_sum, accum = state
    attended = (accum / running_sum[..., None]).astype(jnp.bfloat16)
    slots = req_dev * slot_dev
    attended = jnp.transpose(attended, (0, 2, 1, 3)).reshape(slots, width)
    residual_flat = residual.reshape(slots, width)
    capacity = (slots + devices - 1) // devices
    target = dest_map.reshape(slots)
    is_live = target >= 0
    peer = jnp.where(is_live, target // TOK_DEV, devices)
    onehot = (peer[:, None] == jnp.arange(devices, dtype=jnp.int32)[None, :]).astype(jnp.int32)
    position = jnp.sum((jnp.cumsum(onehot, axis=0) - 1) * onehot, axis=1)
    where_to = jnp.where(is_live, peer * capacity + position, devices * capacity)
    row_ids = (
        jnp.full((devices * capacity,), -1, jnp.int32)
        .at[where_to]
        .set(target % TOK_DEV, mode="drop")
    )
    payload = jnp.stack([attended, residual_flat], axis=1)
    layers = payload.shape[1]
    send_rows = (
        jnp.zeros((devices * capacity, layers, width), jnp.bfloat16)
        .at[where_to]
        .set(payload, mode="drop")
    )
    rows_in, ids_in = (
        lax.all_to_all(
            send_rows.reshape(devices, capacity, layers, width),
            ("req", "tok"),
            split_axis=0,
            concat_axis=0,
            tiled=True,
        ),
        lax.all_to_all(
            row_ids.reshape(devices, capacity),
            ("req", "tok"),
            split_axis=0,
            concat_axis=0,
            tiled=True,
        ),
    )
    rows_in = rows_in.reshape(devices * capacity, layers, width)
    ids_in = ids_in.reshape(devices * capacity)
    landing = jnp.where(ids_in >= 0, ids_in, TOK_DEV)
    even_rows = (
        jnp.zeros((TOK_DEV, layers, width), jnp.bfloat16).at[landing].set(rows_in, mode="drop")
    )
    hidden_state = project_rows(even_rows[:, 0], even_rows[:, 1], w_out, b_out)
    state_f = hidden_state.astype(jnp.float32)
    mean = jnp.mean(state_f, axis=-1, keepdims=True)
    centered = state_f - mean
    variance = jnp.mean(centered * centered, axis=-1, keepdims=True)
    normed = (centered * lax.rsqrt(variance + ln_eps) * ln_gain + ln_bias).astype(jnp.bfloat16)
    units = jax.nn.gelu(
        jnp.dot(
            lax.all_gather(normed, "tok", axis=0, tiled=True),
            w_up,
            preferred_element_type=jnp.float32,
        )
        + b_up,
        approximate=True,
    )
    terms = jnp.dot(units.astype(jnp.bfloat16), w_down, preferred_element_type=jnp.float32)
    summed = lax.psum_scatter(
        terms.astype(jnp.bfloat16), "tok", scatter_dimension=0, tiled=True
    ).astype(jnp.float32)
    return (state_f + summed + b_down).astype(jnp.bfloat16)


def solution(mesh):
    in_specs = (
        P("req", "tok", None),
        P("req", "tok", None),
        P("req", "tok", None),
        P("req", "tok", None),
        P(),
        P("req", "tok"),
        P(),
        P(),
        P(),
        P(),
        P(None, "tok"),
        P("tok"),
        P("tok", None),
        P(),
    )
    out_specs = P(("req", "tok"), None)
    return jax.shard_map(
        per_device, mesh=mesh, in_specs=in_specs, out_specs=out_specs, check_vma=False
    )
```

profile of v0, /device:TPU:0, one launch (start us, length us, event | category | flops | bytes accessed | tf_op | source)
XLA Modules:
  0.0 848.0 jit_solution(4371409342720919751)
XLA Ops:
  28.8 82.8 %all-gather.3.cloned.1.call-done = bf16[2,6144,256]{2,1,0:T(8,128)(2,1)} async-done(((bf16[2,768,256]{2,1,0:T(8,128)(2,1)}), bf16[2,6144,256]{2,1,0:T(8,128)(2,1)}) %all-gather.3.cloned.1.call-update) | async-done | bytes 6291472 | tf_op jit(solution)/shard_map/all_gather | solution.py:113
  111.6 320.0 %while.17 = (s32[]{:T(128)}, f32[2,16,256]{2,1,0:T(8,128)S(1)}, f32[2,16,256]{2,1,0:T(8,128)S(1)}, f32[2,16,256,128]{3,2,1,0:T(8,128)}, s32[8]{0:T(128)S(1)}, /*...) while((s32[]{:T(128)}, f32[2,16,256]{2,1,0:T(8,128)S(1)}, ...), condition=%wide.region_7.8_spmd.clone, body=%wide.region_4.7_spmd.clone.sunk | while | flops 3306812672 | bytes 90852008 | solution.py:122
  125.3 11.4 %fusion.78 = f32[2,16,256]{2,1,0:T(8,128)S(1)} fusion(f32[2,768,256,16]{2,1,3,0:T(8,128)} %get-tuple-element.279, f32[2,16,256]{2,1,0:T(8,128)S(1)} %select_maximum_fusion.2, pred[2,256,768]{1,2,0:T(8,128)(4,1)S(1)} %broadcast_select_fusion.2), kind=kLoop, calls=%fused_computation.8.clone.1 | loop fusion | flops 31449088 | bytes 25624576 | tf_op jit(solution)/shard_map/while/body/eval_jaxpr/reduce_sum | solution.py:43
  136.8 14.3 %fusion.80 = f32[2,16,256,128]{3,2,1,0:T(8,128)} fusion(f32[2,16,256,128]{3,2,1,0:T(8,128)} %get-tuple-element.297, f32[2,16,256]{2,1,0:T(8,128)S(1)} %get-tuple-element.281, pred[]{:T(512)S(6)} %compare.19, f32[2,768,256,16]{2,1,3,0:T(8,128)} %get-tuple-element.279, f32[2,16,256]{2,1,0:T(8,128)S(1)} %select_maximum_fusion.2, ...), kind=kOutput, calls=%fused_computation.12.clone.1 | convolution fusion | flops 1645215744 | bytes 34406400 | tf_op jit(solution)/shard_map/while/body/eval_jaxpr/rhqk,rkd->rhqd/dot_general | solution.py:44
  164.8 11.4 %fusion.78 = f32[2,16,256]{2,1,0:T(8,128)S(1)} fusion(f32[2,768,256,16]{2,1,3,0:T(8,128)} %get-tuple-element.279, f32[2,16,256]{2,1,0:T(8,128)S(1)} %select_maximum_fusion.2, pred[2,256,768]{1,2,0:T(8,128)(4,1)S(1)} %broadcast_select_fusion.2), kind=kLoop, calls=%fused_computation.8.clone.1 | loop fusion | flops 31449088 | bytes 25624576 | tf_op jit(solution)/shard_map/while/body/eval_jaxpr/reduce_sum | solution.py:43
  176.3 14.9 %fusion.80 = f32[2,16,256,128]{3,2,1,0:T(8,128)} fusion(f32[2,16,256,128]{3,2,1,0:T(8,128)} %get-tuple-element.297, f32[2,16,256]{2,1,0:T(8,128)S(1)} %get-tuple-element.281, pred[]{:T(512)S(6)} %compare.19, f32[2,768,256,16]{2,1,3,0:T(8,128)} %get-tuple-element.279, f32[2,16,256]{2,1,0:T(8,128)S(1)} %select_maximum_fusion.2, ...), kind=kOutput, calls=%fused_computation.12.clone.1 | convolution fusion | flops 1645215744 | bytes 34406400 | tf_op jit(solution)/shard_map/while/body/eval_jaxpr/rhqk,rkd->rhqd/dot_general | solution.py:44
  204.9 11.4 %fusion.78 = f32[2,16,256]{2,1,0:T(8,128)S(1)} fusion(f32[2,768,256,16]{2,1,3,0:T(8,128)} %get-tuple-element.279, f32[2,16,256]{2,1,0:T(8,128)S(1)} %select_maximum_fusion.2, pred[2,256,768]{1,2,0:T(8,128)(4,1)S(1)} %broadcast_select_fusion.2), kind=kLoop, calls=%fused_computation.8.clone.1 | loop fusion | flops 31449088 | bytes 25624576 | tf_op jit(solution)/shard_map/while/body/eval_jaxpr/reduce_sum | solution.py:43
  216.3 14.9 %fusion.80 = f32[2,16,256,128]{3,2,1,0:T(8,128)} fusion(f32[2,16,256,128]{3,2,1,0:T(8,128)} %get-tuple-element.297, f32[2,16,256]{2,1,0:T(8,128)S(1)} %get-tuple-element.281, pred[]{:T(512)S(6)} %compare.19, f32[2,768,256,16]{2,1,3,0:T(8,128)} %get-tuple-element.279, f32[2,16,256]{2,1,0:T(8,128)S(1)} %select_maximum_fusion.2, ...), kind=kOutput, calls=%fused_computation.12.clone.1 | convolution fusion | flops 1645215744 | bytes 34406400 | tf_op jit(solution)/shard_map/while/body/eval_jaxpr/rhqk,rkd->rhqd/dot_general | solution.py:44
  245.0 11.4 %fusion.78 = f32[2,16,256]{2,1,0:T(8,128)S(1)} fusion(f32[2,768,256,16]{2,1,3,0:T(8,128)} %get-tuple-element.279, f32[2,16,256]{2,1,0:T(8,128)S(1)} %select_maximum_fusion.2, pred[2,256,768]{1,2,0:T(8,128)(4,1)S(1)} %broadcast_select_fusion.2), kind=kLoop, calls=%fused_computation.8.clone.1 | loop fusion | flops 31449088 | bytes 25624576 | tf_op jit(solution)/shard_map/while/body/eval_jaxpr/reduce_sum | solution.py:43
  256.4 14.9 %fusion.80 = f32[2,16,256,128]{3,2,1,0:T(8,128)} fusion(f32[2,16,256,128]{3,2,1,0:T(8,128)} %get-tuple-element.297, f32[2,16,256]{2,1,0:T(8,128)S(1)} %get-tuple-element.281, pred[]{:T(512)S(6)} %compare.19, f32[2,768,256,16]{2,1,3,0:T(8,128)} %get-tuple-element.279, f32[2,16,256]{2,1,0:T(8,128)S(1)} %select_maximum_fusion.2, ...), kind=kOutput, calls=%fused_computation.12.clone.1 | convolution fusion | flops 1645215744 | bytes 34406400 | tf_op jit(solution)/shard_map/while/body/eval_jaxpr/rhqk,rkd->rhqd/dot_general | solution.py:44
  285.1 11.4 %fusion.78 = f32[2,16,256]{2,1,0:T(8,128)S(1)} fusion(f32[2,768,256,16]{2,1,3,0:T(8,128)} %get-tuple-element.279, f32[2,16,256]{2,1,0:T(8,128)S(1)} %select_maximum_fusion.2, pred[2,256,768]{1,2,0:T(8,128)(4,1)S(1)} %broadcast_select_fusion.2), kind=kLoop, calls=%fused_computation.8.clone.1 | loop fusion | flops 31449088 | bytes 25624576 | tf_op jit(solution)/shard_map/while/body/eval_jaxpr/reduce_sum | solution.py:43
  296.5 14.9 %fusion.80 = f32[2,16,256,128]{3,2,1,0:T(8,128)} fusion(f32[2,16,256,128]{3,2,1,0:T(8,128)} %get-tuple-element.297, f32[2,16,256]{2,1,0:T(8,128)S(1)} %get-tuple-element.281, pred[]{:T(512)S(6)} %compare.19, f32[2,768,256,16]{2,1,3,0:T(8,128)} %get-tuple-element.279, f32[2,16,256]{2,1,0:T(8,128)S(1)} %select_maximum_fusion.2, ...), kind=kOutput, calls=%fused_computation.12.clone.1 | convolution fusion | flops 1645215744 | bytes 34406400 | tf_op jit(solution)/shard_map/while/body/eval_jaxpr/rhqk,rkd->rhqd/dot_general | solution.py:44
  325.1 11.4 %fusion.78 = f32[2,16,256]{2,1,0:T(8,128)S(1)} fusion(f32[2,768,256,16]{2,1,3,0:T(8,128)} %get-tuple-element.279, f32[2,16,256]{2,1,0:T(8,128)S(1)} %select_maximum_fusion.2, pred[2,256,768]{1,2,0:T(8,128)(4,1)S(1)} %broadcast_select_fusion.2), kind=kLoop, calls=%fused_computation.8.clone.1 | loop fusion | flops 31449088 | bytes 25624576 | tf_op jit(solution)/shard_map/while/body/eval_jaxpr/reduce_sum | solution.py:43
  336.6 14.9 %fusion.80 = f32[2,16,256,128]{3,2,1,0:T(8,128)} fusion(f32[2,16,256,128]{3,2,1,0:T(8,128)} %get-tuple-element.297, f32[2,16,256]{2,1,0:T(8,128)S(1)} %get-tuple-element.281, pred[]{:T(512)S(6)} %compare.19, f32[2,768,256,16]{2,1,3,0:T(8,128)} %get-tuple-element.279, f32[2,16,256]{2,1,0:T(8,128)S(1)} %select_maximum_fusion.2, ...), kind=kOutput, calls=%fused_computation.12.clone.1 | convolution fusion | flops 1645215744 | bytes 34406400 | tf_op jit(solution)/shard_map/while/body/eval_jaxpr/rhqk,rkd->rhqd/dot_general | solution.py:44
  365.2 11.4 %fusion.78 = f32[2,16,256]{2,1,0:T(8,128)S(1)} fusion(f32[2,768,256,16]{2,1,3,0:T(8,128)} %get-tuple-element.279, f32[2,16,256]{2,1,0:T(8,128)S(1)} %select_maximum_fusion.2, pred[2,256,768]{1,2,0:T(8,128)(4,1)S(1)} %broadcast_select_fusion.2), kind=kLoop, calls=%fused_computation.8.clone.1 | loop fusion | flops 31449088 | bytes 25624576 | tf_op jit(solution)/shard_map/while/body/eval_jaxpr/reduce_sum | solution.py:43
  376.7 14.9 %fusion.80 = f32[2,16,256,128]{3,2,1,0:T(8,128)} fusion(f32[2,16,256,128]{3,2,1,0:T(8,128)} %get-tuple-element.297, f32[2,16,256]{2,1,0:T(8,128)S(1)} %get-tuple-element.281, pred[]{:T(512)S(6)} %compare.19, f32[2,768,256,16]{2,1,3,0:T(8,128)} %get-tuple-element.279, f32[2,16,256]{2,1,0:T(8,128)S(1)} %select_maximum_fusion.2, ...), kind=kOutput, calls=%fused_computation.12.clone.1 | convolution fusion | flops 1645215744 | bytes 34406400 | tf_op jit(solution)/shard_map/while/body/eval_jaxpr/rhqk,rkd->rhqd/dot_general | solution.py:44
  405.3 11.4 %fusion.78 = f32[2,16,256]{2,1,0:T(8,128)S(1)} fusion(f32[2,768,256,16]{2,1,3,0:T(8,128)} %get-tuple-element.279, f32[2,16,256]{2,1,0:T(8,128)S(1)} %select_maximum_fusion.2, pred[2,256,768]{1,2,0:T(8,128)(4,1)S(1)} %broadcast_select_fusion.2), kind=kLoop, calls=%fused_computation.8.clone.1 | loop fusion | flops 31449088 | bytes 25624576 | tf_op jit(solution)/shard_map/while/body/eval_jaxpr/reduce_sum | solution.py:43
  416.7 14.9 %fusion.80 = f32[2,16,256,128]{3,2,1,0:T(8,128)} fusion(f32[2,16,256,128]{3,2,1,0:T(8,128)} %get-tuple-element.297, f32[2,16,256]{2,1,0:T(8,128)S(1)} %get-tuple-element.281, pred[]{:T(512)S(6)} %compare.19, f32[2,768,256,16]{2,1,3,0:T(8,128)} %get-tuple-element.279, f32[2,16,256]{2,1,0:T(8,128)S(1)} %select_maximum_fusion.2, ...), kind=kOutput, calls=%fused_computation.12.clone.1 | convolution fusion | flops 1645215744 | bytes 34406400 | tf_op jit(solution)/shard_map/while/body/eval_jaxpr/rhqk,rkd->rhqd/dot_general | solution.py:44
  451.2 64.2 %scatter_fusion = bf16[512,2,2048]{2,1,0:T(2,128)(2,1)} fusion(bf16[512,2,2048]{2,1,0:T(2,128)(2,1)} %broadcast_in_dim.112, s32[512]{0:T(512)S(1)} %bitcast.107, bf16[512,2,2048]{2,1,0:T(2,128)(2,1)} %copy.39), kind=kCustom, calls=%fused_computation.1 | custom fusion | bytes 12584960 | tf_op jit(solution)/shard_map/scatter | solution.py:145
  521.1 93.9 %all-to-all-done.1 = bf16[32,16,2,2048]{3,2,1,0:T(2,128)(2,1)} async-done(((bf16[32,16,2,2048]{3,2,1,0:T(2,128)(2,1)}), bf16[32,16,2,2048]{3,2,1,0:T(2,128)(2,1)}, u32[]{:S(2)}, u32[]{:S(2)}) %all-to-all-start.1) | async-done | bytes 4194336 | tf_op jit(solution)/shard_map/all_to_all | solution.py:148
  615.5 43.0 %scatter_fusion.1 = bf16[128,2,2048]{2,1,0:T(2,128)(2,1)S(1)} fusion(bf16[128,2,2048]{2,1,0:T(2,128)(2,1)S(1)} %broadcast_in_dim.106, s32[512]{0:T(512)S(1)} %bitcast.108, bf16[512,2,2048]{2,1,0:T(2,128)(2,1)} %bitcast.11), kind=kCustom, calls=%fused_computation.2 | custom fusion | bytes 12584960 | tf_op jit(solution)/shard_map/scatter | solution.py:167
  667.0 70.8 %all-gather.5.cloned.1.call-done = bf16[1024,2048]{1,0:T(8,128)(2,1)} async-done(((bf16[128,2048]{1,0:T(8,128)(2,1)}), bf16[1024,2048]{1,0:T(8,128)(2,1)}) %all-gather.5.cloned.1.call-update) | async-done | bytes 4194320 | tf_op jit(solution)/shard_map/all_gather | solution.py:177
  737.7 15.2 %convolution_convert_fusion = bf16[1024,2048]{1,0:T(8,128)(2,1)} fusion(bf16[1024,2048]{1,0:T(8,128)(2,1)} %param.28, f32[1024]{0:T(1024)S(1)} %copy-done.7, bf16[1024,2048]{1,0:T(8,128)(2,1)} %all-gather.5.cloned.1.call-done, bf16[2048,1024]{1,0:T(8,128)(2,1)} %param.26), kind=kOutput, calls=%fused_computation.51 | convolution fusion | flops 8602517504 | bytes 16781312 | tf_op jit(solution)/shard_map/dot_general | solution.py:184
  753.0 86.5 %reduce-scatter.2.cloned.1.call-done = bf16[128,2048]{1,0:T(8,128)(2,1)} async-done(((bf16[1024,2048]{1,0:T(8,128)(2,1)}), bf16[128,2048]{1,0:T(8,128)(2,1)}) %reduce-scatter.2.cloned.1.call-update) | async-done | bytes 524304 | tf_op jit(solution)/shard_map/reduce_scatter | solution.py:185
  (163 shorter events, 162.3 us)
Async XLA Ops:
  6.5 16.5 %copy-start = (bf16[2,256,2048]{2,1,0:T(8,128)(2,1)S(1)}, bf16[2,256,2048]{2,1,0:T(8,128)(2,1)}, u32[]{:S(2)}) copy-start(bf16[2,256,2048]{2,1,0:T(8,128)(2,1)} %param.16) | copy-start | bytes 6291460
  6.5 105.1 %all-gather.3.cloned.1.call-start = ((), (), s32[]{:S(2)}) async-start(), calls=%async_computation.3 | async-start | bytes 7077888 | tf_op jit(solution)/shard_map/all_gather | solution.py:113
  12.5 16.2 %copy-start.5 = (s32[512,1]{0,1:T(1,128)}, s32[512,1]{0,1:T(1,128)S(1)}, u32[]{:S(2)}) copy-start(s32[512,1]{0,1:T(1,128)S(1)} %compare_select_fusion.2) | copy-start | bytes 6148
  15.6 499.8 %all-to-all-start = ((s32[32,1,16]{2,1,0:T(1,128)}), s32[32,1,16]{2,1,0:T(1,128)}, u32[]{:S(2)}, u32[]{:S(2)}) async-start(s32[32,1,16]{2,1,0:T(1,128)} %bitcast.3), calls=%async_computation | async-start | bytes 32768 | tf_op jit(solution)/shard_map/all_to_all | solution.py:155
  23.1 5.6 copy-start.8
  447.1 4.1 copy-start.6
  515.4 99.5 %all-to-all-start.1 = ((bf16[32,16,2,2048]{3,2,1,0:T(2,128)(2,1)}), bf16[32,16,2,2048]{3,2,1,0:T(2,128)(2,1)}, u32[]{:S(2)}, u32[]{:S(2)}) async-start(bf16[32,16,2,2048]{3,2,1,0:T(2,128)(2,1)} %bitcast.97), calls=%async_computation.1 | async-start | bytes 8388608 | tf_op jit(solution)/shard_map/all_to_all | solution.py:148
  519.0 218.8 %all-gather.5.cloned.1.call-start = ((), (), s32[]{:S(2)}) async-start(), calls=%async_computation.4 | async-start | bytes 4718592 | tf_op jit(solution)/shard_map/all_gather | solution.py:177
  658.5 1.5 copy-start.1
  660.1 5.8 copy-start.2
  660.1 5.8 copy-start.3
  660.1 77.7 %copy-start.7 = (f32[1024]{0:T(1024)S(1)}, f32[1024]{0:T(1024)}, u32[]{:S(2)}) copy-start(f32[1024]{0:T(1024)} %param.27) | copy-start | bytes 12292
  666.9 172.6 %reduce-scatter.2.cloned.1.call-start = ((), (), s32[]{:S(2)}) async-start(), calls=%async_computation.5 | async-start | bytes 4718592 | tf_op jit(solution)/shard_map/reduce_scatter | solution.py:185
  753.0 86.5 %copy-start.4 = (f32[2048]{0:T(1024)S(1)}, f32[2048]{0:T(1024)}, u32[]{:S(2)}) copy-start(f32[2048]{0:T(1024)} %param.29) | copy-start | bytes 24580
Sparse Core Ops, SparseCore 0:
  9.6 101.9 all-gather.2
  667.0 70.6 all-gather.4
  753.1 86.3 reduce-scatter.1
where the time goes:
time: 850 us; the launch traced here: 848 us
  waiting for transfers between devices  334 us (39%)
  matrix products  221 us (26%)
  local copies, waits for them, and re-layouts  150 us (18%)
  other arithmetic  112 us (13%)
  between operations  13.3 us (2%)
  starting transfers between devices  11.1 us (1%)
    dot_general x8, matrix products, attend_block(): jnp.einsum('rhqk,rkd->rhqd', probs.astype(jnp.bfloat16), block[:, :, head...  119 us
    all_to_all x1, waiting for transfers between devices, per_device(): lax.all_to_all(send_rows.reshape(devices, capacity, layers, width), ('req...  93.9 us
    reduce_sum x8, other arithmetic, attend_block(): new_sum = running_sum * factor + jnp.sum(probs, axis=-1)  91.3 us
    reduce_scatter x1, waiting for transfers between devices, per_device(): lax.psum_scatter(terms.astype(jnp.bfloat16), 'tok', scatter_dimension=0,...  86.5 us
    all_gather x1, waiting for transfers between devices, per_device(): piece = lax.all_gather(local_keys, 'tok', axis=1, tiled=True)  82.8 us
    dot_general x8, matrix products, attend_block(): jnp.einsum('rqhd,rkd->rhqk', queries_four, block[:, :, :head_dim], prefer...  82 us
    all_gather x1, waiting for transfers between devices, per_device(): lax.all_gather(normed, 'tok', axis=0, tiled=True)  70.8 us
    scatter x1, local copies, waits for them, and re-layouts, per_device(): send_rows = jnp.zeros((devices * capacity, layers, width), jnp.bfloat16)....  64.2 us
  transfers between devices with their start and end apart: 5, of which 4 were waited for; matrix products, arithmetic and copies ran while one was open for 49% of the time, Pallas kernels for 0%

commit v1 on v0

v1 whole, which is shorter than its diff:
```python
import functools
import math

import jax
import jax.numpy as jnp
from jax import lax
from jax.experimental import pallas as pl
from jax.experimental.pallas import tpu as pltpu
from jax.sharding import PartitionSpec as P

TOK_DEV = 128


neg_large = -1e30
ln_eps = 1e-05


def flash_kernel(
    scal_ref,
    q_ref,
    ck_ref,
    nk_ref,
    o_ref,
    m_sc,
    l_sc,
    acc_sc,
    *,
    tq,
    tk,
    heads,
    head_dim,
    n_cache,
    n_req,
    scale,
):
    r = pl.program_id(0)
    qi = pl.program_id(1)
    ki = pl.program_id(2)
    prefix = scal_ref[r]
    live = scal_ref[n_req + r]
    base = scal_ref[2 * n_req]
    spt = tq // heads
    tile_lo = qi * spt
    tile_live = tile_lo < live
    q_lo = base + tile_lo
    q_hi = q_lo + spt - 1

    @pl.when(ki == 0)
    def _init():
        m_sc[...] = jnp.full(m_sc.shape, neg_large, jnp.float32)
        l_sc[...] = jnp.zeros(l_sc.shape, jnp.float32)
        acc_sc[...] = jnp.zeros(acc_sc.shape, jnp.float32)

    def step(kv_ref, mask_fn):
        kv = kv_ref[0]
        k = kv[:, :head_dim]
        v = kv[:, head_dim:]
        s = (
            lax.dot_general(
                q_ref[0], k, (((1,), (1,)), ((), ())), preferred_element_type=jnp.float32
            )
            * scale
        )
        mask = None
        if mask_fn is not None:
            mask = mask_fn()
            s = jnp.where(mask, s, neg_large)
        m_prev = m_sc[...]
        m_new = jnp.maximum(m_prev, jnp.max(s, axis=-1, keepdims=True))
        p = jnp.exp(s - m_new)
        if mask is not None:
            p = jnp.where(mask, p, 0.0)
        alpha = jnp.exp(m_prev - m_new)
        l_sc[...] = alpha * l_sc[...] + jnp.sum(p, axis=-1, keepdims=True)
        acc_sc[...] = alpha * acc_sc[...] + jnp.dot(
            p.astype(jnp.bfloat16), v, preferred_element_type=jnp.float32
        )
        m_sc[...] = m_new

    is_cache = ki < n_cache
    kc = ki * tk
    kn = (ki - n_cache) * tk
    run_cache = is_cache & tile_live & (kc < prefix)
    full_cache = kc + tk <= prefix
    run_new = jnp.logical_not(is_cache) & tile_live & (kn <= q_hi)
    full_new = kn + tk - 1 <= q_lo

    def cache_mask():
        col = lax.broadcasted_iota(jnp.int32, (tq, tk), 1) + kc
        return col < prefix

    def new_mask():
        col = lax.broadcasted_iota(jnp.int32, (tq, tk), 1) + kn
        row = lax.broadcasted_iota(jnp.int32, (tq, tk), 0) // heads + q_lo
        return col <= row

    @pl.when(run_cache & full_cache)
    def _c_full():
        step(ck_ref, None)

    @pl.when(run_cache & jnp.logical_not(full_cache))
    def _c_part():
        step(ck_ref, cache_mask)

    @pl.when(run_new & full_new)
    def _n_full():
        step(nk_ref, None)

    @pl.when(run_new & jnp.logical_not(full_new))
    def _n_part():
        step(nk_ref, new_mask)

    @pl.when(ki == pl.num_programs(2) - 1)
    def _fin():
        l = l_sc[...]
        safe = jnp.where(l > 0, l, 1.0)
        out = jnp.where(l > 0, acc_sc[...] / safe, 0.0)
        o_ref[0] = out.astype(o_ref.dtype)


def flash_attention(q, ck, nk, scal, heads, tq, tk):
    n_req, rows, head_dim = q.shape
    n_cache = ck.shape[1] // tk
    n_new = nk.shape[1] // tk
    spt = tq // heads
    scale = 1.0 / math.sqrt(head_dim)

    def q_map(r, qi, ki, s):
        return (r, qi, 0)

    def c_map(r, qi, ki, s):
        last = jnp.maximum((s[r] + tk - 1) // tk - 1, 0)
        return (r, jnp.minimum(ki, last), 0)

    def n_map(r, qi, ki, s):
        q_hi = s[2 * n_req] + (qi + 1) * spt - 1
        last = jnp.minimum(q_hi // tk, n_new - 1)
        return (r, jnp.clip(ki - n_cache, 0, last), 0)

    kernel = functools.partial(
        flash_kernel,
        tq=tq,
        tk=tk,
        heads=heads,
        head_dim=head_dim,
        n_cache=n_cache,
        n_req=n_req,
        scale=scale,
    )
    grid_spec = pltpu.PrefetchScalarGridSpec(
        num_scalar_prefetch=1,
        grid=(n_req, rows // tq, n_cache + n_new),
        in_specs=[
            pl.BlockSpec((1, tq, head_dim), q_map),
            pl.BlockSpec((1, tk, ck.shape[2]), c_map),
            pl.BlockSpec((1, tk, nk.shape[2]), n_map),
        ],
        out_specs=pl.BlockSpec((1, tq, head_dim), q_map),
        scratch_shapes=[
            pltpu.VMEM((tq, 1), jnp.float32),
            pltpu.VMEM((tq, 1), jnp.float32),
            pltpu.VMEM((tq, head_dim), jnp.float32),
        ],
    )
    return pl.pallas_call(
        kernel,
        grid_spec=grid_spec,
        out_shape=jax.ShapeDtypeStruct((n_req, rows, head_dim), jnp.bfloat16),
    )(scal, q, ck, nk)


def per_device(
    queries,
    new_kv,
    cache_kv,
    residual,
    prefix_len,
    dest_map,
    w_out,
    b_out,
    ln_gain,
    ln_bias,
    w_up,
    b_up,
    w_down,
    b_down,
):
    group = lax.axis_index("req")
    member = lax.axis_index("tok")
    n_group = lax.axis_size("req")
    n_member = lax.axis_size("tok")
    devices = n_group * n_member
    req_dev, slot_dev, width = queries.shape
    head_dim = new_kv.shape[2] // 2
    heads = width // head_dim
    own_prefix = lax.dynamic_slice_in_dim(prefix_len, group * req_dev, req_dev)
    live_count = jnp.sum((dest_map >= 0).astype(jnp.int32), axis=1)
    base = (member * slot_dev).astype(jnp.int32)
    rows = slot_dev * heads
    tq = min(1024, rows)
    tk = 512
    q_flat = queries.reshape(req_dev, rows, head_dim)

    outs = []
    for r in range(req_dev):
        ck = lax.all_gather(cache_kv[r], "tok", axis=0, tiled=True)
        nk = lax.all_gather(new_kv[r], "tok", axis=0, tiled=True)
        scal = jnp.stack([own_prefix[r], live_count[r], base]).astype(jnp.int32)
        outs.append(
            flash_attention(q_flat[r : r + 1], ck[None], nk[None], scal, heads, tq, tk)
        )
    attended = jnp.concatenate(outs, axis=0)
    slots = req_dev * slot_dev
    attended = attended.reshape(slots, width)
    residual_flat = residual.reshape(slots, width)
    hidden_all = (
        residual_flat.astype(jnp.float32)
        + jnp.dot(attended, w_out, preferred_element_type=jnp.float32)
        + b_out
    ).astype(jnp.bfloat16)

    capacity = (slots + devices - 1) // devices
    target = dest_map.reshape(slots)
    is_live = target >= 0
    peer = jnp.where(is_live, target // TOK_DEV, devices)
    onehot = (peer[:, None] == jnp.arange(devices, dtype=jnp.int32)[None, :]).astype(jnp.int32)
    position = jnp.sum((jnp.cumsum(onehot, axis=0) - 1) * onehot, axis=1)
    where_to = jnp.where(is_live, peer * capacity + position, devices * capacity)
    send_slots = devices * capacity
    pick = (
        where_to[None, :] == jnp.arange(send_slots, dtype=jnp.int32)[:, None]
    ).astype(jnp.bfloat16)
    send_rows = jnp.dot(pick, hidden_all, preferred_element_type=jnp.float32).astype(
        jnp.bfloat16
    )
    row_ids = jnp.sum(
        jnp.where(
            where_to[None, :] == jnp.arange(send_slots, dtype=jnp.int32)[:, None],
            (target % TOK_DEV)[None, :] + 1,
            0,
        ),
        axis=1,
    ) - 1
    rows_in = lax.all_to_all(
        send_rows.reshape(devices, capacity, width),
        ("req", "tok"),
        split_axis=0,
        concat_axis=0,
        tiled=True,
    ).reshape(send_slots, width)
    ids_in = lax.all_to_all(
        row_ids.reshape(devices, capacity),
        ("req", "tok"),
        split_axis=0,
        concat_axis=0,
        tiled=True,
    ).reshape(send_slots)
    land = (ids_in[None, :] == jnp.arange(TOK_DEV, dtype=jnp.int32)[:, None]).astype(
        jnp.bfloat16
    )
    hidden_state = jnp.dot(land, rows_in, preferred_element_type=jnp.float32).astype(
        jnp.bfloat16
    )
    state_f = hidden_state.astype(jnp.float32)
    mean = jnp.mean(state_f, axis=-1, keepdims=True)
    centered = state_f - mean
    variance = jnp.mean(centered * centered, axis=-1, keepdims=True)
    normed = (centered * lax.rsqrt(variance + ln_eps) * ln_gain + ln_bias).astype(jnp.bfloat16)
    units = jax.nn.gelu(
        jnp.dot(
            lax.all_gather(normed, "tok", axis=0, tiled=True),
            w_up,
            preferred_element_type=jnp.float32,
        )
        + b_up,
        approximate=True,
    )
    terms = jnp.dot(units.astype(jnp.bfloat16), w_down, preferred_element_type=jnp.float32)
    summed = lax.psum_scatter(
        terms.astype(jnp.bfloat16), "tok", scatter_dimension=0, tiled=True
    ).astype(jnp.float32)
    return (state_f + summed + b_down).astype(jnp.bfloat16)


def solution(mesh):
    in_specs = (
        P("req", "tok", None),
        P("req", "tok", None),
        P("req", "tok", None),
        P("req", "tok", None),
        P(),
        P("req", "tok"),
        P(),
        P(),
        P(),
        P(),
        P(None, "tok"),
        P("tok"),
        P("tok", None),
        P(),
    )
    out_specs = P(("req", "tok"), None)
    return jax.shard_map(
        per_device, mesh=mesh, in_specs=in_specs, out_specs=out_specs, check_vma=False
    )
```

time: 850 us -> 547 us (0.64); the launches traced: 848 us -> 558 us
  matrix products: 221 us -> 27.4 us
  Pallas kernels: 0 us -> 148 us
  local copies, waits for them, and re-layouts: 150 us -> 14.4 us
  other arithmetic: 112 us -> 10.1 us
  waiting for transfers between devices: 334 us -> 324 us
  starting transfers between devices: 11.1 us -> 20.6 us
    dot_general x17 -> x2, matrix products: 206 us -> 12.1 us  [the longest x1 11.6 us: per_device(): jnp.dot(pick, hidden_all, preferred_element_type=jnp.float32)]
    pallas_call x0 -> x2, Pallas kernels: none -> 148 us  [flash_attention(): pl.pallas_call(kernel, grid_spec=grid_spec, out_shape=jax.ShapeDtypeStruc...]
    scatter x3 -> x0, local copies, waits for them, and re-layouts: 110 us -> none  [the longest x1 64.2 us: per_device(): send_rows = jnp.zeros((devices * capacity, layers, width), jnp.bfloat16)....]
    reduce_sum x8 -> x2, other arithmetic: 91.3 us -> 0.31 us  [the longest x1 0.19 us: per_device(): jnp.sum(jnp.where(where_to[None, :] == jnp.arange(send_slots, dtype=jnp.i...]
    all_to_all x1, waiting for transfers between devices: 93.9 us -> 48.7 us  [per_device(): lax.all_to_all(send_rows.reshape(devices, capacity, width), ('req', 'tok'...]
    all_gather x1 -> x4, waiting for transfers between devices: 82.8 us -> 116 us  [the longest x2 95.3 us: per_device(): ck = lax.all_gather(cache_kv[r], 'tok', axis=0, tiled=True)]
    squeeze x8 -> x0, local copies, waits for them, and re-layouts: 9.56 us -> none  [per_device(): lax.scan(one_block, state, (blocks, jnp.arange(number, dtype=jnp.int32)))]
    all_to_all x1, starting transfers between devices: 3.57 us -> 13.1 us  [per_device(): lax.all_to_all(send_rows.reshape(devices, capacity, width), ('req', 'tok'...]
  transfers between devices with their start and end apart: 5 -> 8, of which waited for: 4 -> 6; matrix products, arithmetic and copies ran while one was open for 49% -> 6% of each run, Pallas kernels for 0% -> 27%
where the time goes in v1:
time: 547 us; the launch traced here: 558 us
  waiting for transfers between devices  324 us (59%)
  Pallas kernels  148 us (27%)
  matrix products  27.4 us (5%)
  starting transfers between devices  20.6 us (4%)
  local copies, waits for them, and re-layouts  14.4 us (3%)
  between operations  13.6 us (2%)
  other arithmetic  10.1 us (2%)
    pallas_call x2, Pallas kernels, flash_attention(): pl.pallas_call(kernel, grid_spec=grid_spec, out_shape=jax.ShapeDtypeStruc...  148 us
    all_gather x2, waiting for transfers between devices, per_device(): ck = lax.all_gather(cache_kv[r], 'tok', axis=0, tiled=True)  95.3 us
    reduce_scatter x1, waiting for transfers between devices, per_device(): lax.psum_scatter(terms.astype(jnp.bfloat16), 'tok', scatter_dimension=0,...  86.4 us
    all_gather x1, waiting for transfers between devices, per_device(): lax.all_gather(normed, 'tok', axis=0, tiled=True)  71.3 us
    all_to_all x1, waiting for transfers between devices, per_device(): lax.all_to_all(send_rows.reshape(devices, capacity, width), ('req', 'tok'...  48.7 us
    all_gather x2, waiting for transfers between devices, per_device(): nk = lax.all_gather(new_kv[r], 'tok', axis=0, tiled=True)  20.8 us
    dot_general x1, matrix products, per_device(): jnp.dot(units.astype(jnp.bfloat16), w_down, preferred_element_type=jnp.fl...  15.2 us
    all_to_all x1, starting transfers between devices, per_device(): lax.all_to_all(send_rows.reshape(devices, capacity, width), ('req', 'tok'...  13.1 us
  transfers between devices with their start and end apart: 8, of which 6 were waited for; matrix products, arithmetic and copies ran while one was open for 6% of the time, Pallas kernels for 27%

profile of v1, /device:TPU:0, one launch (start us, length us, event | category | flops | bytes accessed | tf_op | source)
XLA Modules:
  0.0 558.1 jit_solution(17891833283543404405)
XLA Ops:
  6.5 1.7 fusion.37
  8.3 1.8 fusion.36
  11.5 0.7 reshape.173
  12.9 1.2 reduce-window.6
  15.4 7.3 %all-to-all-start = ((s32[32,1,16]{2,1,0:T(1,128)}), s32[32,1,16]{2,1,0:T(1,128)S(1)}, u32[]{:S(2)}, u32[]{:S(2)}) async-start(s32[32,1,16]{2,1,0:T(1,128)} %bitcast.1), calls=%async_computation | async-start | bytes 32768 | tf_op jit(solution)/shard_map/all_to_all | solution.py:251
  22.7 1.7 fusion.35
  24.4 1.4 slice.47.q_ref
  25.8 1.3 slice.53.q_ref
  28.4 3.0 add_add_fusion
  31.5 20.8 %all-gather.14.cloned.1.call-done.nk_ref = bf16[1,2048,256]{2,1,0:T(8,128)(2,1)} async-done(((bf16[1,256,256]{2,1,0:T(8,128)(2,1)}), bf16[1,2048,256]{2,1,0:T(8,128)(2,1)}) %all-gather.14.cloned.1.call-update) | async-done | bytes 1048592 | tf_op jit(solution)/shard_map/all_gather | solution.py:207
  52.3 50.2 %all-gather.12.cloned.1.call-done.ck_ref = bf16[1,4096,256]{2,1,0:T(8,128)(2,1)} async-done(((bf16[1,512,256]{2,1,0:T(8,128)(2,1)}), bf16[1,4096,256]{2,1,0:T(8,128)(2,1)}) %all-gather.12.cloned.1.call-update) | async-done | bytes 2097168 | tf_op jit(solution)/shard_map/all_gather | solution.py:206
  102.5 45.8 %shard_map.136 = bf16[1,4096,128]{2,1,0:T(8,128)(2,1)} custom-call(s32[3]{0:T(128)} %get-tuple-element.19.scal_ref, bf16[1,4096,128]{2,1,0:T(8,128)(2,1)} %slice.47.q_ref, bf16[1,4096,256]{2,1,0:T(8,128)(2,1)} %all-gather.12.cloned.1.call-done.ck_ref, bf16[1,2048,256]{2,1,0:T(8,128)(2,1)} %all-gather.14.cloned.1.call-done.nk_ref), custom_call_target="tpu_custom_call" | custom-call | tf_op jit(solution)/shard_map/pallas_call | solution.py:165
  148.3 45.1 %all-gather.16.cloned.1.call-done.ck_ref = bf16[1,4096,256]{2,1,0:T(8,128)(2,1)} async-done(((bf16[1,512,256]{2,1,0:T(8,128)(2,1)}), bf16[1,4096,256]{2,1,0:T(8,128)(2,1)}) %all-gather.16.cloned.1.call-update) | async-done | bytes 2097168 | tf_op jit(solution)/shard_map/all_gather | solution.py:206
  193.4 102.4 %shard_map.137 = bf16[1,4096,128]{2,1,0:T(8,128)(2,1)} custom-call(s32[3]{0:T(128)} %get-tuple-element.20.scal_ref, bf16[1,4096,128]{2,1,0:T(8,128)(2,1)} %slice.53.q_ref, bf16[1,4096,256]{2,1,0:T(8,128)(2,1)} %all-gather.16.cloned.1.call-done.ck_ref, bf16[1,2048,256]{2,1,0:T(8,128)(2,1)} %all-gather.18.cloned.1.call-done.nk_ref), custom_call_target="tpu_custom_call" | custom-call | tf_op jit(solution)/shard_map/pallas_call | solution.py:165
  295.8 1.4 pad_maximum_fusion
  297.2 2.3 reshape.175
  299.5 11.6 %convolution_convert_fusion.1 = bf16[512,2048]{1,0:T(8,128)(2,1)} fusion(bf16[512,2048]{1,0:T(8,128)(2,1)} %bitcast.34, bf16[512,2048]{1,0:T(8,128)(2,1)} %reshape.175, bf16[2048,2048]{1,0:T(8,128)(2,1)} %param.20, f32[2048]{0:T(1024)S(1)} %copy-done.5, s32[512]{0:T(512)S(1)} %add_select_fusion.3), kind=kOutput, calls=%fused_computation.13 | convolution fusion | flops 5374214144 | bytes 14690304 | tf_op jit(solution)/shard_map/dot_general | solution.py:233
  311.1 13.1 %all-to-all-start.1 = ((bf16[32,16,2048]{2,1,0:T(8,128)(2,1)}), bf16[32,16,2048]{2,1,0:T(8,128)(2,1)S(1)}, u32[]{:S(2)}, u32[]{:S(2)}) async-start(bf16[32,16,2048]{2,1,0:T(8,128)(2,1)} %bitcast.30), calls=%async_computation.1 | async-start | bytes 4194304 | tf_op jit(solution)/shard_map/all_to_all | solution.py:244
  325.6 48.7 %all-to-all-done.1 = bf16[32,16,2048]{2,1,0:T(8,128)(2,1)S(1)} async-done(((bf16[32,16,2048]{2,1,0:T(8,128)(2,1)}), bf16[32,16,2048]{2,1,0:T(8,128)(2,1)S(1)}, u32[]{:S(2)}, u32[]{:S(2)}) %all-to-all-start.1) | async-done | bytes 2097184 | tf_op jit(solution)/shard_map/all_to_all | solution.py:244
  375.1 1.0 add_convert_fusion.1
  376.2 71.3 %all-gather.10.cloned.1.call-done = bf16[1024,2048]{1,0:T(8,128)(2,1)} async-done(((bf16[128,2048]{1,0:T(8,128)(2,1)}), bf16[1024,2048]{1,0:T(8,128)(2,1)}) %all-gather.10.cloned.1.call-update) | async-done | bytes 4194320 | tf_op jit(solution)/shard_map/all_gather | solution.py:271
  447.6 15.2 %convolution_convert_fusion = bf16[1024,2048]{1,0:T(8,128)(2,1)} fusion(bf16[1024,2048]{1,0:T(8,128)(2,1)} %param.26, f32[1024]{0:T(1024)S(1)} %copy-done.6, bf16[1024,2048]{1,0:T(8,128)(2,1)} %all-gather.10.cloned.1.call-done, bf16[2048,1024]{1,0:T(8,128)(2,1)} %param.24), kind=kOutput, calls=%fused_computation.12 | convolution fusion | flops 8602517504 | bytes 16781312 | tf_op jit(solution)/shard_map/dot_general | solution.py:278
  462.8 86.4 %reduce-scatter.2.cloned.1.call-done = bf16[128,2048]{1,0:T(8,128)(2,1)} async-done(((bf16[1024,2048]{1,0:T(8,128)(2,1)}), bf16[128,2048]{1,0:T(8,128)(2,1)}) %reduce-scatter.2.cloned.1.call-update) | async-done | bytes 524304 | tf_op jit(solution)/shard_map/reduce_scatter | solution.py:279
  549.3 2.0 add_convert_fusion
  (53 shorter events, 7.0 us)
Async XLA Ops:
  6.5 45.8 %all-gather.14.cloned.1.call-start = ((), (), s32[]{:S(2)}) async-start(), calls=%async_computation.6 | async-start | bytes 1179648 | tf_op jit(solution)/shard_map/all_gather | solution.py:207
  8.3 94.2 %all-gather.12.cloned.1.call-start = ((), (), s32[]{:S(2)}) async-start(), calls=%async_computation.5 | async-start | bytes 2359296 | tf_op jit(solution)/shard_map/all_gather | solution.py:206
  10.2 138.1 %all-gather.18.cloned.1.call-start = ((), (), s32[]{:S(2)}) async-start(), calls=%async_computation.8 | async-start | bytes 1179648 | tf_op jit(solution)/shard_map/all_gather | solution.py:207
  10.9 182.5 %all-gather.16.cloned.1.call-start = ((), (), s32[]{:S(2)}) async-start(), calls=%async_computation.7 | async-start | bytes 2359296 | tf_op jit(solution)/shard_map/all_gather | solution.py:206
  15.4 295.8 %all-to-all-start = ((s32[32,1,16]{2,1,0:T(1,128)}), s32[32,1,16]{2,1,0:T(1,128)S(1)}, u32[]{:S(2)}, u32[]{:S(2)}) async-start(s32[32,1,16]{2,1,0:T(1,128)} %bitcast.1), calls=%async_computation | async-start | bytes 32768 | tf_op jit(solution)/shard_map/all_to_all | solution.py:251
  22.7 4.4 copy-start.7
  22.7 5.0 copy-start.1
  148.3 147.5 %copy-start = (bf16[1,4096,128]{2,1,0:T(8,128)(2,1)S(1)}, bf16[1,4096,128]{2,1,0:T(8,128)(2,1)}, u32[]{:S(2)}) copy-start(bf16[1,4096,128]{2,1,0:T(8,128)(2,1)} %shard_map.136) | copy-start | bytes 3145732
  295.8 3.7 copy-start.5
  311.1 64.0 %copy-start.2 = (f32[2048]{0:T(1024)S(1)}, f32[2048]{0:T(1024)}, u32[]{:S(2)}) copy-start(f32[2048]{0:T(1024)} %param.23) | copy-start | bytes 24580
  311.1 64.0 %copy-start.3 = (f32[2048]{0:T(1024)S(1)}, f32[2048]{0:T(1024)}, u32[]{:S(2)}) copy-start(f32[2048]{0:T(1024)} %param.22) | copy-start | bytes 24580
  311.1 63.2 %all-to-all-start.1 = ((bf16[32,16,2048]{2,1,0:T(8,128)(2,1)}), bf16[32,16,2048]{2,1,0:T(8,128)(2,1)S(1)}, u32[]{:S(2)}, u32[]{:S(2)}) async-start(bf16[32,16,2048]{2,1,0:T(8,128)(2,1)} %bitcast.30), calls=%async_computation.1 | async-start | bytes 4194304 | tf_op jit(solution)/shard_map/all_to_all | solution.py:244
  324.2 123.4 %copy-start.6 = (f32[1024]{0:T(1024)S(1)}, f32[1024]{0:T(1024)}, u32[]{:S(2)}) copy-start(f32[1024]{0:T(1024)} %param.25) | copy-start | bytes 12292
  324.2 123.3 %all-gather.10.cloned.1.call-start = ((), (), s32[]{:S(2)}) async-start(), calls=%async_computation.3 | async-start | bytes 4718592 | tf_op jit(solution)/shard_map/all_gather | solution.py:271
  376.2 173.1 %reduce-scatter.2.cloned.1.call-start = ((), (), s32[]{:S(2)}) async-start(), calls=%async_computation.4 | async-start | bytes 4718592 | tf_op jit(solution)/shard_map/reduce_scatter | solution.py:279
  462.8 86.5 %copy-start.4 = (f32[2048]{0:T(1024)S(1)}, f32[2048]{0:T(1024)}, u32[]{:S(2)}) copy-start(f32[2048]{0:T(1024)} %param.27) | copy-start | bytes 24580
Sparse Core Ops, SparseCore 0:
  9.5 42.7 all-gather.13
  54.4 48.0 all-gather.11
  104.6 38.6 all-gather.17
  145.3 48.0 all-gather.15
  376.3 71.2 all-gather.9
  463.0 86.2 reduce-scatter.1

commit v2 on v1

--- a/solution.py
+++ b/solution.py
@@ -19,7 +19,9 @@
     scal_ref,
     q_ref,
     ck_ref,
+    cv_ref,
     nk_ref,
+    nv_ref,
     o_ref,
     m_sc,
     l_sc,
@@ -28,7 +30,6 @@
     tq,
     tk,
     heads,
-    head_dim,
     n_cache,
     n_req,
     scale,
@@ -51,13 +52,10 @@
         l_sc[...] = jnp.zeros(l_sc.shape, jnp.float32)
         acc_sc[...] = jnp.zeros(acc_sc.shape, jnp.float32)
 
-    def step(kv_ref, mask_fn):
-        kv = kv_ref[0]
-        k = kv[:, :head_dim]
-        v = kv[:, head_dim:]
+    def step(k_ref, v_ref, mask_fn):
         s = (
             lax.dot_general(
-                q_ref[0], k, (((1,), (1,)), ((), ())), preferred_element_type=jnp.float32
+                k_ref[0], q_ref[0], (((1,), (1,)), ((), ())), preferred_element_type=jnp.float32
             )
             * scale
         )
@@ -66,14 +64,14 @@
             mask = mask_fn()
             s = jnp.where(mask, s, neg_large)
         m_prev = m_sc[...]
-        m_new = jnp.maximum(m_prev, jnp.max(s, axis=-1, keepdims=True))
+        m_new = jnp.maximum(m_prev, jnp.max(s, axis=0, keepdims=True))
         p = jnp.exp(s - m_new)
         if mask is not None:
             p = jnp.where(mask, p, 0.0)
         alpha = jnp.exp(m_prev - m_new)
-        l_sc[...] = alpha * l_sc[...] + jnp.sum(p, axis=-1, keepdims=True)
+        l_sc[...] = alpha * l_sc[...] + jnp.sum(p, axis=0, keepdims=True)
         acc_sc[...] = alpha * acc_sc[...] + jnp.dot(
-            p.astype(jnp.bfloat16), v, preferred_element_type=jnp.float32
+            v_ref[0], p.astype(jnp.bfloat16), preferred_element_type=jnp.float32
         )
         m_sc[...] = m_new
 
@@ -86,63 +84,64 @@
     full_new = kn + tk - 1 <= q_lo
 
     def cache_mask():
-        col = lax.broadcasted_iota(jnp.int32, (tq, tk), 1) + kc
-        return col < prefix
+        key = lax.broadcasted_iota(jnp.int32, (tk, tq), 0) + kc
+        return key < prefix
 
     def new_mask():
-        col = lax.broadcasted_iota(jnp.int32, (tq, tk), 1) + kn
-        row = lax.broadcasted_iota(jnp.int32, (tq, tk), 0) // heads + q_lo
-        return col <= row
+        key = lax.broadcasted_iota(jnp.int32, (tk, tq), 0) + kn
+        slot = lax.broadcasted_iota(jnp.int32, (tk, tq), 1) // heads + q_lo
+        return key <= slot
 
     @pl.when(run_cache & full_cache)
     def _c_full():
-        step(ck_ref, None)
+        step(ck_ref, cv_ref, None)
 
     @pl.when(run_cache & jnp.logical_not(full_cache))
     def _c_part():
-        step(ck_ref, cache_mask)
+        step(ck_ref, cv_ref, cache_mask)
 
     @pl.when(run_new & full_new)
     def _n_full():
-        step(nk_ref, None)
+        step(nk_ref, nv_ref, None)
 
     @pl.when(run_new & jnp.logical_not(full_new))
     def _n_part():
-        step(nk_ref, new_mask)
+        step(nk_ref, nv_ref, new_mask)
 
     @pl.when(ki == pl.num_programs(2) - 1)
     def _fin():
         l = l_sc[...]
         safe = jnp.where(l > 0, l, 1.0)
         out = jnp.where(l > 0, acc_sc[...] / safe, 0.0)
-        o_ref[0] = out.astype(o_ref.dtype)
-
-
-def flash_attention(q, ck, nk, scal, heads, tq, tk):
+        o_ref[0] = jnp.transpose(out).astype(o_ref.dtype)
+
+
+def flash_attention(q, ckv, nkv, scal, heads, tq, tk):
     n_req, rows, head_dim = q.shape
-    n_cache = ck.shape[1] // tk
-    n_new = nk.shape[1] // tk
+    n_cache = ckv.shape[1] // tk
+    n_new = nkv.shape[1] // tk
     spt = tq // heads
     scale = 1.0 / math.sqrt(head_dim)
+    cvt = jnp.swapaxes(ckv[:, :, head_dim:], 1, 2)
+    nvt = jnp.swapaxes(nkv[:, :, head_dim:], 1, 2)
 
     def q_map(r, qi, ki, s):
         return (r, qi, 0)
 
-    def c_map(r, qi, ki, s):
+    def c_block(r, ki, s):
         last = jnp.maximum((s[r] + tk - 1) // tk - 1, 0)
-        return (r, jnp.minimum(ki, last), 0)
-
-    def n_map(r, qi, ki, s):
+        return jnp.minimum(ki, last)
+
+    def n_block(r, qi, ki, s):
         q_hi = s[2 * n_req] + (qi + 1) * spt - 1
         last = jnp.minimum(q_hi // tk, n_new - 1)
-        return (r, jnp.clip(ki - n_cache, 0, last), 0)
+        return jnp.clip(ki - n_cache, 0, last)
 
     kernel = functools.partial(
         flash_kernel,
         tq=tq,
         tk=tk,
         heads=heads,
-        head_dim=head_dim,
         n_cache=n_cache,
         n_req=n_req,
         scale=scale,
@@ -152,21 +151,23 @@
         grid=(n_req, rows // tq, n_cache + n_new),
         in_specs=[
             pl.BlockSpec((1, tq, head_dim), q_map),
-            pl.BlockSpec((1, tk, ck.shape[2]), c_map),
-            pl.BlockSpec((1, tk, nk.shape[2]), n_map),
+            pl.BlockSpec((1, tk, head_dim), lambda r, qi, ki, s: (r, c_block(r, ki, s), 0)),
+            pl.BlockSpec((1, head_dim, tk), lambda r, qi, ki, s: (r, 0, c_block(r, ki, s))),
+            pl.BlockSpec((1, tk, head_dim), lambda r, qi, ki, s: (r, n_block(r, qi, ki, s), 0)),
+            pl.BlockSpec((1, head_dim, tk), lambda r, qi, ki, s: (r, 0, n_block(r, qi, ki, s))),
         ],
         out_specs=pl.BlockSpec((1, tq, head_dim), q_map),
         scratch_shapes=[
-            pltpu.VMEM((tq, 1), jnp.float32),
-            pltpu.VMEM((tq, 1), jnp.float32),
-            pltpu.VMEM((tq, head_dim), jnp.float32),
+            pltpu.VMEM((1, tq), jnp.float32),
+            pltpu.VMEM((1, tq), jnp.float32),
+            pltpu.VMEM((head_dim, tq), jnp.float32),
         ],
     )
     return pl.pallas_call(
         kernel,
         grid_spec=grid_spec,
         out_shape=jax.ShapeDtypeStruct((n_req, rows, head_dim), jnp.bfloat16),
-    )(scal, q, ck, nk)
+    )(scal, q, ckv, cvt, nkv, nvt)
 
 
 def per_device(

time: 547 us -> 508 us (0.929); the launches traced: 558 us -> 508 us
  Pallas kernels: 148 us -> 89.8 us
  local copies, waits for them, and re-layouts: 14.4 us -> 34.2 us
  waiting for transfers between devices: 324 us -> 315 us
    pallas_call x2, Pallas kernels: 148 us -> 89.8 us  [flash_attention(): pl.pallas_call(kernel, grid_spec=grid_spec, out_shape=jax.ShapeDtypeStruc...]
    all_gather x2, waiting for transfers between devices: 95.3 us -> 50.3 us  [per_device(): ck = lax.all_gather(cache_kv[r], 'tok', axis=0, tiled=True)]
    all_gather x2, waiting for transfers between devices: 20.8 us -> 57.8 us  [per_device(): nk = lax.all_gather(new_kv[r], 'tok', axis=0, tiled=True)]
    all_gather x0 -> x4, local copies, waits for them, and re-layouts: none -> 13.1 us  [the longest x2 8.44 us: per_device(): ck = lax.all_gather(cache_kv[r], 'tok', axis=0, tiled=True)]
  transfers between devices with their start and end apart: 8 -> 8, of which waited for: 6 -> 7; matrix products, arithmetic and copies ran while one was open for 6% -> 10% of each run, Pallas kernels for 27% -> 18%
where the time goes in v2:
time: 508 us
  waiting for transfers between devices  315 us (62%)
  Pallas kernels  89.8 us (18%)
  local copies, waits for them, and re-layouts  34.2 us (7%)
  matrix products  27.4 us (5%)
  starting transfers between devices  17.7 us (3%)
  between operations  13.6 us (3%)
  other arithmetic  10.2 us (2%)
    pallas_call x2, Pallas kernels, flash_attention(): pl.pallas_call(kernel, grid_spec=grid_spec, out_shape=jax.ShapeDtypeStruc...  89.8 us
    reduce_scatter x1, waiting for transfers between devices, per_device(): lax.psum_scatter(terms.astype(jnp.bfloat16), 'tok', scatter_dimension=0,...  86.3 us
    all_gather x1, waiting for transfers between devices, per_device(): lax.all_gather(normed, 'tok', axis=0, tiled=True)  71.3 us
    all_gather x2, waiting for transfers between devices, per_device(): nk = lax.all_gather(new_kv[r], 'tok', axis=0, tiled=True)  57.8 us
    all_gather x2, waiting for transfers between devices, per_device(): ck = lax.all_gather(cache_kv[r], 'tok', axis=0, tiled=True)  50.3 us
    all_to_all x1, waiting for transfers between devices, per_device(): lax.all_to_all(send_rows.reshape(devices, capacity, width), ('req', 'tok'...  48.7 us
    dot_general x1, matrix products, per_device(): jnp.dot(units.astype(jnp.bfloat16), w_down, preferred_element_type=jnp.fl...  15.3 us
    dot_general x1, matrix products, per_device(): jnp.dot(pick, hidden_all, preferred_element_type=jnp.float32)  11.6 us
  transfers between devices with their start and end apart: 8, of which 7 were waited for; matrix products, arithmetic and copies ran while one was open for 10% of the time, Pallas kernels for 18%

profile of v2, /device:TPU:0, one launch (start us, length us, event | category | flops | bytes accessed | tf_op | source)
XLA Modules:
  0.0 507.5 jit_solution(6946923744379715630)
XLA Ops:
  15.9 7.3 %all-to-all-start = ((s32[32,1,16]{2,1,0:T(1,128)}), s32[32,1,16]{2,1,0:T(1,128)S(1)}, u32[]{:S(2)}, u32[]{:S(2)}) async-start(s32[32,1,16]{2,1,0:T(1,128)} %bitcast.1), calls=%async_computation | async-start | bytes 32768 | tf_op jit(solution)/shard_map/all_to_all | solution.py:252
  23.2 1.7 fusion.35
  24.9 1.4 slice.59.q_ref
  29.0 3.2 add_add_fusion
  32.2 19.7 %all-gather.14.cloned.1.call-done = bf16[1,2048,256]{1,2,0:T(8,128)(2,1)} async-done(((bf16[1,256,256]{1,2,0:T(8,128)(2,1)}), bf16[1,2048,256]{1,2,0:T(8,128)(2,1)}) %all-gather.14.cloned.1.call-update) | async-done | bytes 1048592 | tf_op jit(solution)/shard_map/all_gather | solution.py:208
  51.8 2.3 copy.47.nk_ref
  54.2 38.2 %all-gather.18.cloned.1.call-done = bf16[1,2048,256]{1,2,0:T(8,128)(2,1)} async-done(((bf16[1,256,256]{1,2,0:T(8,128)(2,1)}), bf16[1,2048,256]{1,2,0:T(8,128)(2,1)}) %all-gather.18.cloned.1.call-update) | async-done | bytes 1048592 | tf_op jit(solution)/shard_map/all_gather | solution.py:208
  92.3 2.3 copy.51.nk_ref
  95.5 1.9 slice_bitcast_fusion.2.nv_ref
  97.4 47.0 %all-gather.12.cloned.1.call-done = bf16[1,4096,256]{1,2,0:T(8,128)(2,1)} async-done(((bf16[1,512,256]{1,2,0:T(8,128)(2,1)}), bf16[1,4096,256]{1,2,0:T(8,128)(2,1)}) %all-gather.12.cloned.1.call-update) | async-done | bytes 2097168 | tf_op jit(solution)/shard_map/all_gather | solution.py:207
  144.4 4.2 copy.46.ck_ref
  149.7 42.6 %shard_map.136 = bf16[1,4096,128]{2,1,0:T(8,128)(2,1)} custom-call(s32[3]{0:T(128)} %get-tuple-element.19.scal_ref, bf16[1,4096,128]{2,1,0:T(8,128)(2,1)} %slice.59.q_ref, bf16[1,4096,256]{2,1,0:T(8,128)(2,1)} %copy.46.ck_ref, bf16[1,128,4096]{2,1,0:T(8,128)(2,1)} %slice_bitcast_fusion.1.cv_ref, bf16[1,2048,256]{2,1,0:T(8,128)(2,1)} %copy.47.nk_ref, ...), custom_call_target="tpu_custom_call" | custom-call | tf_op jit(solution)/shard_map/pallas_call | solution.py:166
  192.3 3.3 all-gather.16.cloned.1.call-done
  195.6 4.2 copy.50.ck_ref
  200.9 47.2 %shard_map.137 = bf16[1,4096,128]{2,1,0:T(8,128)(2,1)} custom-call(s32[3]{0:T(128)} %get-tuple-element.20.scal_ref, bf16[1,4096,128]{2,1,0:T(8,128)(2,1)} %slice.67.q_ref, bf16[1,4096,256]{2,1,0:T(8,128)(2,1)} %copy.50.ck_ref, bf16[1,128,4096]{2,1,0:T(8,128)(2,1)} %slice_bitcast_fusion.cv_ref, bf16[1,2048,256]{2,1,0:T(8,128)(2,1)} %copy.51.nk_ref, ...), custom_call_target="tpu_custom_call" | custom-call | tf_op jit(solution)/shard_map/pallas_call | solution.py:166
  248.1 1.4 pad_maximum_fusion
  249.5 2.5 reshape.175
  252.0 11.6 %convolution_convert_fusion.1 = bf16[512,2048]{1,0:T(8,128)(2,1)} fusion(bf16[512,2048]{1,0:T(8,128)(2,1)} %bitcast.42, bf16[512,2048]{1,0:T(8,128)(2,1)} %reshape.175, bf16[2048,2048]{1,0:T(8,128)(2,1)} %param.20, f32[2048]{0:T(1024)S(1)} %copy-done.8, s32[512]{0:T(512)S(1)} %add_select_fusion.3), kind=kOutput, calls=%fused_computation.13 | convolution fusion | flops 5374214144 | bytes 14690304 | tf_op jit(solution)/shard_map/dot_general | solution.py:234
  263.6 10.2 %all-to-all-start.1 = ((bf16[32,16,2048]{2,1,0:T(8,128)(2,1)}), bf16[32,16,2048]{2,1,0:T(8,128)(2,1)S(1)}, u32[]{:S(2)}, u32[]{:S(2)}) async-start(bf16[32,16,2048]{2,1,0:T(8,128)(2,1)} %bitcast.38), calls=%async_computation.1 | async-start | bytes 4194304 | tf_op jit(solution)/shard_map/all_to_all | solution.py:245
  275.1 48.7 %all-to-all-done.1 = bf16[32,16,2048]{2,1,0:T(8,128)(2,1)S(1)} async-done(((bf16[32,16,2048]{2,1,0:T(8,128)(2,1)}), bf16[32,16,2048]{2,1,0:T(8,128)(2,1)S(1)}, u32[]{:S(2)}, u32[]{:S(2)}) %all-to-all-start.1) | async-done | bytes 2097184 | tf_op jit(solution)/shard_map/all_to_all | solution.py:245
  325.8 71.3 %all-gather.10.cloned.1.call-done = bf16[1024,2048]{1,0:T(8,128)(2,1)} async-done(((bf16[128,2048]{1,0:T(8,128)(2,1)}), bf16[1024,2048]{1,0:T(8,128)(2,1)}) %all-gather.10.cloned.1.call-update) | async-done | bytes 4194320 | tf_op jit(solution)/shard_map/all_gather | solution.py:272
  397.1 15.3 %convolution_convert_fusion = bf16[1024,2048]{1,0:T(8,128)(2,1)} fusion(bf16[1024,2048]{1,0:T(8,128)(2,1)} %param.26, f32[1024]{0:T(1024)S(1)} %copy-done.9, bf16[1024,2048]{1,0:T(8,128)(2,1)} %all-gather.10.cloned.1.call-done, bf16[2048,1024]{1,0:T(8,128)(2,1)} %param.24), kind=kOutput, calls=%fused_computation.12 | convolution fusion | flops 8602517504 | bytes 16781312 | tf_op jit(solution)/shard_map/dot_general | solution.py:279
  412.4 86.3 %reduce-scatter.2.cloned.1.call-done = bf16[128,2048]{1,0:T(8,128)(2,1)} async-done(((bf16[1024,2048]{1,0:T(8,128)(2,1)}), bf16[128,2048]{1,0:T(8,128)(2,1)}) %reduce-scatter.2.cloned.1.call-update) | async-done | bytes 524304 | tf_op jit(solution)/shard_map/reduce_scatter | solution.py:280
  498.7 2.0 add_convert_fusion
  (71 shorter events, 18.2 us)
Async XLA Ops:
  6.5 45.3 %all-gather.14.cloned.1.call-start = ((), (), s32[]{:S(2)}) async-start(), calls=%async_computation.6 | async-start | bytes 1179648 | tf_op jit(solution)/shard_map/all_gather | solution.py:208
  8.3 84.0 %all-gather.18.cloned.1.call-start = ((), (), s32[]{:S(2)}) async-start(), calls=%async_computation.8 | async-start | bytes 1179648 | tf_op jit(solution)/shard_map/all_gather | solution.py:208
  9.1 135.2 %all-gather.12.cloned.1.call-start = ((), (), s32[]{:S(2)}) async-start(), calls=%async_computation.5 | async-start | bytes 2359296 | tf_op jit(solution)/shard_map/all_gather | solution.py:207
  11.1 184.5 %all-gather.16.cloned.1.call-start = ((), (), s32[]{:S(2)}) async-start(), calls=%async_computation.7 | async-start | bytes 2359296 | tf_op jit(solution)/shard_map/all_gather | solution.py:207
  15.9 247.7 %all-to-all-start = ((s32[32,1,16]{2,1,0:T(1,128)}), s32[32,1,16]{2,1,0:T(1,128)S(1)}, u32[]{:S(2)}, u32[]{:S(2)}) async-start(s32[32,1,16]{2,1,0:T(1,128)} %bitcast.1), calls=%async_computation | async-start | bytes 32768 | tf_op jit(solution)/shard_map/all_to_all | solution.py:252
  23.2 4.4 copy-start.10
  23.2 5.0 copy-start.4
  51.8 42.8 %copy-start.3 = (bf16[1,2048,256]{1,2,0:T(8,128)(2,1)S(1)}, bf16[1,2048,256]{1,2,0:T(8,128)(2,1)}, u32[]{:S(2)}) copy-start(bf16[1,2048,256]{1,2,0:T(8,128)(2,1)} %all-gather.14.cloned.1.call-done) | copy-start | bytes 3145732
  144.4 4.2 copy-start.1
  195.6 4.2 copy-start
  199.8 48.2 %copy-start.2 = (bf16[1,4096,128]{2,1,0:T(8,128)(2,1)S(1)}, bf16[1,4096,128]{2,1,0:T(8,128)(2,1)}, u32[]{:S(2)}) copy-start(bf16[1,4096,128]{2,1,0:T(8,128)(2,1)} %shard_map.136) | copy-start | bytes 3145732
  248.1 3.9 copy-start.8
  263.6 61.1 %copy-start.5 = (f32[2048]{0:T(1024)S(1)}, f32[2048]{0:T(1024)}, u32[]{:S(2)}) copy-start(f32[2048]{0:T(1024)} %param.23) | copy-start | bytes 24580
  263.6 61.1 %copy-start.6 = (f32[2048]{0:T(1024)S(1)}, f32[2048]{0:T(1024)}, u32[]{:S(2)}) copy-start(f32[2048]{0:T(1024)} %param.22) | copy-start | bytes 24580
  263.6 60.3 %all-to-all-start.1 = ((bf16[32,16,2048]{2,1,0:T(8,128)(2,1)}), bf16[32,16,2048]{2,1,0:T(8,128)(2,1)S(1)}, u32[]{:S(2)}, u32[]{:S(2)}) async-start(bf16[32,16,2048]{2,1,0:T(8,128)(2,1)} %bitcast.38), calls=%async_computation.1 | async-start | bytes 4194304 | tf_op jit(solution)/shard_map/all_to_all | solution.py:245
  273.8 123.4 %copy-start.9 = (f32[1024]{0:T(1024)S(1)}, f32[1024]{0:T(1024)}, u32[]{:S(2)}) copy-start(f32[1024]{0:T(1024)} %param.25) | copy-start | bytes 12292
  273.8 123.3 %all-gather.10.cloned.1.call-start = ((), (), s32[]{:S(2)}) async-start(), calls=%async_computation.3 | async-start | bytes 4718592 | tf_op jit(solution)/shard_map/all_gather | solution.py:272
  325.7 173.0 %reduce-scatter.2.cloned.1.call-start = ((), (), s32[]{:S(2)}) async-start(), calls=%async_computation.4 | async-start | bytes 4718592 | tf_op jit(solution)/shard_map/reduce_scatter | solution.py:280
  412.4 86.3 %copy-start.7 = (f32[2048]{0:T(1024)S(1)}, f32[2048]{0:T(1024)}, u32[]{:S(2)}) copy-start(f32[2048]{0:T(1024)} %param.27) | copy-start | bytes 24580
Sparse Core Ops, SparseCore 0:
  9.4 42.3 all-gather.13
  53.9 38.4 all-gather.17
  94.4 49.9 all-gather.11
  146.3 49.2 all-gather.15
  325.9 71.2 all-gather.9
  412.5 86.1 reduce-scatter.1

commit v3 on v2

--- a/solution.py
+++ b/solution.py
@@ -202,10 +202,17 @@
     tk = 512
     q_flat = queries.reshape(req_dev, rows, head_dim)
 
+    prefix_dev = cache_kv.shape[1]
+    local_kv = jnp.concatenate([cache_kv, new_kv], axis=1)
+    gathered = [lax.all_gather(local_kv[0], "tok", axis=0, tiled=True)]
+    for r in range(1, req_dev):
+        mine, gathered[-1] = lax.optimization_barrier((local_kv[r], gathered[-1]))
+        gathered.append(lax.all_gather(mine, "tok", axis=0, tiled=True))
     outs = []
     for r in range(req_dev):
-        ck = lax.all_gather(cache_kv[r], "tok", axis=0, tiled=True)
-        nk = lax.all_gather(new_kv[r], "tok", axis=0, tiled=True)
+        both = gathered[r].reshape(n_member, prefix_dev + slot_dev, local_kv.shape[-1])
+        ck = both[:, :prefix_dev].reshape(n_member * prefix_dev, local_kv.shape[-1])
+        nk = both[:, prefix_dev:].reshape(n_member * slot_dev, local_kv.shape[-1])
         scal = jnp.stack([own_prefix[r], live_count[r], base]).astype(jnp.int32)
         outs.append(
             flash_attention(q_flat[r : r + 1], ck[None], nk[None], scal, heads, tq, tk)
@@ -277,9 +284,14 @@
         approximate=True,
     )
     terms = jnp.dot(units.astype(jnp.bfloat16), w_down, preferred_element_type=jnp.float32)
-    summed = lax.psum_scatter(
-        terms.astype(jnp.bfloat16), "tok", scatter_dimension=0, tiled=True
-    ).astype(jnp.float32)
+    parts = lax.all_to_all(
+        terms.astype(jnp.bfloat16).reshape(n_member, TOK_DEV, width),
+        "tok",
+        split_axis=0,
+        concat_axis=0,
+        tiled=True,
+    )
+    summed = jnp.sum(parts.astype(jnp.float32), axis=0)
     return (state_f + summed + b_down).astype(jnp.bfloat16)
 
 

time: 508 us -> 473 us (0.931)
  waiting for transfers between devices: 315 us -> 183 us
  blocking collectives: 0 us -> 96.4 us
  Pallas kernels: 89.8 us -> 103 us
  starting transfers between devices: 17.7 us -> 6.18 us
    all_to_all x0 -> x1, blocking collectives: none -> 96.4 us  [per_device(): lax.all_to_all(terms.astype(jnp.bfloat16).reshape(n_member, TOK_DEV, widt...]
    reduce_scatter x1 -> x0, waiting for transfers between devices: 86.3 us -> none  [per_device(): lax.psum_scatter(terms.astype(jnp.bfloat16), 'tok', scatter_dimension=0,...]
    all_gather x4 -> x2, waiting for transfers between devices: 108 us -> 63.3 us  [the longest x1 63.3 us: per_device(): gathered = [lax.all_gather(local_kv[0], 'tok', axis=0, tiled=True)]]
    all_gather x4 -> x0, local copies, waits for them, and re-layouts: 13.1 us -> none  [the longest x2 8.44 us: per_device(): ck = lax.all_gather(cache_kv[r], 'tok', axis=0, tiled=True)]
    pallas_call x2, Pallas kernels: 89.8 us -> 103 us  [flash_attention(): pl.pallas_call(kernel, grid_spec=grid_spec, out_shape=jax.ShapeDtypeStruc...]
    slice x3 -> x10, local copies, waits for them, and re-layouts: 2.27 us -> 12.7 us  [the longest x2 4.11 us: per_device(): nk = both[:, prefix_dev:].reshape(n_member * slot_dev, local_kv.shape[-1])]
    all_to_all x1, starting transfers between devices: 10.2 us -> 2.87 us  [per_device(): lax.all_to_all(send_rows.reshape(devices, capacity, width), ('req', 'tok'...]
    unnamed x27 -> x30, local copies, waits for them, and re-layouts: 3.93 us -> 10.6 us
  transfers between devices with their start and end apart: 8 -> 5, of which waited for: 7 -> 3; matrix products, arithmetic and copies ran while one was open for 10% -> 10% of each run, Pallas kernels for 18% -> 22%
where the time goes in v3:
time: 473 us
  waiting for transfers between devices  183 us (39%)
  Pallas kernels  103 us (22%)
  blocking collectives  96.4 us (20%)
  local copies, waits for them, and re-layouts  34.2 us (7%)
  matrix products  27.4 us (6%)
  between operations  13.3 us (3%)
  other arithmetic  9.82 us (2%)
  starting transfers between devices  6.18 us (1%)
    pallas_call x2, Pallas kernels, flash_attention(): pl.pallas_call(kernel, grid_spec=grid_spec, out_shape=jax.ShapeDtypeStruc...  103 us
    all_to_all x1, blocking collectives, per_device(): lax.all_to_all(terms.astype(jnp.bfloat16).reshape(n_member, TOK_DEV, widt...  96.4 us
    all_gather x1, waiting for transfers between devices, per_device(): lax.all_gather(normed, 'tok', axis=0, tiled=True)  71.2 us
    all_gather x1, waiting for transfers between devices, per_device(): gathered = [lax.all_gather(local_kv[0], 'tok', axis=0, tiled=True)]  63.3 us
    all_to_all x1, waiting for transfers between devices, per_device(): lax.all_to_all(send_rows.reshape(devices, capacity, width), ('req', 'tok'...  48.7 us
    dot_general x1, matrix products, per_device(): jnp.dot(units.astype(jnp.bfloat16), w_down, preferred_element_type=jnp.fl...  15.3 us
    dot_general x1, matrix products, per_device(): jnp.dot(pick, hidden_all, preferred_element_type=jnp.float32)  11.6 us
    unnamed x30, local copies, waits for them, and re-layouts  10.6 us
  transfers between devices with their start and end apart: 5, of which 3 were waited for; matrix products, arithmetic and copies ran while one was open for 10% of the time, Pallas kernels for 22%

profile of v3, /device:TPU:0, one launch (start us, length us, event | category | flops | bytes accessed | tf_op | source)
XLA Modules:
  0.0 473.4 jit_solution(4084231745648878961)
XLA Ops:
  9.6 63.3 %all-gather.9.cloned.1.call-done = bf16[1,6144,256]{2,1,0:T(8,128)(2,1)} async-done(((bf16[1,768,256]{2,1,0:T(8,128)(2,1)}), bf16[1,6144,256]{2,1,0:T(8,128)(2,1)}) %all-gather.9.cloned.1.call-update) | async-done | bytes 3145744 | tf_op jit(solution)/shard_map/all_gather | solution.py:207
  76.8 3.2 all-to-all-start
  80.0 1.8 fusion.35
  81.8 1.3 slice.65.q_ref
  83.1 1.3 slice.75.q_ref
  85.8 3.1 add_add_fusion
  89.0 1.7 slice.83
  90.7 2.1 slice.85
  93.9 2.3 copy.60
  97.0 2.1 copy.61
  99.1 55.5 %shard_map.136 = bf16[1,4096,128]{2,1,0:T(8,128)(2,1)} custom-call(s32[3]{0:T(128)} %get-tuple-element.21.scal_ref, bf16[1,4096,128]{2,1,0:T(8,128)(2,1)} %slice.65.q_ref, bf16[1,4096,256]{2,1,0:T(8,128)(2,1)} %bitcast.46, bf16[1,128,4096]{2,1,0:T(8,128)(2,1)} %bitcast.54, bf16[1,2048,256]{2,1,0:T(8,128)(2,1)} %bitcast.51, bf16[1,128,2048]{2,1,0:T(8,128)(2,1)} %bitcast.61), custom_call_target="tpu_custom_call" | custom-call | tf_op jit(solution)/shard_map/pallas_call | solution.py:166
  154.6 1.7 slice.87
  156.3 2.1 slice.89
  159.5 2.3 copy.62
  162.7 2.0 copy.63
  164.8 47.3 %shard_map.137 = bf16[1,4096,128]{2,1,0:T(8,128)(2,1)} custom-call(s32[3]{0:T(128)} %get-tuple-element.22.scal_ref, bf16[1,4096,128]{2,1,0:T(8,128)(2,1)} %slice.75.q_ref, bf16[1,4096,256]{2,1,0:T(8,128)(2,1)} %bitcast.44, bf16[1,128,4096]{2,1,0:T(8,128)(2,1)} %bitcast.53, bf16[1,2048,256]{2,1,0:T(8,128)(2,1)} %bitcast.49, bf16[1,128,2048]{2,1,0:T(8,128)(2,1)} %bitcast.60), custom_call_target="tpu_custom_call" | custom-call | tf_op jit(solution)/shard_map/pallas_call | solution.py:166
  212.0 1.4 pad_maximum_fusion
  213.5 2.3 reshape.186
  215.8 11.6 %convolution_convert_fusion.1 = bf16[512,2048]{1,0:T(8,128)(2,1)} fusion(bf16[512,2048]{1,0:T(8,128)(2,1)} %bitcast.65, bf16[512,2048]{1,0:T(8,128)(2,1)} %reshape.186, bf16[2048,2048]{1,0:T(8,128)(2,1)} %param.20, f32[2048]{0:T(1024)S(1)} %copy-done.9, s32[512]{0:T(512)S(1)} %add_select_fusion.3), kind=kOutput, calls=%fused_computation.14 | convolution fusion | flops 5374214144 | bytes 14690304 | tf_op jit(solution)/shard_map/dot_general | solution.py:241
  227.4 2.9 all-to-all-start.1
  231.6 48.7 %all-to-all-done.1 = bf16[32,16,2048]{2,1,0:T(8,128)(2,1)S(1)} async-done(((bf16[32,16,2048]{2,1,0:T(8,128)(2,1)}), bf16[32,16,2048]{2,1,0:T(8,128)(2,1)S(1)}, u32[]{:S(2)}, u32[]{:S(2)}) %all-to-all-start.1) | async-done | bytes 2097184 | tf_op jit(solution)/shard_map/all_to_all | solution.py:252
  282.2 71.2 %all-gather.7.cloned.1.call-done = bf16[1024,2048]{1,0:T(8,128)(2,1)} async-done(((bf16[128,2048]{1,0:T(8,128)(2,1)}), bf16[1024,2048]{1,0:T(8,128)(2,1)}) %all-gather.7.cloned.1.call-update) | async-done | bytes 4194320 | tf_op jit(solution)/shard_map/all_gather | solution.py:279
  353.5 15.3 %convolution_convert_fusion = bf16[1024,2048]{1,0:T(8,128)(2,1)} fusion(bf16[1024,2048]{1,0:T(8,128)(2,1)} %param.26, f32[1024]{0:T(1024)S(1)} %copy-done.10, bf16[1024,2048]{1,0:T(8,128)(2,1)} %all-gather.7.cloned.1.call-done, bf16[2048,1024]{1,0:T(8,128)(2,1)} %param.24), kind=kOutput, calls=%fused_computation.13 | convolution fusion | flops 8602517504 | bytes 16781312 | tf_op jit(solution)/shard_map/dot_general | solution.py:286
  368.8 96.4 %all_to_all.16 = bf16[8,128,2048]{2,1,0:T(8,128)(2,1)S(1)} all-to-all(bf16[8,128,2048]{2,1,0:T(8,128)(2,1)} %bitcast.52), channel_id=1, replica_groups=mesh['req'=4,'tok'=8] {'tok'}, dimensions={0} | all-to-all | bytes 8388608 | tf_op jit(solution)/shard_map/all_to_all | solution.py:287
  (67 shorter events, 17.1 us)
Async XLA Ops:
  6.5 66.3 %all-gather.9.cloned.1.call-start = ((), (), s32[]{:S(2)}) async-start(), calls=%async_computation.5 | async-start | bytes 3538944 | tf_op jit(solution)/shard_map/all_gather | solution.py:207
  9.6 145.0 %all-gather.5.cloned.1.call-start = ((), (), s32[]{:S(2)}) async-start(), calls=%async_computation.3 | async-start | bytes 3538944 | tf_op jit(solution)/shard_map/all_gather | solution.py:210
  76.8 150.6 %all-to-all-start = ((s32[32,1,16]{2,1,0:T(1,128)}), s32[32,1,16]{2,1,0:T(1,128)S(1)}, u32[]{:S(2)}, u32[]{:S(2)}) async-start(s32[32,1,16]{2,1,0:T(1,128)} %bitcast.1), calls=%async_computation | async-start | bytes 32768 | tf_op jit(solution)/shard_map/all_to_all | solution.py:259
  80.0 4.5 copy-start.11
  80.0 5.1 %copy-start.5 = (s32[2,256]{1,0:T(2,128)S(1)}, s32[2,256]{1,0:T(2,128)}, u32[]{:S(2)}) copy-start(s32[2,256]{1,0:T(2,128)} %param.19) | copy-start | bytes 6148
  90.7 8.4 %copy-start.1 = (bf16[8,512,256]{2,1,0:T(8,128)(2,1)}, bf16[8,512,256]{2,1,0:T(8,128)(2,1)S(1)}, u32[]{:S(2)}) copy-start(bf16[8,512,256]{2,1,0:T(8,128)(2,1)S(1)} %slice.83) | copy-start | bytes 6291460
  92.8 6.3 %copy-start.3 = (bf16[8,256,256]{2,1,0:T(8,128)(2,1)}, bf16[8,256,256]{2,1,0:T(8,128)(2,1)S(1)}, u32[]{:S(2)}) copy-start(bf16[8,256,256]{2,1,0:T(8,128)(2,1)S(1)} %slice.85) | copy-start | bytes 3145732
  156.3 8.4 %copy-start = (bf16[8,512,256]{2,1,0:T(8,128)(2,1)}, bf16[8,512,256]{2,1,0:T(8,128)(2,1)S(1)}, u32[]{:S(2)}) copy-start(bf16[8,512,256]{2,1,0:T(8,128)(2,1)S(1)} %slice.87) | copy-start | bytes 6291460
  158.4 6.4 %copy-start.2 = (bf16[8,256,256]{2,1,0:T(8,128)(2,1)}, bf16[8,256,256]{2,1,0:T(8,128)(2,1)S(1)}, u32[]{:S(2)}) copy-start(bf16[8,256,256]{2,1,0:T(8,128)(2,1)S(1)} %slice.89) | copy-start | bytes 3145732
  164.7 47.3 %copy-start.4 = (bf16[1,4096,128]{2,1,0:T(8,128)(2,1)S(1)}, bf16[1,4096,128]{2,1,0:T(8,128)(2,1)}, u32[]{:S(2)}) copy-start(bf16[1,4096,128]{2,1,0:T(8,128)(2,1)} %shard_map.136) | copy-start | bytes 3145732
  212.0 3.7 copy-start.9
  227.4 53.8 %copy-start.6 = (f32[2048]{0:T(1024)S(1)}, f32[2048]{0:T(1024)}, u32[]{:S(2)}) copy-start(f32[2048]{0:T(1024)} %param.23) | copy-start | bytes 24580
  227.4 53.8 %copy-start.7 = (f32[2048]{0:T(1024)S(1)}, f32[2048]{0:T(1024)}, u32[]{:S(2)}) copy-start(f32[2048]{0:T(1024)} %param.22) | copy-start | bytes 24580
  227.4 53.0 %all-to-all-start.1 = ((bf16[32,16,2048]{2,1,0:T(8,128)(2,1)}), bf16[32,16,2048]{2,1,0:T(8,128)(2,1)S(1)}, u32[]{:S(2)}, u32[]{:S(2)}) async-start(bf16[32,16,2048]{2,1,0:T(8,128)(2,1)} %bitcast.59), calls=%async_computation.1 | async-start | bytes 4194304 | tf_op jit(solution)/shard_map/all_to_all | solution.py:252
  230.2 123.2 %copy-start.10 = (f32[1024]{0:T(1024)S(1)}, f32[1024]{0:T(1024)}, u32[]{:S(2)}) copy-start(f32[1024]{0:T(1024)} %param.25) | copy-start | bytes 12292
  230.3 123.2 %all-gather.7.cloned.1.call-start = ((), (), s32[]{:S(2)}) async-start(), calls=%async_computation.4 | async-start | bytes 4718592 | tf_op jit(solution)/shard_map/all_gather | solution.py:279
  465.2 0.7 copy-start.8
Sparse Core Ops, SparseCore 0:
  9.7 63.1 all-gather.8
  75.1 59.1 all-gather.4
  282.3 71.0 all-gather.6

commit v4 on v3

--- a/solution.py
+++ b/solution.py
@@ -24,10 +24,10 @@
     nv_ref,
     o_ref,
     m_sc,
-    l_sc,
     acc_sc,
     *,
     tq,
+    head_dim,
     tk,
     heads,
     n_cache,
@@ -49,7 +49,6 @@
     @pl.when(ki == 0)
     def _init():
         m_sc[...] = jnp.full(m_sc.shape, neg_large, jnp.float32)
-        l_sc[...] = jnp.zeros(l_sc.shape, jnp.float32)
         acc_sc[...] = jnp.zeros(acc_sc.shape, jnp.float32)
 
     def step(k_ref, v_ref, mask_fn):
@@ -69,7 +68,6 @@
         if mask is not None:
             p = jnp.where(mask, p, 0.0)
         alpha = jnp.exp(m_prev - m_new)
-        l_sc[...] = alpha * l_sc[...] + jnp.sum(p, axis=0, keepdims=True)
         acc_sc[...] = alpha * acc_sc[...] + jnp.dot(
             v_ref[0], p.astype(jnp.bfloat16), preferred_element_type=jnp.float32
         )
@@ -110,9 +108,10 @@
 
     @pl.when(ki == pl.num_programs(2) - 1)
     def _fin():
-        l = l_sc[...]
+        acc = acc_sc[...]
+        l = acc[head_dim : head_dim + 1]
         safe = jnp.where(l > 0, l, 1.0)
-        out = jnp.where(l > 0, acc_sc[...] / safe, 0.0)
+        out = jnp.where(l > 0, acc[:head_dim] / safe, 0.0)
         o_ref[0] = jnp.transpose(out).astype(o_ref.dtype)
 
 
@@ -122,8 +121,12 @@
     n_new = nkv.shape[1] // tk
     spt = tq // heads
     scale = 1.0 / math.sqrt(head_dim)
+    ones = jnp.ones((n_req, 8, 1), jnp.bfloat16)
     cvt = jnp.swapaxes(ckv[:, :, head_dim:], 1, 2)
+    cvt = jnp.concatenate([cvt, jnp.broadcast_to(ones, (n_req, 8, cvt.shape[2]))], axis=1)
     nvt = jnp.swapaxes(nkv[:, :, head_dim:], 1, 2)
+    nvt = jnp.concatenate([nvt, jnp.broadcast_to(ones, (n_req, 8, nvt.shape[2]))], axis=1)
+    ext = head_dim + 8
 
     def q_map(r, qi, ki, s):
         return (r, qi, 0)
@@ -142,6 +145,7 @@
         tq=tq,
         tk=tk,
         heads=heads,
+        head_dim=head_dim,
         n_cache=n_cache,
         n_req=n_req,
         scale=scale,
@@ -152,15 +156,14 @@
         in_specs=[
             pl.BlockSpec((1, tq, head_dim), q_map),
             pl.BlockSpec((1, tk, head_dim), lambda r, qi, ki, s: (r, c_block(r, ki, s), 0)),
-            pl.BlockSpec((1, head_dim, tk), lambda r, qi, ki, s: (r, 0, c_block(r, ki, s))),
+            pl.BlockSpec((1, ext, tk), lambda r, qi, ki, s: (r, 0, c_block(r, ki, s))),
             pl.BlockSpec((1, tk, head_dim), lambda r, qi, ki, s: (r, n_block(r, qi, ki, s), 0)),
-            pl.BlockSpec((1, head_dim, tk), lambda r, qi, ki, s: (r, 0, n_block(r, qi, ki, s))),
+            pl.BlockSpec((1, ext, tk), lambda r, qi, ki, s: (r, 0, n_block(r, qi, ki, s))),
         ],
         out_specs=pl.BlockSpec((1, tq, head_dim), q_map),
         scratch_shapes=[
             pltpu.VMEM((1, tq), jnp.float32),
-            pltpu.VMEM((1, tq), jnp.float32),
-            pltpu.VMEM((head_dim, tq), jnp.float32),
+            pltpu.VMEM((ext, tq), jnp.float32),
         ],
     )
     return pl.pallas_call(
@@ -198,8 +201,8 @@
     live_count = jnp.sum((dest_map >= 0).astype(jnp.int32), axis=1)
     base = (member * slot_dev).astype(jnp.int32)
     rows = slot_dev * heads
-    tq = min(1024, rows)
-    tk = 512
+    tq = min(2048, rows)
+    tk = 1024
     q_flat = queries.reshape(req_dev, rows, head_dim)
 
     prefix_dev = cache_kv.shape[1]
@@ -284,14 +287,9 @@
         approximate=True,
     )
     terms = jnp.dot(units.astype(jnp.bfloat16), w_down, preferred_element_type=jnp.float32)
-    parts = lax.all_to_all(
-        terms.astype(jnp.bfloat16).reshape(n_member, TOK_DEV, width),
-        "tok",
-        split_axis=0,
-        concat_axis=0,
-        tiled=True,
-    )
-    summed = jnp.sum(parts.astype(jnp.float32), axis=0)
+    summed = lax.psum_scatter(
+        terms.astype(jnp.bfloat16), "tok", scatter_dimension=0, tiled=True
+    ).astype(jnp.float32)
     return (state_f + summed + b_down).astype(jnp.bfloat16)
 
 

time: 473 us -> 446 us (0.943)
  blocking collectives: 96.4 us -> 0 us
  waiting for transfers between devices: 183 us -> 270 us
  Pallas kernels: 103 us -> 58.4 us
  starting transfers between devices: 6.18 us -> 24.4 us
    all_to_all x1 -> x0, blocking collectives: 96.4 us -> none  [per_device(): lax.all_to_all(terms.astype(jnp.bfloat16).reshape(n_member, TOK_DEV, widt...]
    reduce_scatter x0 -> x1, waiting for transfers between devices: none -> 86.3 us  [per_device(): lax.psum_scatter(terms.astype(jnp.bfloat16), 'tok', scatter_dimension=0,...]
    pallas_call x2, Pallas kernels: 103 us -> 58.4 us  [flash_attention(): pl.pallas_call(kernel, grid_spec=grid_spec, out_shape=jax.ShapeDtypeStruc...]
    all_to_all x1, starting transfers between devices: 2.87 us -> 21.1 us  [per_device(): lax.all_to_all(send_rows.reshape(devices, capacity, width), ('req', 'tok'...]
    concatenate x0 -> x4, local copies, waits for them, and re-layouts: none -> 7.44 us  [the longest x2 4.68 us: flash_attention(): jnp.concatenate([cvt, jnp.broadcast_to(ones, (n_req, 8, cvt.shape[2]))],...]
  transfers between devices with their start and end apart: 5 -> 6, of which waited for: 3 -> 4; matrix products, arithmetic and copies ran while one was open for 10% -> 12% of each run, Pallas kernels for 22% -> 13%
where the time goes in v4:
time: 446 us; the launch traced here: 443 us
  waiting for transfers between devices  270 us (61%)
  Pallas kernels  58.4 us (13%)
  local copies, waits for them, and re-layouts  38.9 us (9%)
  matrix products  27.4 us (6%)
  starting transfers between devices  24.4 us (5%)
  between operations  13.8 us (3%)
  other arithmetic  10.2 us (2%)
    reduce_scatter x1, waiting for transfers between devices, per_device(): lax.psum_scatter(terms.astype(jnp.bfloat16), 'tok', scatter_dimension=0,...  86.3 us
    all_gather x1, waiting for transfers between devices, per_device(): lax.all_gather(normed, 'tok', axis=0, tiled=True)  71.3 us
    all_gather x1, waiting for transfers between devices, per_device(): gathered = [lax.all_gather(local_kv[0], 'tok', axis=0, tiled=True)]  63.3 us
    pallas_call x2, Pallas kernels, flash_attention(): pl.pallas_call(kernel, grid_spec=grid_spec, out_shape=jax.ShapeDtypeStruc...  58.4 us
    all_to_all x1, waiting for transfers between devices, per_device(): lax.all_to_all(send_rows.reshape(devices, capacity, width), ('req', 'tok'...  48.7 us
    all_to_all x1, starting transfers between devices, per_device(): lax.all_to_all(send_rows.reshape(devices, capacity, width), ('req', 'tok'...  21.1 us
    dot_general x1, matrix products, per_device(): jnp.dot(units.astype(jnp.bfloat16), w_down, preferred_element_type=jnp.fl...  15.2 us
    dot_general x1, matrix products, per_device(): jnp.dot(pick, hidden_all, preferred_element_type=jnp.float32)  11.6 us
  transfers between devices with their start and end apart: 6, of which 4 were waited for; matrix products, arithmetic and copies ran while one was open for 12% of the time, Pallas kernels for 13%

profile of v4, /device:TPU:0, one launch (start us, length us, event | category | flops | bytes accessed | tf_op | source)
XLA Modules:
  0.0 442.8 jit_solution(1062642660161786623)
XLA Ops:
  9.6 63.3 %all-gather.9.cloned.1.call-done = bf16[1,6144,256]{2,1,0:T(8,128)(2,1)} async-done(((bf16[1,768,256]{2,1,0:T(8,128)(2,1)}), bf16[1,6144,256]{2,1,0:T(8,128)(2,1)}) %all-gather.9.cloned.1.call-update) | async-done | bytes 3145744 | tf_op jit(solution)/shard_map/all_gather | solution.py:210
  76.7 3.2 all-to-all-start
  80.0 1.8 fusion.35
  85.9 3.2 add_add_fusion
  89.0 1.7 slice.83
  90.8 2.1 slice.85
  94.0 2.3 copy.60
  97.0 2.1 copy.61
  99.1 2.4 concatenate.19.cv_ref
  101.5 1.9 concatenate.20.nv_ref
  103.4 38.6 %shard_map.136 = bf16[1,4096,128]{2,1,0:T(8,128)(2,1)} custom-call(s32[3]{0:T(128)} %get-tuple-element.21.scal_ref, bf16[1,4096,128]{2,1,0:T(8,128)(2,1)} %slice.65.q_ref, bf16[1,4096,256]{2,1,0:T(8,128)(2,1)} %bitcast.45, bf16[1,136,4096]{2,1,0:T(8,128)(2,1)} %concatenate.19.cv_ref, bf16[1,2048,256]{2,1,0:T(8,128)(2,1)} %bitcast.50, ...), custom_call_target="tpu_custom_call" | custom-call | tf_op jit(solution)/shard_map/pallas_call | solution.py:169
  141.9 1.7 slice.87
  143.7 2.1 slice.89
  146.9 2.3 copy.62
  149.2 2.3 concatenate.21.cv_ref
  152.6 19.8 %shard_map.137 = bf16[1,4096,128]{2,1,0:T(8,128)(2,1)} custom-call(s32[3]{0:T(128)} %get-tuple-element.22.scal_ref, bf16[1,4096,128]{2,1,0:T(8,128)(2,1)} %slice.75.q_ref, bf16[1,4096,256]{2,1,0:T(8,128)(2,1)} %bitcast.43, bf16[1,136,4096]{2,1,0:T(8,128)(2,1)} %concatenate.21.cv_ref, bf16[1,2048,256]{2,1,0:T(8,128)(2,1)} %bitcast.48, ...), custom_call_target="tpu_custom_call" | custom-call | tf_op jit(solution)/shard_map/pallas_call | solution.py:169
  173.9 2.3 reshape.183
  176.2 11.6 %convolution_convert_fusion.1 = bf16[512,2048]{1,0:T(8,128)(2,1)} fusion(bf16[512,2048]{1,0:T(8,128)(2,1)} %bitcast.63, bf16[512,2048]{1,0:T(8,128)(2,1)} %reshape.183, bf16[2048,2048]{1,0:T(8,128)(2,1)} %param.20, f32[2048]{0:T(1024)S(1)} %copy-done.9, s32[512]{0:T(512)S(1)} %add_select_fusion.3), kind=kOutput, calls=%fused_computation.13 | convolution fusion | flops 5374214144 | bytes 14690304 | tf_op jit(solution)/shard_map/dot_general | solution.py:244
  187.8 21.1 %all-to-all-start.1 = ((bf16[32,16,2048]{2,1,0:T(8,128)(2,1)}), bf16[32,16,2048]{2,1,0:T(8,128)(2,1)S(1)}, u32[]{:S(2)}, u32[]{:S(2)}) async-start(bf16[32,16,2048]{2,1,0:T(8,128)(2,1)} %bitcast.57), calls=%async_computation.1 | async-start | bytes 4194304 | tf_op jit(solution)/shard_map/all_to_all | solution.py:255
  210.3 48.7 %all-to-all-done.1 = bf16[32,16,2048]{2,1,0:T(8,128)(2,1)S(1)} async-done(((bf16[32,16,2048]{2,1,0:T(8,128)(2,1)}), bf16[32,16,2048]{2,1,0:T(8,128)(2,1)S(1)}, u32[]{:S(2)}, u32[]{:S(2)}) %all-to-all-start.1) | async-done | bytes 2097184 | tf_op jit(solution)/shard_map/all_to_all | solution.py:255
  260.9 71.3 %all-gather.7.cloned.1.call-done = bf16[1024,2048]{1,0:T(8,128)(2,1)} async-done(((bf16[128,2048]{1,0:T(8,128)(2,1)}), bf16[1024,2048]{1,0:T(8,128)(2,1)}) %all-gather.7.cloned.1.call-update) | async-done | bytes 4194320 | tf_op jit(solution)/shard_map/all_gather | solution.py:282
  332.3 15.2 %convolution_convert_fusion = bf16[1024,2048]{1,0:T(8,128)(2,1)} fusion(bf16[1024,2048]{1,0:T(8,128)(2,1)} %param.26, f32[1024]{0:T(1024)S(1)} %copy-done.10, bf16[1024,2048]{1,0:T(8,128)(2,1)} %all-gather.7.cloned.1.call-done, bf16[2048,1024]{1,0:T(8,128)(2,1)} %param.24), kind=kOutput, calls=%fused_computation.12 | convolution fusion | flops 8602517504 | bytes 16781312 | tf_op jit(solution)/shard_map/dot_general | solution.py:289
  347.5 86.3 %reduce-scatter.2.cloned.1.call-done = bf16[128,2048]{1,0:T(8,128)(2,1)} async-done(((bf16[1024,2048]{1,0:T(8,128)(2,1)}), bf16[128,2048]{1,0:T(8,128)(2,1)}) %reduce-scatter.2.cloned.1.call-update) | async-done | bytes 524304 | tf_op jit(solution)/shard_map/reduce_scatter | solution.py:290
  433.9 2.0 add_convert_fusion
  (72 shorter events, 19.8 us)
Async XLA Ops:
  6.5 66.3 %all-gather.9.cloned.1.call-start = ((), (), s32[]{:S(2)}) async-start(), calls=%async_computation.6 | async-start | bytes 3538944 | tf_op jit(solution)/shard_map/all_gather | solution.py:210
  9.5 132.4 %all-gather.5.cloned.1.call-start = ((), (), s32[]{:S(2)}) async-start(), calls=%async_computation.3 | async-start | bytes 3538944 | tf_op jit(solution)/shard_map/all_gather | solution.py:213
  76.7 111.1 %all-to-all-start = ((s32[32,1,16]{2,1,0:T(1,128)}), s32[32,1,16]{2,1,0:T(1,128)S(1)}, u32[]{:S(2)}, u32[]{:S(2)}) async-start(s32[32,1,16]{2,1,0:T(1,128)} %bitcast.1), calls=%async_computation | async-start | bytes 32768 | tf_op jit(solution)/shard_map/all_to_all | solution.py:262
  80.0 4.4 %copy-start.11 = (s32[8]{0:T(128)S(1)}, s32[8]{0:T(128)}, u32[]{:S(2)}) copy-start(s32[8]{0:T(128)} %param.18) | copy-start | bytes 100
  80.0 5.2 %copy-start.5 = (s32[2,256]{1,0:T(2,128)S(1)}, s32[2,256]{1,0:T(2,128)}, u32[]{:S(2)}) copy-start(s32[2,256]{1,0:T(2,128)} %param.19) | copy-start | bytes 6148
  90.8 8.3 %copy-start.1 = (bf16[8,512,256]{2,1,0:T(8,128)(2,1)}, bf16[8,512,256]{2,1,0:T(8,128)(2,1)S(1)}, u32[]{:S(2)}) copy-start(bf16[8,512,256]{2,1,0:T(8,128)(2,1)S(1)} %slice.83) | copy-start | bytes 6291460
  92.9 8.6 %copy-start.3 = (bf16[8,256,256]{2,1,0:T(8,128)(2,1)}, bf16[8,256,256]{2,1,0:T(8,128)(2,1)S(1)}, u32[]{:S(2)}) copy-start(bf16[8,256,256]{2,1,0:T(8,128)(2,1)S(1)} %slice.85) | copy-start | bytes 3145732
  143.7 7.8 %copy-start = (bf16[8,512,256]{2,1,0:T(8,128)(2,1)}, bf16[8,512,256]{2,1,0:T(8,128)(2,1)S(1)}, u32[]{:S(2)}) copy-start(bf16[8,512,256]{2,1,0:T(8,128)(2,1)S(1)} %slice.87) | copy-start | bytes 6291460
  145.7 6.0 %copy-start.2 = (bf16[8,256,256]{2,1,0:T(8,128)(2,1)}, bf16[8,256,256]{2,1,0:T(8,128)(2,1)S(1)}, u32[]{:S(2)}) copy-start(bf16[8,256,256]{2,1,0:T(8,128)(2,1)S(1)} %slice.89) | copy-start | bytes 3145732
  151.8 20.7 %copy-start.4 = (bf16[1,4096,128]{2,1,0:T(8,128)(2,1)S(1)}, bf16[1,4096,128]{2,1,0:T(8,128)(2,1)}, u32[]{:S(2)}) copy-start(bf16[1,4096,128]{2,1,0:T(8,128)(2,1)} %shard_map.136) | copy-start | bytes 3145732
  172.4 3.7 copy-start.9
  187.8 72.0 %copy-start.6 = (f32[2048]{0:T(1024)S(1)}, f32[2048]{0:T(1024)}, u32[]{:S(2)}) copy-start(f32[2048]{0:T(1024)} %param.23) | copy-start | bytes 24580
  187.8 72.0 %copy-start.7 = (f32[2048]{0:T(1024)S(1)}, f32[2048]{0:T(1024)}, u32[]{:S(2)}) copy-start(f32[2048]{0:T(1024)} %param.22) | copy-start | bytes 24580
  187.8 71.2 %all-to-all-start.1 = ((bf16[32,16,2048]{2,1,0:T(8,128)(2,1)}), bf16[32,16,2048]{2,1,0:T(8,128)(2,1)S(1)}, u32[]{:S(2)}, u32[]{:S(2)}) async-start(bf16[32,16,2048]{2,1,0:T(8,128)(2,1)} %bitcast.57), calls=%async_computation.1 | async-start | bytes 4194304 | tf_op jit(solution)/shard_map/all_to_all | solution.py:255
  208.9 123.4 %copy-start.10 = (f32[1024]{0:T(1024)S(1)}, f32[1024]{0:T(1024)}, u32[]{:S(2)}) copy-start(f32[1024]{0:T(1024)} %param.25) | copy-start | bytes 12292
  208.9 123.3 %all-gather.7.cloned.1.call-start = ((), (), s32[]{:S(2)}) async-start(), calls=%async_computation.4 | async-start | bytes 4718592 | tf_op jit(solution)/shard_map/all_gather | solution.py:282
  260.9 173.0 %reduce-scatter.2.cloned.1.call-start = ((), (), s32[]{:S(2)}) async-start(), calls=%async_computation.5 | async-start | bytes 4718592 | tf_op jit(solution)/shard_map/reduce_scatter | solution.py:290
  347.5 86.3 %copy-start.8 = (f32[2048]{0:T(1024)S(1)}, f32[2048]{0:T(1024)}, u32[]{:S(2)}) copy-start(f32[2048]{0:T(1024)} %param.27) | copy-start | bytes 24580
Sparse Core Ops, SparseCore 0:
  9.7 63.1 all-gather.8
  75.0 59.0 all-gather.4
  261.0 71.2 all-gather.6
  347.7 86.1 reduce-scatter.1

commit v5 on v4

--- a/solution.py
+++ b/solution.py
@@ -27,19 +27,17 @@
     acc_sc,
     *,
     tq,
-    head_dim,
     tk,
     heads,
+    head_dim,
     n_cache,
-    n_req,
     scale,
 ):
-    r = pl.program_id(0)
     qi = pl.program_id(1)
     ki = pl.program_id(2)
-    prefix = scal_ref[r]
-    live = scal_ref[n_req + r]
-    base = scal_ref[2 * n_req]
+    prefix = scal_ref[0]
+    live = scal_ref[1]
+    base = scal_ref[2]
     spt = tq // heads
     tile_lo = qi * spt
     tile_live = tile_lo < live
@@ -52,9 +50,11 @@
         acc_sc[...] = jnp.zeros(acc_sc.shape, jnp.float32)
 
     def step(k_ref, v_ref, mask_fn):
+        pieces, chunk = k_ref.shape[0], k_ref.shape[1]
+        k = k_ref[...].reshape(pieces * chunk, head_dim)
         s = (
             lax.dot_general(
-                k_ref[0], q_ref[0], (((1,), (1,)), ((), ())), preferred_element_type=jnp.float32
+                k, q_ref[0], (((1,), (1,)), ((), ())), preferred_element_type=jnp.float32
             )
             * scale
         )
@@ -68,9 +68,15 @@
         if mask is not None:
             p = jnp.where(mask, p, 0.0)
         alpha = jnp.exp(m_prev - m_new)
-        acc_sc[...] = alpha * acc_sc[...] + jnp.dot(
-            v_ref[0], p.astype(jnp.bfloat16), preferred_element_type=jnp.float32
-        )
+        pb = p.astype(jnp.bfloat16)
+        total = alpha * acc_sc[...]
+        for piece in range(pieces):
+            total = total + jnp.dot(
+                v_ref[piece],
+                pb[piece * chunk : (piece + 1) * chunk],
+                preferred_element_type=jnp.float32,
+            )
+        acc_sc[...] = total
         m_sc[...] = m_new
 
     is_cache = ki < n_cache
@@ -115,28 +121,32 @@
         o_ref[0] = jnp.transpose(out).astype(o_ref.dtype)
 
 
-def flash_attention(q, ckv, nkv, scal, heads, tq, tk):
+def flash_attention(q, req, both, scal, heads, tq, tk, prefix_dev, slot_dev):
     n_req, rows, head_dim = q.shape
-    n_cache = ckv.shape[1] // tk
-    n_new = nkv.shape[1] // tk
+    n_member = both.shape[0]
+    n_cache = n_member * prefix_dev // tk
+    n_new = n_member * slot_dev // tk
+    per_cache = tk // prefix_dev
+    per_new = tk // slot_dev
+    new_at = prefix_dev // slot_dev
     spt = tq // heads
     scale = 1.0 / math.sqrt(head_dim)
-    ones = jnp.ones((n_req, 8, 1), jnp.bfloat16)
-    cvt = jnp.swapaxes(ckv[:, :, head_dim:], 1, 2)
-    cvt = jnp.concatenate([cvt, jnp.broadcast_to(ones, (n_req, 8, cvt.shape[2]))], axis=1)
-    nvt = jnp.swapaxes(nkv[:, :, head_dim:], 1, 2)
-    nvt = jnp.concatenate([nvt, jnp.broadcast_to(ones, (n_req, 8, nvt.shape[2]))], axis=1)
+    ones = jnp.ones((n_member, 8, both.shape[1]), jnp.bfloat16)
+    vt = jnp.concatenate([jnp.swapaxes(both[:, :, head_dim:], 1, 2), ones], axis=1)
     ext = head_dim + 8
 
     def q_map(r, qi, ki, s):
-        return (r, qi, 0)
-
-    def c_block(r, ki, s):
-        last = jnp.maximum((s[r] + tk - 1) // tk - 1, 0)
+        return (req, qi, 0)
+
+    def o_map(r, qi, ki, s):
+        return (0, qi, 0)
+
+    def c_block(ki, s):
+        last = jnp.maximum((s[0] + tk - 1) // tk - 1, 0)
         return jnp.minimum(ki, last)
 
-    def n_block(r, qi, ki, s):
-        q_hi = s[2 * n_req] + (qi + 1) * spt - 1
+    def n_block(qi, ki, s):
+        q_hi = s[2] + (qi + 1) * spt - 1
         last = jnp.minimum(q_hi // tk, n_new - 1)
         return jnp.clip(ki - n_cache, 0, last)
 
@@ -147,20 +157,31 @@
         heads=heads,
         head_dim=head_dim,
         n_cache=n_cache,
-        n_req=n_req,
         scale=scale,
     )
     grid_spec = pltpu.PrefetchScalarGridSpec(
         num_scalar_prefetch=1,
-        grid=(n_req, rows // tq, n_cache + n_new),
+        grid=(1, rows // tq, n_cache + n_new),
         in_specs=[
             pl.BlockSpec((1, tq, head_dim), q_map),
-            pl.BlockSpec((1, tk, head_dim), lambda r, qi, ki, s: (r, c_block(r, ki, s), 0)),
-            pl.BlockSpec((1, ext, tk), lambda r, qi, ki, s: (r, 0, c_block(r, ki, s))),
-            pl.BlockSpec((1, tk, head_dim), lambda r, qi, ki, s: (r, n_block(r, qi, ki, s), 0)),
-            pl.BlockSpec((1, ext, tk), lambda r, qi, ki, s: (r, 0, n_block(r, qi, ki, s))),
+            pl.BlockSpec(
+                (per_cache, prefix_dev, head_dim),
+                lambda r, qi, ki, s: (c_block(ki, s), 0, 0),
+            ),
+            pl.BlockSpec(
+                (per_cache, ext, prefix_dev),
+                lambda r, qi, ki, s: (c_block(ki, s), 0, 0),
+            ),
+            pl.BlockSpec(
+                (per_new, slot_dev, head_dim),
+                lambda r, qi, ki, s: (n_block(qi, ki, s), new_at, 0),
+            ),
+            pl.BlockSpec(
+                (per_new, ext, slot_dev),
+                lambda r, qi, ki, s: (n_block(qi, ki, s), 0, new_at),
+            ),
         ],
-        out_specs=pl.BlockSpec((1, tq, head_dim), q_map),
+        out_specs=pl.BlockSpec((1, tq, head_dim), o_map),
         scratch_shapes=[
             pltpu.VMEM((1, tq), jnp.float32),
             pltpu.VMEM((ext, tq), jnp.float32),
@@ -169,8 +190,8 @@
     return pl.pallas_call(
         kernel,
         grid_spec=grid_spec,
-        out_shape=jax.ShapeDtypeStruct((n_req, rows, head_dim), jnp.bfloat16),
-    )(scal, q, ckv, cvt, nkv, nvt)
+        out_shape=jax.ShapeDtypeStruct((1, rows, head_dim), jnp.bfloat16),
+    )(scal, q, both, vt, both, vt)
 
 
 def per_device(
@@ -205,31 +226,7 @@
     tk = 1024
     q_flat = queries.reshape(req_dev, rows, head_dim)
 
-    prefix_dev = cache_kv.shape[1]
-    local_kv = jnp.concatenate([cache_kv, new_kv], axis=1)
-    gathered = [lax.all_gather(local_kv[0], "tok", axis=0, tiled=True)]
-    for r in range(1, req_dev):
-        mine, gathered[-1] = lax.optimization_barrier((local_kv[r], gathered[-1]))
-        gathered.append(lax.all_gather(mine, "tok", axis=0, tiled=True))
-    outs = []
-    for r in range(req_dev):
-        both = gathered[r].reshape(n_member, prefix_dev + slot_dev, local_kv.shape[-1])
-        ck = both[:, :prefix_dev].reshape(n_member * prefix_dev, local_kv.shape[-1])
-        nk = both[:, prefix_dev:].reshape(n_member * slot_dev, local_kv.shape[-1])
-        scal = jnp.stack([own_prefix[r], live_count[r], base]).astype(jnp.int32)
-        outs.append(
-            flash_attention(q_flat[r : r + 1], ck[None], nk[None], scal, heads, tq, tk)
-        )
-    attended = jnp.concatenate(outs, axis=0)
     slots = req_dev * slot_dev
-    attended = attended.reshape(slots, width)
-    residual_flat = residual.reshape(slots, width)
-    hidden_all = (
-        residual_flat.astype(jnp.float32)
-        + jnp.dot(attended, w_out, preferred_element_type=jnp.float32)
-        + b_out
-    ).astype(jnp.bfloat16)
-
     capacity = (slots + devices - 1) // devices
     target = dest_map.reshape(slots)
     is_live = target >= 0
@@ -241,9 +238,6 @@
     pick = (
         where_to[None, :] == jnp.arange(send_slots, dtype=jnp.int32)[:, None]
     ).astype(jnp.bfloat16)
-    send_rows = jnp.dot(pick, hidden_all, preferred_element_type=jnp.float32).astype(
-        jnp.bfloat16
-    )
     row_ids = jnp.sum(
         jnp.where(
             where_to[None, :] == jnp.arange(send_slots, dtype=jnp.int32)[:, None],
@@ -252,6 +246,39 @@
         ),
         axis=1,
     ) - 1
+    ids_in = lax.all_to_all(
+        row_ids.reshape(devices, capacity),
+        ("req", "tok"),
+        split_axis=0,
+        concat_axis=0,
+        tiled=True,
+    ).reshape(send_slots)
+    prefix_dev = cache_kv.shape[1]
+    local_kv = jnp.concatenate([cache_kv, new_kv], axis=1)
+    gathered = [lax.all_gather(local_kv[0], "tok", axis=0, tiled=True)]
+    gathered[0], pick, ids_in = lax.optimization_barrier((gathered[0], pick, ids_in))
+    for r in range(1, req_dev):
+        mine, gathered[-1] = lax.optimization_barrier((local_kv[r], gathered[-1]))
+        gathered.append(lax.all_gather(mine, "tok", axis=0, tiled=True))
+    outs = []
+    for r in range(req_dev):
+        both = gathered[r].reshape(n_member, prefix_dev + slot_dev, local_kv.shape[-1])
+        scal = jnp.stack([own_prefix[r], live_count[r], base]).astype(jnp.int32)
+        outs.append(
+            flash_attention(q_flat, r, both, scal, heads, tq, tk, prefix_dev, slot_dev)
+        )
+    attended = jnp.concatenate(outs, axis=0)
+    attended = attended.reshape(slots, width)
+    residual_flat = residual.reshape(slots, width)
+    hidden_all = (
+        residual_flat.astype(jnp.float32)
+        + jnp.dot(attended, w_out, preferred_element_type=jnp.float32)
+        + b_out
+    ).astype(jnp.bfloat16)
+
+    send_rows = jnp.dot(pick, hidden_all, preferred_element_type=jnp.float32).astype(
+        jnp.bfloat16
+    )
     rows_in = lax.all_to_all(
         send_rows.reshape(devices, capacity, width),
         ("req", "tok"),
@@ -259,13 +286,6 @@
         concat_axis=0,
         tiled=True,
     ).reshape(send_slots, width)
-    ids_in = lax.all_to_all(
-        row_ids.reshape(devices, capacity),
-        ("req", "tok"),
-        split_axis=0,
-        concat_axis=0,
-        tiled=True,
-    ).reshape(send_slots)
     land = (ids_in[None, :] == jnp.arange(TOK_DEV, dtype=jnp.int32)[:, None]).astype(
         jnp.bfloat16
     )

time: 446 us -> 433 us (0.971); the launches traced: 443 us -> 425 us
  blocking collectives: 0 us -> 69.3 us
  waiting for transfers between devices: 270 us -> 217 us
  starting transfers between devices: 24.4 us -> 7.42 us
  local copies, waits for them, and re-layouts: 38.9 us -> 22 us
    all_to_all x0 -> x1, blocking collectives: none -> 69.3 us  [per_device(): lax.all_to_all(send_rows.reshape(devices, capacity, width), ('req', 'tok'...]
    all_to_all x1 -> x0, waiting for transfers between devices: 48.7 us -> none  [per_device(): lax.all_to_all(send_rows.reshape(devices, capacity, width), ('req', 'tok'...]
    all_to_all x1 -> x0, starting transfers between devices: 21.1 us -> none  [per_device(): lax.all_to_all(send_rows.reshape(devices, capacity, width), ('req', 'tok'...]
    all_gather x1, waiting for transfers between devices: 63.3 us -> 43.8 us  [per_device(): gathered = [lax.all_gather(local_kv[0], 'tok', axis=0, tiled=True)]]
    slice x13 -> x3, local copies, waits for them, and re-layouts: 16.3 us -> 3.24 us  [the longest x2 3.02 us: flash_attention(): both[:, :, head_dim:]]
    all_gather x1, waiting for transfers between devices: 0.01 us -> 9.78 us  [per_device(): gathered.append(lax.all_gather(mine, 'tok', axis=0, tiled=True))]
    all_to_all x1, waiting for transfers between devices: 0.01 us -> 6.14 us  [per_device(): lax.all_to_all(row_ids.reshape(devices, capacity), ('req', 'tok'), split_...]
    concatenate x4 -> x2, local copies, waits for them, and re-layouts: 7.44 us -> 2.68 us  [flash_attention(): jnp.concatenate([jnp.swapaxes(both[:, :, head_dim:], 1, 2), ones], axis=1)]
  transfers between devices with their start and end apart: 6 -> 5, of which waited for: 4 -> 5; matrix products, arithmetic and copies ran while one was open for 12% -> 5% of each run, Pallas kernels for 13% -> 9%
where the time goes in v5:
time: 433 us; the launch traced here: 425 us
  waiting for transfers between devices  217 us (50%)
  blocking collectives  69.3 us (16%)
  Pallas kernels  58 us (13%)
  matrix products  26 us (6%)
  local copies, waits for them, and re-layouts  22 us (5%)
  between operations  13.8 us (3%)
  other arithmetic  10.9 us (3%)
  starting transfers between devices  7.42 us (2%)
    reduce_scatter x1, waiting for transfers between devices, per_device(): lax.psum_scatter(terms.astype(jnp.bfloat16), 'tok', scatter_dimension=0,...  86.3 us
    all_gather x1, waiting for transfers between devices, per_device(): lax.all_gather(normed, 'tok', axis=0, tiled=True)  71.2 us
    all_to_all x1, blocking collectives, per_device(): lax.all_to_all(send_rows.reshape(devices, capacity, width), ('req', 'tok'...  69.3 us
    pallas_call x2, Pallas kernels, flash_attention(): pl.pallas_call(kernel, grid_spec=grid_spec, out_shape=jax.ShapeDtypeStruc...  58 us
    all_gather x1, waiting for transfers between devices, per_device(): gathered = [lax.all_gather(local_kv[0], 'tok', axis=0, tiled=True)]  43.8 us
    dot_general x1, matrix products, per_device(): jnp.dot(units.astype(jnp.bfloat16), w_down, preferred_element_type=jnp.fl...  15.3 us
    dot_general x1, matrix products, per_device(): jnp.dot(pick, hidden_all, preferred_element_type=jnp.float32)  10.2 us
    all_gather x1, waiting for transfers between devices, per_device(): gathered.append(lax.all_gather(mine, 'tok', axis=0, tiled=True))  9.78 us
  transfers between devices with their start and end apart: 5, of which 5 were waited for; matrix products, arithmetic and copies ran while one was open for 5% of the time, Pallas kernels for 9%

profile of v5, /device:TPU:0, one launch (start us, length us, event | category | flops | bytes accessed | tf_op | source)
XLA Modules:
  0.0 424.7 jit_solution(11180144178869993312)
XLA Ops:
  6.5 1.1 constant_dynamic-update-slice_fusion.1
  11.0 1.2 reduce-window.6
  13.5 7.3 %all-to-all-start = ((s32[32,1,16]{2,1,0:T(1,128)}), s32[32,1,16]{2,1,0:T(1,128)S(1)}, u32[]{:S(2)}, u32[]{:S(2)}) async-start(s32[32,1,16]{2,1,0:T(1,128)} %bitcast.2), calls=%async_computation | async-start | bytes 32768 | tf_op jit(solution)/shard_map/all_to_all | solution.py:249
  21.8 6.1 %all-to-all-done = s32[32,1,16]{2,1,0:T(1,128)S(1)} async-done(((s32[32,1,16]{2,1,0:T(1,128)}), s32[32,1,16]{2,1,0:T(1,128)S(1)}, u32[]{:S(2)}, u32[]{:S(2)}) %all-to-all-start) | async-done | bytes 2080 | tf_op jit(solution)/shard_map/all_to_all | solution.py:249
  29.2 43.8 %all-gather.9.cloned.1.call-done = bf16[1,6144,256]{2,1,0:T(8,128)(2,1)} async-done(((bf16[1,768,256]{2,1,0:T(8,128)(2,1)}), bf16[1,6144,256]{2,1,0:T(8,128)(2,1)}) %all-gather.9.cloned.1.call-update) | async-done | bytes 3145744 | tf_op jit(solution)/shard_map/all_gather | solution.py:258
  73.1 4.4 %reshape.185.q_ref = bf16[2,4096,128]{2,1,0:T(8,128)(2,1)} reshape(bf16[2,256,2048]{2,1,0:T(8,128)(2,1)} %param.14) | data formatting | bytes 4194304 | tf_op jit(solution)/shard_map/reshape | solution.py:227
  78.8 3.0 add_add_fusion
  81.8 1.5 slice.43
  83.3 1.7 copy.30
  85.0 1.4 concatenate.13.cv_ref.nv_ref
  86.4 38.1 %shard_map.136 = bf16[1,4096,128]{2,1,0:T(8,128)(2,1)} custom-call(s32[3]{0:T(128)} %get-tuple-element.25.scal_ref, bf16[2,4096,128]{2,1,0:T(8,128)(2,1)} %reshape.185.q_ref, bf16[8,768,256]{2,1,0:T(8,128)(2,1)} %bitcast.37, bf16[8,136,768]{2,1,0:T(8,128)(2,1)} %concatenate.13.cv_ref.nv_ref, bf16[8,768,256]{2,1,0:T(8,128)(2,1)} %bitcast.38, ...), custom_call_target="tpu_custom_call" | custom-call | tf_op jit(solution)/shard_map/pallas_call | solution.py:190
  124.5 9.8 %all-gather.5.cloned.1.call-done = bf16[6144,256]{1,0:T(8,128)(2,1)} async-done(((bf16[768,256]{1,0:T(8,128)(2,1)}), bf16[6144,256]{1,0:T(8,128)(2,1)}) %all-gather.5.cloned.1.call-update) | async-done | bytes 3145744 | tf_op jit(solution)/shard_map/all_gather | solution.py:262
  134.3 1.5 slice.44
  136.5 1.3 concatenate.14.cv_ref.nv_ref
  137.8 19.9 %shard_map.137 = bf16[1,4096,128]{2,1,0:T(8,128)(2,1)} custom-call(s32[3]{0:T(128)} %get-tuple-element.26.scal_ref, bf16[2,4096,128]{2,1,0:T(8,128)(2,1)} %reshape.185.q_ref, bf16[8,768,256]{2,1,0:T(8,128)(2,1)} %bitcast.41, bf16[8,136,768]{2,1,0:T(8,128)(2,1)} %concatenate.14.cv_ref.nv_ref, bf16[8,768,256]{2,1,0:T(8,128)(2,1)} %bitcast.42, ...), custom_call_target="tpu_custom_call" | custom-call | tf_op jit(solution)/shard_map/pallas_call | solution.py:190
  157.8 1.4 pad_maximum_fusion
  159.2 2.3 reshape.188
  161.6 10.2 %convolution_convert_fusion.1 = bf16[512,2048]{1,0:T(8,128)(2,1)S(1)} fusion(bf16[512,512]{1,0:T(8,128)(2,1)S(1)} %copy-done.2, bf16[512,2048]{1,0:T(8,128)(2,1)} %bitcast.50, bf16[512,2048]{1,0:T(8,128)(2,1)} %reshape.188, bf16[2048,2048]{1,0:T(8,128)(2,1)} %param.20, f32[2048]{0:T(1024)S(1)} %copy-done.7), kind=kOutput, calls=%fused_computation.13 | convolution fusion | flops 5373952000 | bytes 15212544 | tf_op jit(solution)/shard_map/dot_general | solution.py:279
  171.8 69.3 %all_to_all.11 = bf16[32,16,2048]{2,1,0:T(8,128)(2,1)S(1)} all-to-all(bf16[32,16,2048]{2,1,0:T(8,128)(2,1)S(1)} %bitcast.46), channel_id=1, replica_groups=mesh['req'=4,'tok'=8] {'req','tok'}, dimensions={0} | all-to-all | bytes 4194304 | tf_op jit(solution)/shard_map/all_to_all | solution.py:282
  241.9 1.0 add_convert_fusion.1
  243.0 71.2 %all-gather.7.cloned.1.call-done = bf16[1024,2048]{1,0:T(8,128)(2,1)} async-done(((bf16[128,2048]{1,0:T(8,128)(2,1)}), bf16[1024,2048]{1,0:T(8,128)(2,1)}) %all-gather.7.cloned.1.call-update) | async-done | bytes 4194320 | tf_op jit(solution)/shard_map/all_gather | solution.py:302
  314.2 15.3 %convolution_convert_fusion = bf16[1024,2048]{1,0:T(8,128)(2,1)} fusion(bf16[1024,2048]{1,0:T(8,128)(2,1)} %param.26, f32[1024]{0:T(1024)S(1)} %copy-done.8, bf16[1024,2048]{1,0:T(8,128)(2,1)} %all-gather.7.cloned.1.call-done, bf16[2048,1024]{1,0:T(8,128)(2,1)} %param.24), kind=kOutput, calls=%fused_computation.12 | convolution fusion | flops 8602517504 | bytes 16781312 | tf_op jit(solution)/shard_map/dot_general | solution.py:309
  329.5 86.3 %reduce-scatter.2.cloned.1.call-done = bf16[128,2048]{1,0:T(8,128)(2,1)} async-done(((bf16[1024,2048]{1,0:T(8,128)(2,1)}), bf16[128,2048]{1,0:T(8,128)(2,1)}) %reduce-scatter.2.cloned.1.call-update) | async-done | bytes 524304 | tf_op jit(solution)/shard_map/reduce_scatter | solution.py:310
  415.8 2.0 add_convert_fusion
  (56 shorter events, 9.9 us)
Async XLA Ops:
  6.5 66.5 %all-gather.9.cloned.1.call-start = ((), (), s32[]{:S(2)}) async-start(), calls=%async_computation.6 | async-start | bytes 3538944 | tf_op jit(solution)/shard_map/all_gather | solution.py:258
  7.6 69.9 %copy-start.9 = (s32[8]{0:T(128)S(1)}, s32[8]{0:T(128)}, u32[]{:S(2)}) copy-start(s32[8]{0:T(128)} %param.18) | copy-start | bytes 100
  7.6 70.5 %copy-start.3 = (s32[2,256]{1,0:T(2,128)S(1)}, s32[2,256]{1,0:T(2,128)}, u32[]{:S(2)}) copy-start(s32[2,256]{1,0:T(2,128)} %param.19) | copy-start | bytes 6148
  13.5 14.4 %all-to-all-start = ((s32[32,1,16]{2,1,0:T(1,128)}), s32[32,1,16]{2,1,0:T(1,128)S(1)}, u32[]{:S(2)}, u32[]{:S(2)}) async-start(s32[32,1,16]{2,1,0:T(1,128)} %bitcast.2), calls=%async_computation | async-start | bytes 32768 | tf_op jit(solution)/shard_map/all_to_all | solution.py:249
  20.8 113.5 %all-gather.5.cloned.1.call-start = ((), (), s32[]{:S(2)}) async-start(), calls=%async_computation.3 | async-start | bytes 3538944 | tf_op jit(solution)/shard_map/all_gather | solution.py:262
  73.0 8.8 %copy-start = (bf16[1,6144,256]{2,1,0:T(8,128)(2,1)S(1)}, bf16[1,6144,256]{2,1,0:T(8,128)(2,1)}, u32[]{:S(2)}) copy-start(bf16[1,6144,256]{2,1,0:T(8,128)(2,1)} %all-gather.9.cloned.1.call-done) | copy-start | bytes 9437188
  73.0 241.1 %all-gather.7.cloned.1.call-start = ((), (), s32[]{:S(2)}) async-start(), calls=%async_computation.4 | async-start | bytes 4718592 | tf_op jit(solution)/shard_map/all_gather | solution.py:302
  137.8 19.9 %copy-start.1 = (bf16[1,4096,128]{2,1,0:T(8,128)(2,1)S(1)}, bf16[1,4096,128]{2,1,0:T(8,128)(2,1)}, u32[]{:S(2)}) copy-start(bf16[1,4096,128]{2,1,0:T(8,128)(2,1)} %shard_map.136) | copy-start | bytes 3145732
  157.8 3.8 copy-start.7
  159.2 2.3 copy-start.2
  171.7 70.1 %copy-start.4 = (f32[2048]{0:T(1024)S(1)}, f32[2048]{0:T(1024)}, u32[]{:S(2)}) copy-start(f32[2048]{0:T(1024)} %param.23) | copy-start | bytes 24580
  171.8 70.1 %copy-start.5 = (f32[2048]{0:T(1024)S(1)}, f32[2048]{0:T(1024)}, u32[]{:S(2)}) copy-start(f32[2048]{0:T(1024)} %param.22) | copy-start | bytes 24580
  241.0 73.1 %copy-start.8 = (f32[1024]{0:T(1024)S(1)}, f32[1024]{0:T(1024)}, u32[]{:S(2)}) copy-start(f32[1024]{0:T(1024)} %param.25) | copy-start | bytes 12292
  242.9 172.8 %reduce-scatter.2.cloned.1.call-start = ((), (), s32[]{:S(2)}) async-start(), calls=%async_computation.5 | async-start | bytes 4718592 | tf_op jit(solution)/shard_map/reduce_scatter | solution.py:310
  329.4 86.3 %copy-start.6 = (f32[2048]{0:T(1024)S(1)}, f32[2048]{0:T(1024)}, u32[]{:S(2)}) copy-start(f32[2048]{0:T(1024)} %param.27) | copy-start | bytes 24580
Sparse Core Ops, SparseCore 0:
  9.7 63.2 all-gather.8
  75.2 59.0 all-gather.4
  243.1 71.0 all-gather.6
  329.6 86.1 reduce-scatter.1

commit v6 on v5

--- a/solution.py
+++ b/solution.py
@@ -121,18 +121,24 @@
         o_ref[0] = jnp.transpose(out).astype(o_ref.dtype)
 
 
-def flash_attention(q, req, both, scal, heads, tq, tk, prefix_dev, slot_dev):
+def flash_attention(q, req, gc, gn, scal, heads, tq, tk):
     n_req, rows, head_dim = q.shape
-    n_member = both.shape[0]
+    n_member, prefix_dev = gc.shape[0], gc.shape[1]
+    slot_dev = gn.shape[1]
     n_cache = n_member * prefix_dev // tk
     n_new = n_member * slot_dev // tk
     per_cache = tk // prefix_dev
     per_new = tk // slot_dev
-    new_at = prefix_dev // slot_dev
     spt = tq // heads
     scale = 1.0 / math.sqrt(head_dim)
-    ones = jnp.ones((n_member, 8, both.shape[1]), jnp.bfloat16)
-    vt = jnp.concatenate([jnp.swapaxes(both[:, :, head_dim:], 1, 2), ones], axis=1)
+    vc = jnp.concatenate(
+        [jnp.swapaxes(gc[:, :, head_dim:], 1, 2), jnp.ones((n_member, 8, prefix_dev), gc.dtype)],
+        axis=1,
+    )
+    vn = jnp.concatenate(
+        [jnp.swapaxes(gn[:, :, head_dim:], 1, 2), jnp.ones((n_member, 8, slot_dev), gn.dtype)],
+        axis=1,
+    )
     ext = head_dim + 8
 
     def q_map(r, qi, ki, s):
@@ -174,11 +180,11 @@
             ),
             pl.BlockSpec(
                 (per_new, slot_dev, head_dim),
-                lambda r, qi, ki, s: (n_block(qi, ki, s), new_at, 0),
+                lambda r, qi, ki, s: (n_block(qi, ki, s), 0, 0),
             ),
             pl.BlockSpec(
                 (per_new, ext, slot_dev),
-                lambda r, qi, ki, s: (n_block(qi, ki, s), 0, new_at),
+                lambda r, qi, ki, s: (n_block(qi, ki, s), 0, 0),
             ),
         ],
         out_specs=pl.BlockSpec((1, tq, head_dim), o_map),
@@ -191,7 +197,7 @@
         kernel,
         grid_spec=grid_spec,
         out_shape=jax.ShapeDtypeStruct((1, rows, head_dim), jnp.bfloat16),
-    )(scal, q, both, vt, both, vt)
+    )(scal, q, gc, vc, gn, vn)
 
 
 def per_device(
@@ -253,20 +259,33 @@
         concat_axis=0,
         tiled=True,
     ).reshape(send_slots)
-    prefix_dev = cache_kv.shape[1]
-    local_kv = jnp.concatenate([cache_kv, new_kv], axis=1)
-    gathered = [lax.all_gather(local_kv[0], "tok", axis=0, tiled=True)]
+    def exchange(cache_r, new_r):
+        cache_in = [cache_r]
+        new_in = [new_r]
+        for step in range(n_member - 1, 0, -1):
+            cache_in.append(
+                lax.ppermute(
+                    cache_r, "tok", [(i, (i + step) % n_member) for i in range(n_member)]
+                )
+            )
+            new_in.append(
+                lax.ppermute(new_r, "tok", [(i, i + step) for i in range(n_member - step)])
+            )
+        return (
+            jnp.roll(jnp.stack(cache_in), member, axis=0),
+            jnp.roll(jnp.stack(new_in), member, axis=0),
+        )
+
+    gathered = [exchange(cache_kv[0], new_kv[0])]
     gathered[0], pick, ids_in = lax.optimization_barrier((gathered[0], pick, ids_in))
     for r in range(1, req_dev):
-        mine, gathered[-1] = lax.optimization_barrier((local_kv[r], gathered[-1]))
-        gathered.append(lax.all_gather(mine, "tok", axis=0, tiled=True))
+        mine, gathered[-1] = lax.optimization_barrier(((cache_kv[r], new_kv[r]), gathered[-1]))
+        gathered.append(exchange(*mine))
     outs = []
     for r in range(req_dev):
-        both = gathered[r].reshape(n_member, prefix_dev + slot_dev, local_kv.shape[-1])
+        gc, gn = gathered[r]
         scal = jnp.stack([own_prefix[r], live_count[r], base]).astype(jnp.int32)
-        outs.append(
-            flash_attention(q_flat, r, both, scal, heads, tq, tk, prefix_dev, slot_dev)
-        )
+        outs.append(flash_attention(q_flat, r, gc, gn, scal, heads, tq, tk))
     attended = jnp.concatenate(outs, axis=0)
     attended = attended.reshape(slots, width)
     residual_flat = residual.reshape(slots, width)

time: 433 us -> 518 us (1.20); the launches traced: 425 us -> 516 us
  starting transfers between devices: 7.42 us -> 77.6 us
  local copies, waits for them, and re-layouts: 22 us -> 45.7 us
  blocking collectives: 69.3 us -> 51.8 us
  Pallas kernels: 58 us -> 64.5 us
  other arithmetic: 10.9 us -> 16.5 us
    ppermute x0 -> x28, starting transfers between devices: none -> 75.1 us  [the longest x14 52.5 us: exchange(): lax.ppermute(new_r, 'tok', [(i, i + step) for i in range(n_member - step)])]
    ppermute x0 -> x28, waiting for transfers between devices: none -> 55.4 us  [the longest x14 33.3 us: exchange(): lax.ppermute(cache_r, 'tok', [(i, (i + step) % n_member) for i in range(n...]
    all_gather x2 -> x0, waiting for transfers between devices: 53.6 us -> none  [the longest x1 43.8 us: per_device(): gathered = [lax.all_gather(local_kv[0], 'tok', axis=0, tiled=True)]]
    all_to_all x1, blocking collectives: 69.3 us -> 51.8 us  [per_device(): lax.all_to_all(send_rows.reshape(devices, capacity, width), ('req', 'tok'...]
    unnamed x24 -> x55, local copies, waits for them, and re-layouts: 4.22 us -> 20.5 us
    pallas_call x2, Pallas kernels: 58 us -> 64.5 us  [flash_attention(): pl.pallas_call(kernel, grid_spec=grid_spec, out_shape=jax.ShapeDtypeStruc...]
    concatenate x0 -> x4, other arithmetic: none -> 5.47 us  [the longest x2 4.68 us: exchange(): jnp.roll(jnp.stack(cache_in), member, axis=0)]
  transfers between devices with their start and end apart: 5 -> 31, of which waited for: 5 -> 16; matrix products, arithmetic and copies ran while one was open for 5% -> 7% of each run, Pallas kernels for 9% -> 5%
where the time goes in v6:
time: 518 us; the launch traced here: 516 us
  waiting for transfers between devices  220 us (42%)
  starting transfers between devices  77.6 us (15%)
  Pallas kernels  64.5 us (12%)
  blocking collectives  51.8 us (10%)
  local copies, waits for them, and re-layouts  45.7 us (9%)
  matrix products  26 us (5%)
  other arithmetic  16.5 us (3%)
  between operations  14.1 us (3%)
    reduce_scatter x1, waiting for transfers between devices, per_device(): lax.psum_scatter(terms.astype(jnp.bfloat16), 'tok', scatter_dimension=0,...  86.5 us
    all_gather x1, waiting for transfers between devices, per_device(): lax.all_gather(normed, 'tok', axis=0, tiled=True)  71.1 us
    pallas_call x2, Pallas kernels, flash_attention(): pl.pallas_call(kernel, grid_spec=grid_spec, out_shape=jax.ShapeDtypeStruc...  64.5 us
    ppermute x14, starting transfers between devices, exchange(): lax.ppermute(new_r, 'tok', [(i, i + step) for i in range(n_member - step)])  52.5 us
    all_to_all x1, blocking collectives, per_device(): lax.all_to_all(send_rows.reshape(devices, capacity, width), ('req', 'tok'...  51.8 us
    ppermute x14, waiting for transfers between devices, exchange(): lax.ppermute(cache_r, 'tok', [(i, (i + step) % n_member) for i in range(n...  33.3 us
    ppermute x14, starting transfers between devices, exchange(): lax.ppermute(cache_r, 'tok', [(i, (i + step) % n_member) for i in range(n...  22.5 us
    ppermute x14, waiting for transfers between devices, exchange(): lax.ppermute(new_r, 'tok', [(i, i + step) for i in range(n_member - step)])  22.1 us
  transfers between devices with their start and end apart: 31, of which 16 were waited for; matrix products, arithmetic and copies ran while one was open for 7% of the time, Pallas kernels for 5%

profile of v6, /device:TPU:0, one launch (start us, length us, event | category | flops | bytes accessed | tf_op | source)
XLA Modules:
  0.0 516.0 jit_solution(5267840533784093645)
XLA Ops:
  9.2 6.0 %collective-permute-start = (bf16[512,256]{0,1:T(8,128)(2,1)}, bf16[512,256]{0,1:T(8,128)(2,1)}, u32[]{:S(2)}, u32[]{:S(2)}) collective-permute-start(bf16[512,256]{0,1:T(8,128)(2,1)} %bitcast), channel_id=1, source_target_pairs={{0,7},{1,0},{2,1},{3,2},{4,3},{5,4},{6,5},{7,6},{8,15},{9,8},{10,9... | collective-permute-start | bytes 786440 | tf_op jit(solution)/shard_map/ppermute | solution.py:267
  15.7 3.0 collective-permute-start.3
  21.0 4.9 collective-permute-start.7
  35.9 3.1 add_add_fusion
  43.5 6.7 %all-to-all-done = s32[32,1,16]{2,1,0:T(1,128)S(1)} async-done(((s32[32,1,16]{2,1,0:T(1,128)}), s32[32,1,16]{2,1,0:T(1,128)S(1)}, u32[]{:S(2)}, u32[]{:S(2)}) %all-to-all-start) | async-done | bytes 2080 | tf_op jit(solution)/shard_map/all_to_all | solution.py:255
  51.5 9.1 %collective-permute-start.8 = (bf16[256,256]{0,1:T(8,128)(2,1)}, bf16[256,256]{0,1:T(8,128)(2,1)S(1)}, u32[]{:S(2)}, u32[]{:S(2)}) collective-permute-start(bf16[256,256]{0,1:T(8,128)(2,1)} %bitcast.8), channel_id=1, source_target_pairs={{0,6},{1,7},{8,14},{9,15},{16,22},{17,23},{24,30},{25,31}} | collective-permute-start | bytes 393224 | tf_op jit(solution)/shard_map/ppermute | solution.py:272
  71.8 15.0 %collective-permute-start.11 = (bf16[256,256]{0,1:T(8,128)(2,1)}, bf16[256,256]{0,1:T(8,128)(2,1)S(1)}, u32[]{:S(2)}, u32[]{:S(2)}) collective-permute-start(bf16[256,256]{0,1:T(8,128)(2,1)} %bitcast.8), channel_id=1, source_target_pairs={{0,3},{1,4},{2,5},{3,6},{4,7},{8,11},{9,12},{10,13},{11,14},{12,15... | collective-permute-start | bytes 393224 | tf_op jit(solution)/shard_map/ppermute | solution.py:272
  86.8 4.1 collective-permute-done.11
  95.0 7.0 %collective-permute-start.13 = (bf16[256,256]{0,1:T(8,128)(2,1)}, bf16[256,256]{0,1:T(8,128)(2,1)S(1)}, u32[]{:S(2)}, u32[]{:S(2)}) collective-permute-start(bf16[256,256]{0,1:T(8,128)(2,1)} %bitcast.8), channel_id=1, source_target_pairs={{0,1},{1,2},{2,3},{3,4},{4,5},{5,6},{6,7},{8,9},{9,10},{10,11},{11... | collective-permute-start | bytes 393224 | tf_op jit(solution)/shard_map/ppermute | solution.py:272
  102.0 5.6 %collective-permute-done.13 = bf16[256,256]{0,1:T(8,128)(2,1)S(1)} collective-permute-done((bf16[256,256]{0,1:T(8,128)(2,1)}, bf16[256,256]{0,1:T(8,128)(2,1)S(1)}, u32[]{:S(2)}, u32[]{:S(2)}) %collective-permute-start.13) | collective-permute-done | bytes 131104 | tf_op jit(solution)/shard_map/ppermute | solution.py:272
  107.6 3.6 collective-permute-start.4
  116.2 3.4 collective-permute-start.6
  140.1 4.2 collective-permute-start.24
  148.2 25.8 %shard_map.136 = bf16[1,4096,128]{2,1,0:T(8,128)(2,1)} custom-call(s32[3]{0:T(128)} %get-tuple-element.35.scal_ref, bf16[2,4096,128]{2,1,0:T(8,128)(2,1)} %reshape.179.q_ref, bf16[8,512,256]{2,1,0:T(8,128)(2,1)} %copy.48.ck_ref, bf16[8,136,512]{2,1,0:T(8,128)(2,1)} %concatenate.21.cv_ref, bf16[8,256,256]{2,1,0:T(8,128)(2,1)} %copy.49.nk_ref, ...), custom_call_target="tpu_custom_call" | custom-call | tf_op jit(solution)/shard_map/pallas_call | solution.py:196
  186.9 3.2 collective-permute-done.15
  190.9 4.9 collective-permute-done.16
  196.5 18.5 %collective-permute-done.17 = bf16[512,256]{0,1:T(8,128)(2,1)S(1)} collective-permute-done((bf16[512,256]{0,1:T(8,128)(2,1)S(1)}, bf16[512,256]{0,1:T(8,128)(2,1)S(1)}, u32[]{:S(2)}, u32[]{:S(2)}) %collective-permute-start.17) | collective-permute-done | bytes 262176 | tf_op jit(solution)/shard_map/ppermute | solution.py:267
  215.7 3.9 collective-permute-done.18
  227.6 38.8 %shard_map.137 = bf16[1,4096,128]{2,1,0:T(8,128)(2,1)} custom-call(s32[3]{0:T(128)} %get-tuple-element.36.scal_ref, bf16[2,4096,128]{2,1,0:T(8,128)(2,1)} %reshape.179.q_ref, bf16[8,512,256]{2,1,0:T(8,128)(2,1)} %copy.50.ck_ref, bf16[8,136,512]{2,1,0:T(8,128)(2,1)} %concatenate.23.cv_ref, bf16[8,256,256]{2,1,0:T(8,128)(2,1)} %copy.51.nk_ref, ...), custom_call_target="tpu_custom_call" | custom-call | tf_op jit(solution)/shard_map/pallas_call | solution.py:196
  270.2 10.2 %convolution_convert_fusion.1 = bf16[512,2048]{1,0:T(8,128)(2,1)S(1)} fusion(bf16[512,512]{1,0:T(8,128)(2,1)S(1)} %copy-done.3, bf16[512,2048]{1,0:T(8,128)(2,1)} %bitcast.123, bf16[512,2048]{1,0:T(8,128)(2,1)} %reshape.180, bf16[2048,2048]{1,0:T(8,128)(2,1)} %param.24, f32[2048]{0:T(1024)S(1)} %copy-done.8), kind=kOutput, calls=%fused_computation.17 | convolution fusion | flops 5373952000 | bytes 15212544 | tf_op jit(solution)/shard_map/dot_general | solution.py:298
  280.4 51.8 %all_to_all.11 = bf16[32,16,2048]{2,1,0:T(8,128)(2,1)S(1)} all-to-all(bf16[32,16,2048]{2,1,0:T(8,128)(2,1)S(1)} %bitcast.103), channel_id=1, replica_groups=mesh['req'=4,'tok'=8] {'req','tok'}, dimensions={0} | all-to-all | bytes 4194304 | tf_op jit(solution)/shard_map/all_to_all | solution.py:301
  334.1 71.1 %all-gather.2.cloned.1.call-done = bf16[1024,2048]{1,0:T(8,128)(2,1)} async-done(((bf16[128,2048]{1,0:T(8,128)(2,1)}), bf16[1024,2048]{1,0:T(8,128)(2,1)}) %all-gather.2.cloned.1.call-update) | async-done | bytes 4194320 | tf_op jit(solution)/shard_map/all_gather | solution.py:321
  405.2 15.3 %convolution_convert_fusion = bf16[1024,2048]{1,0:T(8,128)(2,1)} fusion(bf16[1024,2048]{1,0:T(8,128)(2,1)} %param.30, f32[1024]{0:T(1024)S(1)} %copy-done.9, bf16[1024,2048]{1,0:T(8,128)(2,1)} %all-gather.2.cloned.1.call-done, bf16[2048,1024]{1,0:T(8,128)(2,1)} %param.28), kind=kOutput, calls=%fused_computation.16 | convolution fusion | flops 8602517504 | bytes 16781312 | tf_op jit(solution)/shard_map/dot_general | solution.py:328
  420.5 86.5 %reduce-scatter.2.cloned.1.call-done = bf16[128,2048]{1,0:T(8,128)(2,1)} async-done(((bf16[1024,2048]{1,0:T(8,128)(2,1)}), bf16[128,2048]{1,0:T(8,128)(2,1)}) %reduce-scatter.2.cloned.1.call-update) | async-done | bytes 524304 | tf_op jit(solution)/shard_map/reduce_scatter | solution.py:329
  (153 shorter events, 96.5 us)
Async XLA Ops:
  9.2 102.4 %collective-permute-start = (bf16[512,256]{0,1:T(8,128)(2,1)}, bf16[512,256]{0,1:T(8,128)(2,1)}, u32[]{:S(2)}, u32[]{:S(2)}) collective-permute-start(bf16[512,256]{0,1:T(8,128)(2,1)} %bitcast), channel_id=1, source_target_pairs={{0,7},{1,0},{2,1},{3,2},{4,3},{5,4},{6,5},{7,6},{8,15},{9,8},{10,9... | collective-permute-start | bytes 786440 | tf_op jit(solution)/shard_map/ppermute | solution.py:267
  15.2 101.0 %collective-permute-start.1 = (bf16[512,256]{0,1:T(8,128)(2,1)}, bf16[512,256]{0,1:T(8,128)(2,1)}, u32[]{:S(2)}, u32[]{:S(2)}) collective-permute-start(bf16[512,256]{0,1:T(8,128)(2,1)} %bitcast), channel_id=1, source_target_pairs={{0,6},{1,7},{2,0},{3,1},{4,2},{5,3},{6,4},{7,5},{8,14},{9,15},{10,... | collective-permute-start | bytes 786440 | tf_op jit(solution)/shard_map/ppermute | solution.py:267
  15.7 105.6 %collective-permute-start.2 = (bf16[512,256]{0,1:T(8,128)(2,1)}, bf16[512,256]{0,1:T(8,128)(2,1)}, u32[]{:S(2)}, u32[]{:S(2)}) collective-permute-start(bf16[512,256]{0,1:T(8,128)(2,1)} %bitcast), channel_id=1, source_target_pairs={{0,5},{1,6},{2,7},{3,0},{4,1},{5,2},{6,3},{7,4},{8,13},{9,14},{10,... | collective-permute-start | bytes 786440 | tf_op jit(solution)/shard_map/ppermute | solution.py:267
  15.7 107.3 %collective-permute-start.3 = (bf16[512,256]{0,1:T(8,128)(2,1)}, bf16[512,256]{0,1:T(8,128)(2,1)}, u32[]{:S(2)}, u32[]{:S(2)}) collective-permute-start(bf16[512,256]{0,1:T(8,128)(2,1)} %bitcast), channel_id=1, source_target_pairs={{0,4},{1,5},{2,6},{3,7},{4,0},{5,1},{6,2},{7,3},{8,12},{9,13},{10,... | collective-permute-start | bytes 786440 | tf_op jit(solution)/shard_map/ppermute | solution.py:267
  21.0 30.4 %collective-permute-start.7 = (bf16[256,256]{0,1:T(8,128)(2,1)}, bf16[256,256]{0,1:T(8,128)(2,1)}, u32[]{:S(2)}, u32[]{:S(2)}) collective-permute-start(bf16[256,256]{0,1:T(8,128)(2,1)} %bitcast.8), channel_id=1, source_target_pairs={{0,7},{8,15},{16,23},{24,31}} | collective-permute-start | bytes 393224 | tf_op jit(solution)/shard_map/ppermute | solution.py:272
  28.4 21.8 %all-to-all-start = ((s32[32,1,16]{2,1,0:T(1,128)}), s32[32,1,16]{2,1,0:T(1,128)S(1)}, u32[]{:S(2)}, u32[]{:S(2)}) async-start(s32[32,1,16]{2,1,0:T(1,128)} %bitcast.17), calls=%async_computation | async-start | bytes 32768 | tf_op jit(solution)/shard_map/all_to_all | solution.py:255
  30.9 374.3 %all-gather.2.cloned.1.call-start = ((), (), s32[]{:S(2)}) async-start(), calls=%async_computation.3 | async-start | bytes 4718592 | tf_op jit(solution)/shard_map/all_gather | solution.py:321
  51.5 12.2 %collective-permute-start.8 = (bf16[256,256]{0,1:T(8,128)(2,1)}, bf16[256,256]{0,1:T(8,128)(2,1)S(1)}, u32[]{:S(2)}, u32[]{:S(2)}) collective-permute-start(bf16[256,256]{0,1:T(8,128)(2,1)} %bitcast.8), channel_id=1, source_target_pairs={{0,6},{1,7},{8,14},{9,15},{16,22},{17,23},{24,30},{25,31}} | collective-permute-start | bytes 393224 | tf_op jit(solution)/shard_map/ppermute | solution.py:272
  71.8 19.1 %collective-permute-start.11 = (bf16[256,256]{0,1:T(8,128)(2,1)}, bf16[256,256]{0,1:T(8,128)(2,1)S(1)}, u32[]{:S(2)}, u32[]{:S(2)}) collective-permute-start(bf16[256,256]{0,1:T(8,128)(2,1)} %bitcast.8), channel_id=1, source_target_pairs={{0,3},{1,4},{2,5},{3,6},{4,7},{8,11},{9,12},{10,13},{11,14},{12,15... | collective-permute-start | bytes 393224 | tf_op jit(solution)/shard_map/ppermute | solution.py:272
  95.0 12.6 %collective-permute-start.13 = (bf16[256,256]{0,1:T(8,128)(2,1)}, bf16[256,256]{0,1:T(8,128)(2,1)S(1)}, u32[]{:S(2)}, u32[]{:S(2)}) collective-permute-start(bf16[256,256]{0,1:T(8,128)(2,1)} %bitcast.8), channel_id=1, source_target_pairs={{0,1},{1,2},{2,3},{3,4},{4,5},{5,6},{6,7},{8,9},{9,10},{10,11},{11... | collective-permute-start | bytes 393224 | tf_op jit(solution)/shard_map/ppermute | solution.py:272
  107.6 18.3 %collective-permute-start.4 = (bf16[512,256]{0,1:T(8,128)(2,1)}, bf16[512,256]{0,1:T(8,128)(2,1)S(1)}, u32[]{:S(2)}, u32[]{:S(2)}) collective-permute-start(bf16[512,256]{0,1:T(8,128)(2,1)} %bitcast), channel_id=1, source_target_pairs={{0,3},{1,4},{2,5},{3,6},{4,7},{5,0},{6,1},{7,2},{8,11},{9,12},{10,... | collective-permute-start | bytes 786440 | tf_op jit(solution)/shard_map/ppermute | solution.py:267
  111.6 15.0 %collective-permute-start.5 = (bf16[512,256]{0,1:T(8,128)(2,1)}, bf16[512,256]{0,1:T(8,128)(2,1)S(1)}, u32[]{:S(2)}, u32[]{:S(2)}) collective-permute-start(bf16[512,256]{0,1:T(8,128)(2,1)} %bitcast), channel_id=1, source_target_pairs={{0,2},{1,3},{2,4},{3,5},{4,6},{5,7},{6,0},{7,1},{8,10},{9,11},{10,... | collective-permute-start | bytes 786440 | tf_op jit(solution)/shard_map/ppermute | solution.py:267
  135.3 38.7 %collective-permute-start.21 = (bf16[256,256]{0,1:T(8,128)(2,1)S(1)}, bf16[256,256]{0,1:T(8,128)(2,1)S(1)}, u32[]{:S(2)}, u32[]{:S(2)}) collective-permute-start(bf16[256,256]{0,1:T(8,128)(2,1)S(1)} %bitcast.112), channel_id=1, source_target_pairs={{0,7},{8,15},{16,23},{24,31}} | collective-permute-start | bytes 393224 | tf_op jit(solution)/shard_map/ppermute | solution.py:272
  137.1 38.2 %collective-permute-start.22 = (bf16[256,256]{0,1:T(8,128)(2,1)S(1)}, bf16[256,256]{0,1:T(8,128)(2,1)S(1)}, u32[]{:S(2)}, u32[]{:S(2)}) collective-permute-start(bf16[256,256]{0,1:T(8,128)(2,1)S(1)} %bitcast.113), channel_id=1, source_target_pairs={{0,6},{1,7},{8,14},{9,15},{16,22},{17,23},{24,30},{25,31}} | collective-permute-start | bytes 393224 | tf_op jit(solution)/shard_map/ppermute | solution.py:272
  138.5 38.2 %collective-permute-start.23 = (bf16[256,256]{0,1:T(8,128)(2,1)S(1)}, bf16[256,256]{0,1:T(8,128)(2,1)S(1)}, u32[]{:S(2)}, u32[]{:S(2)}) collective-permute-start(bf16[256,256]{0,1:T(8,128)(2,1)S(1)} %bitcast.114), channel_id=1, source_target_pairs={{0,5},{1,6},{2,7},{8,13},{9,14},{10,15},{16,21},{17,22},{18,23},{2... | collective-permute-start | bytes 393224 | tf_op jit(solution)/shard_map/ppermute | solution.py:272
  140.1 36.7 %collective-permute-start.24 = (bf16[256,256]{0,1:T(8,128)(2,1)S(1)}, bf16[256,256]{0,1:T(8,128)(2,1)S(1)}, u32[]{:S(2)}, u32[]{:S(2)}) collective-permute-start(bf16[256,256]{0,1:T(8,128)(2,1)S(1)} %bitcast.115), channel_id=1, source_target_pairs={{0,4},{1,5},{2,6},{3,7},{8,12},{9,13},{10,14},{11,15},{16,20},{17,... | collective-permute-start | bytes 393224 | tf_op jit(solution)/shard_map/ppermute | solution.py:272
  144.2 32.6 %collective-permute-start.25 = (bf16[256,256]{0,1:T(8,128)(2,1)S(1)}, bf16[256,256]{0,1:T(8,128)(2,1)S(1)}, u32[]{:S(2)}, u32[]{:S(2)}) collective-permute-start(bf16[256,256]{0,1:T(8,128)(2,1)S(1)} %bitcast.116), channel_id=1, source_target_pairs={{0,3},{1,4},{2,5},{3,6},{4,7},{8,11},{9,12},{10,13},{11,14},{12,15... | collective-permute-start | bytes 393224 | tf_op jit(solution)/shard_map/ppermute | solution.py:272
  176.8 13.4 %collective-permute-start.15 = (bf16[512,256]{0,1:T(8,128)(2,1)S(1)}, bf16[512,256]{0,1:T(8,128)(2,1)S(1)}, u32[]{:S(2)}, u32[]{:S(2)}) collective-permute-start(bf16[512,256]{0,1:T(8,128)(2,1)S(1)} %bitcast.106), channel_id=1, source_target_pairs={{0,6},{1,7},{2,0},{3,1},{4,2},{5,3},{6,4},{7,5},{8,14},{9,15},{10,... | collective-permute-start | bytes 786440 | tf_op jit(solution)/shard_map/ppermute | solution.py:267
  176.9 18.9 %collective-permute-start.16 = (bf16[512,256]{0,1:T(8,128)(2,1)S(1)}, bf16[512,256]{0,1:T(8,128)(2,1)S(1)}, u32[]{:S(2)}, u32[]{:S(2)}) collective-permute-start(bf16[512,256]{0,1:T(8,128)(2,1)S(1)} %bitcast.107), channel_id=1, source_target_pairs={{0,5},{1,6},{2,7},{3,0},{4,1},{5,2},{6,3},{7,4},{8,13},{9,14},{10,... | collective-permute-start | bytes 786440 | tf_op jit(solution)/shard_map/ppermute | solution.py:267
  178.8 36.1 %collective-permute-start.17 = (bf16[512,256]{0,1:T(8,128)(2,1)S(1)}, bf16[512,256]{0,1:T(8,128)(2,1)S(1)}, u32[]{:S(2)}, u32[]{:S(2)}) collective-permute-start(bf16[512,256]{0,1:T(8,128)(2,1)S(1)} %bitcast.108), channel_id=1, source_target_pairs={{0,4},{1,5},{2,6},{3,7},{4,0},{5,1},{6,2},{7,3},{8,12},{9,13},{10,... | collective-permute-start | bytes 786440 | tf_op jit(solution)/shard_map/ppermute | solution.py:267
  181.4 38.1 %collective-permute-start.18 = (bf16[512,256]{0,1:T(8,128)(2,1)S(1)}, bf16[512,256]{0,1:T(8,128)(2,1)S(1)}, u32[]{:S(2)}, u32[]{:S(2)}) collective-permute-start(bf16[512,256]{0,1:T(8,128)(2,1)S(1)} %bitcast.109), channel_id=1, source_target_pairs={{0,3},{1,4},{2,5},{3,6},{4,7},{5,0},{6,1},{7,2},{8,11},{9,12},{10,... | collective-permute-start | bytes 786440 | tf_op jit(solution)/shard_map/ppermute | solution.py:267
  185.8 34.5 %collective-permute-start.19 = (bf16[512,256]{0,1:T(8,128)(2,1)S(1)}, bf16[512,256]{0,1:T(8,128)(2,1)S(1)}, u32[]{:S(2)}, u32[]{:S(2)}) collective-permute-start(bf16[512,256]{0,1:T(8,128)(2,1)S(1)} %bitcast.110), channel_id=1, source_target_pairs={{0,2},{1,3},{2,4},{3,5},{4,6},{5,7},{6,0},{7,1},{8,10},{9,11},{10,... | collective-permute-start | bytes 786440 | tf_op jit(solution)/shard_map/ppermute | solution.py:267
  190.1 30.8 %collective-permute-start.20 = (bf16[512,256]{0,1:T(8,128)(2,1)S(1)}, bf16[512,256]{0,1:T(8,128)(2,1)S(1)}, u32[]{:S(2)}, u32[]{:S(2)}) collective-permute-start(bf16[512,256]{0,1:T(8,128)(2,1)S(1)} %bitcast.111), channel_id=1, source_target_pairs={{0,1},{1,2},{2,3},{3,4},{4,5},{5,6},{6,7},{7,0},{8,9},{9,10},{10,1... | collective-permute-start | bytes 786440 | tf_op jit(solution)/shard_map/ppermute | solution.py:267
  334.1 172.9 %reduce-scatter.2.cloned.1.call-start = ((), (), s32[]{:S(2)}) async-start(), calls=%async_computation.4 | async-start | bytes 4718592 | tf_op jit(solution)/shard_map/reduce_scatter | solution.py:329
  (18 other events, 339.4 us)
Sparse Core Ops, SparseCore 0:
  334.2 70.9 all-gather.1
  420.6 86.3 reduce-scatter.1

commit v7 on v5

--- a/solution.py
+++ b/solution.py
@@ -264,21 +264,22 @@
     for r in range(req_dev):
         both = gathered[r].reshape(n_member, prefix_dev + slot_dev, local_kv.shape[-1])
         scal = jnp.stack([own_prefix[r], live_count[r], base]).astype(jnp.int32)
+        attended = flash_attention(
+            q_flat, r, both, scal, heads, tq, tk, prefix_dev, slot_dev
+        ).reshape(slot_dev, width)
+        hidden_r = (
+            residual[r].astype(jnp.float32)
+            + jnp.dot(attended, w_out, preferred_element_type=jnp.float32)
+            + b_out
+        ).astype(jnp.bfloat16)
         outs.append(
-            flash_attention(q_flat, r, both, scal, heads, tq, tk, prefix_dev, slot_dev)
+            jnp.dot(
+                pick[:, r * slot_dev : (r + 1) * slot_dev],
+                hidden_r,
+                preferred_element_type=jnp.float32,
+            )
         )
-    attended = jnp.concatenate(outs, axis=0)
-    attended = attended.reshape(slots, width)
-    residual_flat = residual.reshape(slots, width)
-    hidden_all = (
-        residual_flat.astype(jnp.float32)
-        + jnp.dot(attended, w_out, preferred_element_type=jnp.float32)
-        + b_out
-    ).astype(jnp.bfloat16)
-
-    send_rows = jnp.dot(pick, hidden_all, preferred_element_type=jnp.float32).astype(
-        jnp.bfloat16
-    )
+    send_rows = functools.reduce(jnp.add, outs).astype(jnp.bfloat16)
     rows_in = lax.all_to_all(
         send_rows.reshape(devices, capacity, width),
         ("req", "tok"),

time: 433 us -> 427 us (0.986)
  Pallas kernels: 58 us -> 77 us
  blocking collectives: 69.3 us -> 51.8 us
  waiting for transfers between devices: 217 us -> 208 us
  matrix products: 26 us -> 32.1 us
    pallas_call x2, Pallas kernels: 58 us -> 77 us  [flash_attention(): pl.pallas_call(kernel, grid_spec=grid_spec, out_shape=jax.ShapeDtypeStruc...]
    all_to_all x1, blocking collectives: 69.3 us -> 51.8 us  [per_device(): lax.all_to_all(send_rows.reshape(devices, capacity, width), ('req', 'tok'...]
    all_gather x1, waiting for transfers between devices: 9.78 us -> 0.01 us  [per_device(): gathered.append(lax.all_gather(mine, 'tok', axis=0, tiled=True))]
    dot_general x1 -> x2, matrix products: 10.2 us -> 16.3 us  [per_device(): jnp.dot(pick[:, r * slot_dev:(r + 1) * slot_dev], hidden_r, preferred_ele...]
  transfers between devices with their start and end apart: 5 -> 5, of which waited for: 5 -> 4; matrix products, arithmetic and copies ran while one was open for 5% -> 7% of each run, Pallas kernels for 9% -> 9%
where the time goes in v7:
time: 427 us; the launch traced here: 422 us
  waiting for transfers between devices  208 us (49%)
  Pallas kernels  77 us (18%)
  blocking collectives  51.8 us (12%)
  matrix products  32.1 us (8%)
  local copies, waits for them, and re-layouts  22.1 us (5%)
  between operations  13.8 us (3%)
  other arithmetic  10.2 us (2%)
  starting transfers between devices  7.42 us (2%)
    reduce_scatter x1, waiting for transfers between devices, per_device(): lax.psum_scatter(terms.astype(jnp.bfloat16), 'tok', scatter_dimension=0,...  86.3 us
    pallas_call x2, Pallas kernels, flash_attention(): pl.pallas_call(kernel, grid_spec=grid_spec, out_shape=jax.ShapeDtypeStruc...  77 us
    all_gather x1, waiting for transfers between devices, per_device(): lax.all_gather(normed, 'tok', axis=0, tiled=True)  71.1 us
    all_to_all x1, blocking collectives, per_device(): lax.all_to_all(send_rows.reshape(devices, capacity, width), ('req', 'tok'...  51.8 us
    all_gather x1, waiting for transfers between devices, per_device(): gathered = [lax.all_gather(local_kv[0], 'tok', axis=0, tiled=True)]  43.9 us
    dot_general x2, matrix products, per_device(): jnp.dot(pick[:, r * slot_dev:(r + 1) * slot_dev], hidden_r, preferred_ele...  16.3 us
    dot_general x1, matrix products, per_device(): jnp.dot(units.astype(jnp.bfloat16), w_down, preferred_element_type=jnp.fl...  15.2 us
  transfers between devices with their start and end apart: 5, of which 4 were waited for; matrix products, arithmetic and copies ran while one was open for 7% of the time, Pallas kernels for 9%

profile of v7, /device:TPU:0, one launch (start us, length us, event | category | flops | bytes accessed | tf_op | source)
XLA Modules:
  0.0 421.8 jit_solution(10105577722736225840)
XLA Ops:
  6.5 1.1 constant_dynamic-update-slice_fusion.1
  11.0 1.2 reduce-window.6
  13.4 7.3 %all-to-all-start = ((s32[32,1,16]{2,1,0:T(1,128)}), s32[32,1,16]{2,1,0:T(1,128)S(1)}, u32[]{:S(2)}, u32[]{:S(2)}) async-start(s32[32,1,16]{2,1,0:T(1,128)} %bitcast.2), calls=%async_computation | async-start | bytes 32768 | tf_op jit(solution)/shard_map/all_to_all | solution.py:249
  21.7 6.1 %all-to-all-done = s32[32,1,16]{2,1,0:T(1,128)S(1)} async-done(((s32[32,1,16]{2,1,0:T(1,128)}), s32[32,1,16]{2,1,0:T(1,128)S(1)}, u32[]{:S(2)}, u32[]{:S(2)}) %all-to-all-start) | async-done | bytes 2080 | tf_op jit(solution)/shard_map/all_to_all | solution.py:249
  29.1 43.9 %all-gather.9.cloned.1.call-done = bf16[1,6144,256]{2,1,0:T(8,128)(2,1)} async-done(((bf16[1,768,256]{2,1,0:T(8,128)(2,1)}), bf16[1,6144,256]{2,1,0:T(8,128)(2,1)}) %all-gather.9.cloned.1.call-update) | async-done | bytes 3145744 | tf_op jit(solution)/shard_map/all_gather | solution.py:258
  73.1 4.4 %reshape.189.q_ref = bf16[2,4096,128]{2,1,0:T(8,128)(2,1)} reshape(bf16[2,256,2048]{2,1,0:T(8,128)(2,1)} %param.14) | data formatting | bytes 4194304 | tf_op jit(solution)/shard_map/reshape | solution.py:227
  78.3 1.8 add_add_fusion.scal_ref
  80.1 2.0 add_add_fusion.1.scal_ref
  82.1 1.4 slice.59
  83.5 1.7 copy.30
  85.2 1.3 concatenate.10.cv_ref.nv_ref
  86.5 38.8 %shard_map.136 = bf16[1,4096,128]{2,1,0:T(8,128)(2,1)} custom-call(s32[3]{0:T(128)} %add_add_fusion.scal_ref, bf16[2,4096,128]{2,1,0:T(8,128)(2,1)} %reshape.189.q_ref, bf16[8,768,256]{2,1,0:T(8,128)(2,1)} %bitcast.47, bf16[8,136,768]{2,1,0:T(8,128)(2,1)} %concatenate.10.cv_ref.nv_ref, bf16[8,768,256]{2,1,0:T(8,128)(2,1)} %bitcast.48, ...), custom_call_target="tpu_custom_call" | custom-call | tf_op jit(solution)/shard_map/pallas_call | solution.py:190
  125.3 1.5 reshape.191
  126.9 8.4 %fusion.19 = f32[512,2048]{1,0:T(8,128)} fusion(bf16[256,2048]{1,0:T(8,128)(2,1)S(1)} %reshape.191, bf16[2048,2048]{1,0:T(8,128)(2,1)} %param.20, f32[2048]{0:T(1024)S(1)} %copy-done.6, bf16[2,256,2048]{2,1,0:T(8,128)(2,1)} %param.17, bf16[512,512]{1,0:T(8,128)(2,1)S(1)} %copy-done.1), kind=kOutput, calls=%fused_computation.24 | convolution fusion | flops 2686451712 | bytes 14950400 | tf_op jit(solution)/shard_map/dot_general | solution.py:276
  135.3 1.5 slice.60
  137.5 1.3 concatenate.11.cv_ref.nv_ref
  138.8 38.2 %shard_map.137 = bf16[1,4096,128]{2,1,0:T(8,128)(2,1)} custom-call(s32[3]{0:T(128)} %add_add_fusion.1.scal_ref, bf16[2,4096,128]{2,1,0:T(8,128)(2,1)} %reshape.189.q_ref, bf16[8,768,256]{2,1,0:T(8,128)(2,1)} %bitcast.51, bf16[8,136,768]{2,1,0:T(8,128)(2,1)} %concatenate.11.cv_ref.nv_ref, bf16[8,768,256]{2,1,0:T(8,128)(2,1)} %bitcast.52, ...), custom_call_target="tpu_custom_call" | custom-call | tf_op jit(solution)/shard_map/pallas_call | solution.py:190
  177.0 1.5 reshape.193
  178.5 7.9 %add_convert_fusion = bf16[512,2048]{1,0:T(8,128)(2,1)S(1)} fusion(f32[512,2048]{1,0:T(8,128)} %fusion.19, bf16[256,2048]{1,0:T(8,128)(2,1)S(1)} %reshape.193, bf16[2048,2048]{1,0:T(8,128)(2,1)} %param.20, bf16[2,256,2048]{2,1,0:T(8,128)(2,1)} %param.17, f32[2048]{0:T(1024)S(1)} %copy-done.6, bf16[512,512]{1,0:T(8,128)(2,1)} %fusion.25), kind=kOutput, calls=%fused_computation.9 | convolution fusion | flops 2688548864 | bytes 17047552 | tf_op jit(solution)/shard_map/dot_general | solution.py:276
  186.4 51.8 %all_to_all.11 = bf16[32,16,2048]{2,1,0:T(8,128)(2,1)S(1)} all-to-all(bf16[32,16,2048]{2,1,0:T(8,128)(2,1)S(1)} %bitcast.56), channel_id=1, replica_groups=mesh['req'=4,'tok'=8] {'req','tok'}, dimensions={0} | all-to-all | bytes 4194304 | tf_op jit(solution)/shard_map/all_to_all | solution.py:283
  240.2 71.1 %all-gather.7.cloned.1.call-done = bf16[1024,2048]{1,0:T(8,128)(2,1)} async-done(((bf16[128,2048]{1,0:T(8,128)(2,1)}), bf16[1024,2048]{1,0:T(8,128)(2,1)}) %all-gather.7.cloned.1.call-update) | async-done | bytes 4194320 | tf_op jit(solution)/shard_map/all_gather | solution.py:303
  311.3 15.2 %convolution_convert_fusion = bf16[1024,2048]{1,0:T(8,128)(2,1)} fusion(bf16[1024,2048]{1,0:T(8,128)(2,1)} %param.26, f32[1024]{0:T(1024)S(1)} %copy-done.7, bf16[1024,2048]{1,0:T(8,128)(2,1)} %all-gather.7.cloned.1.call-done, bf16[2048,1024]{1,0:T(8,128)(2,1)} %param.24), kind=kOutput, calls=%fused_computation.10 | convolution fusion | flops 8602517504 | bytes 16781312 | tf_op jit(solution)/shard_map/dot_general | solution.py:310
  326.5 86.3 %reduce-scatter.2.cloned.1.call-done = bf16[128,2048]{1,0:T(8,128)(2,1)} async-done(((bf16[1024,2048]{1,0:T(8,128)(2,1)}), bf16[128,2048]{1,0:T(8,128)(2,1)}) %reduce-scatter.2.cloned.1.call-update) | async-done | bytes 524304 | tf_op jit(solution)/shard_map/reduce_scatter | solution.py:311
  412.9 2.0 add_convert_fusion.1
  (55 shorter events, 10.3 us)
Async XLA Ops:
  6.5 66.5 %all-gather.9.cloned.1.call-start = ((), (), s32[]{:S(2)}) async-start(), calls=%async_computation.6 | async-start | bytes 3538944 | tf_op jit(solution)/shard_map/all_gather | solution.py:258
  7.6 69.9 %copy-start.8 = (s32[8]{0:T(128)S(1)}, s32[8]{0:T(128)}, u32[]{:S(2)}) copy-start(s32[8]{0:T(128)} %param.18) | copy-start | bytes 100
  7.6 69.9 %copy-start.2 = (s32[2,256]{1,0:T(2,128)S(1)}, s32[2,256]{1,0:T(2,128)}, u32[]{:S(2)}) copy-start(s32[2,256]{1,0:T(2,128)} %param.19) | copy-start | bytes 6148
  13.4 14.4 %all-to-all-start = ((s32[32,1,16]{2,1,0:T(1,128)}), s32[32,1,16]{2,1,0:T(1,128)S(1)}, u32[]{:S(2)}, u32[]{:S(2)}) async-start(s32[32,1,16]{2,1,0:T(1,128)} %bitcast.2), calls=%async_computation | async-start | bytes 32768 | tf_op jit(solution)/shard_map/all_to_all | solution.py:249
  20.8 114.6 %all-gather.5.cloned.1.call-start = ((), (), s32[]{:S(2)}) async-start(), calls=%async_computation.3 | async-start | bytes 3538944 | tf_op jit(solution)/shard_map/all_gather | solution.py:262
  73.0 9.1 %copy-start = (bf16[1,6144,256]{2,1,0:T(8,128)(2,1)S(1)}, bf16[1,6144,256]{2,1,0:T(8,128)(2,1)}, u32[]{:S(2)}) copy-start(bf16[1,6144,256]{2,1,0:T(8,128)(2,1)} %all-gather.9.cloned.1.call-done) | copy-start | bytes 9437188
  73.0 238.2 %all-gather.7.cloned.1.call-start = ((), (), s32[]{:S(2)}) async-start(), calls=%async_computation.4 | async-start | bytes 4718592 | tf_op jit(solution)/shard_map/all_gather | solution.py:303
  86.5 40.3 %copy-start.1 = (bf16[512,512]{1,0:T(8,128)(2,1)S(1)}, bf16[512,512]{1,0:T(8,128)(2,1)}, u32[]{:S(2)}) copy-start(bf16[512,512]{1,0:T(8,128)(2,1)} %fusion.25) | copy-start | bytes 1572868
  86.5 40.3 %copy-start.6 = (f32[2048]{0:T(1024)S(1)}, f32[2048]{0:T(1024)}, u32[]{:S(2)}) copy-start(f32[2048]{0:T(1024)} %param.21) | copy-start | bytes 24580
  186.4 52.6 %copy-start.3 = (f32[2048]{0:T(1024)S(1)}, f32[2048]{0:T(1024)}, u32[]{:S(2)}) copy-start(f32[2048]{0:T(1024)} %param.23) | copy-start | bytes 24580
  186.4 52.6 %copy-start.4 = (f32[2048]{0:T(1024)S(1)}, f32[2048]{0:T(1024)}, u32[]{:S(2)}) copy-start(f32[2048]{0:T(1024)} %param.22) | copy-start | bytes 24580
  238.2 73.0 %copy-start.7 = (f32[1024]{0:T(1024)S(1)}, f32[1024]{0:T(1024)}, u32[]{:S(2)}) copy-start(f32[1024]{0:T(1024)} %param.25) | copy-start | bytes 12292
  240.1 172.8 %reduce-scatter.2.cloned.1.call-start = ((), (), s32[]{:S(2)}) async-start(), calls=%async_computation.5 | async-start | bytes 4718592 | tf_op jit(solution)/shard_map/reduce_scatter | solution.py:311
  326.5 86.4 %copy-start.5 = (f32[2048]{0:T(1024)S(1)}, f32[2048]{0:T(1024)}, u32[]{:S(2)}) copy-start(f32[2048]{0:T(1024)} %param.27) | copy-start | bytes 24580
Sparse Core Ops, SparseCore 0:
  9.7 63.2 all-gather.8
  75.2 59.0 all-gather.4
  240.2 70.9 all-gather.6
  326.7 86.1 reduce-scatter.1

commit v8 on v5

--- a/solution.py
+++ b/solution.py
@@ -31,13 +31,15 @@
     heads,
     head_dim,
     n_cache,
+    n_req,
     scale,
 ):
+    r = pl.program_id(0)
     qi = pl.program_id(1)
     ki = pl.program_id(2)
-    prefix = scal_ref[0]
-    live = scal_ref[1]
-    base = scal_ref[2]
+    prefix = scal_ref[r]
+    live = scal_ref[n_req + r]
+    base = scal_ref[2 * n_req]
     spt = tq // heads
     tile_lo = qi * spt
     tile_live = tile_lo < live
@@ -50,8 +52,8 @@
         acc_sc[...] = jnp.zeros(acc_sc.shape, jnp.float32)
 
     def step(k_ref, v_ref, mask_fn):
-        pieces, chunk = k_ref.shape[0], k_ref.shape[1]
-        k = k_ref[...].reshape(pieces * chunk, head_dim)
+        pieces, chunk = k_ref.shape[1], k_ref.shape[2]
+        k = k_ref[0].reshape(pieces * chunk, head_dim)
         s = (
             lax.dot_general(
                 k, q_ref[0], (((1,), (1,)), ((), ())), preferred_element_type=jnp.float32
@@ -72,7 +74,7 @@
         total = alpha * acc_sc[...]
         for piece in range(pieces):
             total = total + jnp.dot(
-                v_ref[piece],
+                v_ref[0, piece],
                 pb[piece * chunk : (piece + 1) * chunk],
                 preferred_element_type=jnp.float32,
             )
@@ -121,9 +123,9 @@
         o_ref[0] = jnp.transpose(out).astype(o_ref.dtype)
 
 
-def flash_attention(q, req, both, scal, heads, tq, tk, prefix_dev, slot_dev):
+def flash_attention(q, both, scal, heads, tq, tk, prefix_dev, slot_dev):
     n_req, rows, head_dim = q.shape
-    n_member = both.shape[0]
+    n_member = both.shape[1]
     n_cache = n_member * prefix_dev // tk
     n_new = n_member * slot_dev // tk
     per_cache = tk // prefix_dev
@@ -131,22 +133,19 @@
     new_at = prefix_dev // slot_dev
     spt = tq // heads
     scale = 1.0 / math.sqrt(head_dim)
-    ones = jnp.ones((n_member, 8, both.shape[1]), jnp.bfloat16)
-    vt = jnp.concatenate([jnp.swapaxes(both[:, :, head_dim:], 1, 2), ones], axis=1)
+    ones = jnp.ones((n_req, n_member, 8, both.shape[2]), jnp.bfloat16)
+    vt = jnp.concatenate([jnp.swapaxes(both[..., head_dim:], 2, 3), ones], axis=2)
     ext = head_dim + 8
 
     def q_map(r, qi, ki, s):
-        return (req, qi, 0)
-
-    def o_map(r, qi, ki, s):
-        return (0, qi, 0)
-
-    def c_block(ki, s):
-        last = jnp.maximum((s[0] + tk - 1) // tk - 1, 0)
+        return (r, qi, 0)
+
+    def c_block(r, ki, s):
+        last = jnp.maximum((s[r] + tk - 1) // tk - 1, 0)
         return jnp.minimum(ki, last)
 
-    def n_block(qi, ki, s):
-        q_hi = s[2] + (qi + 1) * spt - 1
+    def n_block(r, qi, ki, s):
+        q_hi = s[2 * n_req] + (qi + 1) * spt - 1
         last = jnp.minimum(q_hi // tk, n_new - 1)
         return jnp.clip(ki - n_cache, 0, last)
 
@@ -157,31 +156,32 @@
         heads=heads,
         head_dim=head_dim,
         n_cache=n_cache,
+        n_req=n_req,
         scale=scale,
     )
     grid_spec = pltpu.PrefetchScalarGridSpec(
         num_scalar_prefetch=1,
-        grid=(1, rows // tq, n_cache + n_new),
+        grid=(n_req, rows // tq, n_cache + n_new),
         in_specs=[
             pl.BlockSpec((1, tq, head_dim), q_map),
             pl.BlockSpec(
-                (per_cache, prefix_dev, head_dim),
-                lambda r, qi, ki, s: (c_block(ki, s), 0, 0),
+                (1, per_cache, prefix_dev, head_dim),
+                lambda r, qi, ki, s: (r, c_block(r, ki, s), 0, 0),
             ),
             pl.BlockSpec(
-                (per_cache, ext, prefix_dev),
-                lambda r, qi, ki, s: (c_block(ki, s), 0, 0),
+                (1, per_cache, ext, prefix_dev),
+                lambda r, qi, ki, s: (r, c_block(r, ki, s), 0, 0),
             ),
             pl.BlockSpec(
-                (per_new, slot_dev, head_dim),
-                lambda r, qi, ki, s: (n_block(qi, ki, s), new_at, 0),
+                (1, per_new, slot_dev, head_dim),
+                lambda r, qi, ki, s: (r, n_block(r, qi, ki, s), new_at, 0),
             ),
             pl.BlockSpec(
-                (per_new, ext, slot_dev),
-                lambda r, qi, ki, s: (n_block(qi, ki, s), 0, new_at),
+                (1, per_new, ext, slot_dev),
+                lambda r, qi, ki, s: (r, n_block(r, qi, ki, s), 0, new_at),
             ),
         ],
-        out_specs=pl.BlockSpec((1, tq, head_dim), o_map),
+        out_specs=pl.BlockSpec((1, tq, head_dim), q_map),
         scratch_shapes=[
             pltpu.VMEM((1, tq), jnp.float32),
             pltpu.VMEM((ext, tq), jnp.float32),
@@ -190,7 +190,7 @@
     return pl.pallas_call(
         kernel,
         grid_spec=grid_spec,
-        out_shape=jax.ShapeDtypeStruct((1, rows, head_dim), jnp.bfloat16),
+        out_shape=jax.ShapeDtypeStruct((n_req, rows, head_dim), jnp.bfloat16),
     )(scal, q, both, vt, both, vt)
 
 
@@ -255,27 +255,17 @@
     ).reshape(send_slots)
     prefix_dev = cache_kv.shape[1]
     local_kv = jnp.concatenate([cache_kv, new_kv], axis=1)
-    gathered = [lax.all_gather(local_kv[0], "tok", axis=0, tiled=True)]
-    gathered[0], pick, ids_in = lax.optimization_barrier((gathered[0], pick, ids_in))
-    for r in range(1, req_dev):
-        mine, gathered[-1] = lax.optimization_barrier((local_kv[r], gathered[-1]))
-        gathered.append(lax.all_gather(mine, "tok", axis=0, tiled=True))
-    outs = []
-    for r in range(req_dev):
-        both = gathered[r].reshape(n_member, prefix_dev + slot_dev, local_kv.shape[-1])
-        scal = jnp.stack([own_prefix[r], live_count[r], base]).astype(jnp.int32)
-        outs.append(
-            flash_attention(q_flat, r, both, scal, heads, tq, tk, prefix_dev, slot_dev)
-        )
-    attended = jnp.concatenate(outs, axis=0)
+    gathered = lax.all_gather(local_kv, "tok", axis=1, tiled=True)
+    gathered, pick, ids_in = lax.optimization_barrier((gathered, pick, ids_in))
+    both = gathered.reshape(req_dev, n_member, prefix_dev + slot_dev, local_kv.shape[-1])
+    scal = jnp.concatenate([own_prefix, live_count, base[None]]).astype(jnp.int32)
+    attended = flash_attention(q_flat, both, scal, heads, tq, tk, prefix_dev, slot_dev)
     attended = attended.reshape(slots, width)
-    residual_flat = residual.reshape(slots, width)
     hidden_all = (
-        residual_flat.astype(jnp.float32)
+        residual.reshape(slots, width).astype(jnp.float32)
         + jnp.dot(attended, w_out, preferred_element_type=jnp.float32)
         + b_out
     ).astype(jnp.bfloat16)
-
     send_rows = jnp.dot(pick, hidden_all, preferred_element_type=jnp.float32).astype(
         jnp.bfloat16
     )

time: 433 us -> 435 us (level); the launches traced: 425 us -> 437 us
  waiting for transfers between devices: 217 us -> 242 us
  blocking collectives: 69.3 us -> 64.2 us
    all_gather x2 -> x1, waiting for transfers between devices: 53.6 us -> 82.8 us  [per_device(): gathered = lax.all_gather(local_kv, 'tok', axis=1, tiled=True)]
    all_to_all x1, blocking collectives: 69.3 us -> 64.2 us  [per_device(): lax.all_to_all(send_rows.reshape(devices, capacity, width), ('req', 'tok'...]
    all_to_all x1, waiting for transfers between devices: 6.14 us -> 1.71 us  [per_device(): lax.all_to_all(row_ids.reshape(devices, capacity), ('req', 'tok'), split_...]
    pallas_call x2 -> x1, Pallas kernels: 58 us -> 57.2 us  [flash_attention(): pl.pallas_call(kernel, grid_spec=grid_spec, out_shape=jax.ShapeDtypeStruc...]
  transfers between devices with their start and end apart: 5 -> 4, of which waited for: 5 -> 4; matrix products, arithmetic and copies ran while one was open for 5% -> 2% of each run, Pallas kernels for 9% -> 0%
where the time goes in v8:
time: 435 us; the launch traced here: 437 us
  waiting for transfers between devices  242 us (56%)
  blocking collectives  64.2 us (15%)
  Pallas kernels  57.2 us (13%)
  matrix products  25.1 us (6%)
  local copies, waits for them, and re-layouts  18 us (4%)
  between operations  13.2 us (3%)
  other arithmetic  10.1 us (2%)
  starting transfers between devices  7.38 us (2%)
    reduce_scatter x1, waiting for transfers between devices, per_device(): lax.psum_scatter(terms.astype(jnp.bfloat16), 'tok', scatter_dimension=0,...  86.3 us
    all_gather x1, waiting for transfers between devices, per_device(): gathered = lax.all_gather(local_kv, 'tok', axis=1, tiled=True)  82.8 us
    all_gather x1, waiting for transfers between devices, per_device(): lax.all_gather(normed, 'tok', axis=0, tiled=True)  71.2 us
    all_to_all x1, blocking collectives, per_device(): lax.all_to_all(send_rows.reshape(devices, capacity, width), ('req', 'tok'...  64.2 us
    pallas_call x1, Pallas kernels, flash_attention(): pl.pallas_call(kernel, grid_spec=grid_spec, out_shape=jax.ShapeDtypeStruc...  57.2 us
    dot_general x1, matrix products, per_device(): jnp.dot(units.astype(jnp.bfloat16), w_down, preferred_element_type=jnp.fl...  15.2 us
    dot_general x1, matrix products, per_device(): jnp.dot(pick, hidden_all, preferred_element_type=jnp.float32)  9.3 us
  transfers between devices with their start and end apart: 4, of which 4 were waited for; matrix products, arithmetic and copies ran while one was open for 2% of the time, Pallas kernels for 0%

profile of v8, /device:TPU:0, one launch (start us, length us, event | category | flops | bytes accessed | tf_op | source)
XLA Modules:
  0.0 437.2 jit_solution(5164797844688506773)
XLA Ops:
  6.5 2.2 pad_maximum_fusion
  8.8 0.7 reshape.179
  10.2 1.2 reduce-window.6
  11.9 0.7 sub.36
  12.6 7.3 %all-to-all-start = ((s32[32,1,16]{2,1,0:T(1,128)}), s32[32,1,16]{2,1,0:T(1,128)S(1)}, u32[]{:S(2)}, u32[]{:S(2)}) async-start(s32[32,1,16]{2,1,0:T(1,128)} %bitcast.1), calls=%async_computation | async-start | bytes 32768 | tf_op jit(solution)/shard_map/all_to_all | solution.py:249
  20.0 0.7 dynamic_slice.3
  20.7 0.8 fusion.28
  21.5 0.9 fusion.19
  23.1 2.3 reshape.182.q_ref
  25.4 1.7 all-to-all-done
  27.7 0.7 reduce.5
  28.5 82.8 %all-gather.3.cloned.1.call-done = bf16[2,6144,256]{2,1,0:T(8,128)(2,1)} async-done(((bf16[2,768,256]{2,1,0:T(8,128)(2,1)}), bf16[2,6144,256]{2,1,0:T(8,128)(2,1)}) %all-gather.3.cloned.1.call-update) | async-done | bytes 6291472 | tf_op jit(solution)/shard_map/all_gather | solution.py:258
  111.3 3.9 slice.13
  115.2 3.2 copy.25
  118.4 2.0 concatenate.11.cv_ref.nv_ref
  120.4 57.2 %shard_map.136 = bf16[2,4096,128]{2,1,0:T(8,128)(2,1)} custom-call(s32[5]{0:T(128)} %pad_add_fusion.scal_ref, bf16[2,4096,128]{2,1,0:T(8,128)(2,1)} %reshape.182.q_ref, bf16[2,8,768,256]{3,2,1,0:T(8,128)(2,1)} %bitcast.33, bf16[2,8,136,768]{3,2,1,0:T(8,128)(2,1)} %concatenate.11.cv_ref.nv_ref, bf16[2,8,768,256]{3,2,1,0:T(8,128)(2,1)} %bitcast.34, ...), custom_call_target="tpu_custom_call" | custom-call | tf_op jit(solution)/shard_map/pallas_call | solution.py:190
  177.6 2.9 reshape.184
  180.5 9.3 %convolution_convert_fusion.1 = bf16[512,2048]{1,0:T(8,128)(2,1)} fusion(bf16[512,512]{1,0:T(8,128)(2,1)S(1)} %copy-done.1, bf16[512,2048]{1,0:T(8,128)(2,1)} %bitcast.41, bf16[512,2048]{1,0:T(8,128)(2,1)S(1)} %reshape.184, bf16[2048,2048]{1,0:T(8,128)(2,1)} %param.20, f32[2048]{0:T(1024)S(1)} %copy-done.5), kind=kOutput, calls=%fused_computation.13 | convolution fusion | flops 5373952000 | bytes 15212544 | tf_op jit(solution)/shard_map/dot_general | solution.py:269
  189.8 64.2 %all_to_all.11 = bf16[32,16,2048]{2,1,0:T(8,128)(2,1)S(1)} all-to-all(bf16[32,16,2048]{2,1,0:T(8,128)(2,1)} %bitcast.37), channel_id=1, replica_groups=mesh['req'=4,'tok'=8] {'req','tok'}, dimensions={0} | all-to-all | bytes 4194304 | tf_op jit(solution)/shard_map/all_to_all | solution.py:272
  254.8 1.0 add_convert_fusion.1
  255.9 71.2 %all-gather.5.cloned.1.call-done = bf16[1024,2048]{1,0:T(8,128)(2,1)} async-done(((bf16[128,2048]{1,0:T(8,128)(2,1)}), bf16[1024,2048]{1,0:T(8,128)(2,1)}) %all-gather.5.cloned.1.call-update) | async-done | bytes 4194320 | tf_op jit(solution)/shard_map/all_gather | solution.py:292
  327.1 15.2 %convolution_convert_fusion = bf16[1024,2048]{1,0:T(8,128)(2,1)} fusion(bf16[1024,2048]{1,0:T(8,128)(2,1)} %param.26, f32[1024]{0:T(1024)S(1)} %copy-done.6, bf16[1024,2048]{1,0:T(8,128)(2,1)} %all-gather.5.cloned.1.call-done, bf16[2048,1024]{1,0:T(8,128)(2,1)} %param.24), kind=kOutput, calls=%fused_computation.12 | convolution fusion | flops 8602517504 | bytes 16781312 | tf_op jit(solution)/shard_map/dot_general | solution.py:299
  342.4 86.3 %reduce-scatter.2.cloned.1.call-done = bf16[128,2048]{1,0:T(8,128)(2,1)} async-done(((bf16[1024,2048]{1,0:T(8,128)(2,1)}), bf16[128,2048]{1,0:T(8,128)(2,1)}) %reduce-scatter.2.cloned.1.call-update) | async-done | bytes 524304 | tf_op jit(solution)/shard_map/reduce_scatter | solution.py:300
  428.6 2.0 add_convert_fusion
  (38 shorter events, 3.5 us)
Async XLA Ops:
  6.5 16.5 %copy-start = (bf16[2,256,2048]{2,1,0:T(8,128)(2,1)S(1)}, bf16[2,256,2048]{2,1,0:T(8,128)(2,1)}, u32[]{:S(2)}) copy-start(bf16[2,256,2048]{2,1,0:T(8,128)(2,1)} %param.14) | copy-start | bytes 6291460
  6.5 104.8 %all-gather.3.cloned.1.call-start = ((), (), s32[]{:S(2)}) async-start(), calls=%async_computation.3 | async-start | bytes 7077888 | tf_op jit(solution)/shard_map/all_gather | solution.py:258
  12.6 14.5 %all-to-all-start = ((s32[32,1,16]{2,1,0:T(1,128)}), s32[32,1,16]{2,1,0:T(1,128)S(1)}, u32[]{:S(2)}, u32[]{:S(2)}) async-start(s32[32,1,16]{2,1,0:T(1,128)} %bitcast.1), calls=%async_computation | async-start | bytes 32768 | tf_op jit(solution)/shard_map/all_to_all | solution.py:249
  19.9 307.1 %all-gather.5.cloned.1.call-start = ((), (), s32[]{:S(2)}) async-start(), calls=%async_computation.4 | async-start | bytes 4718592 | tf_op jit(solution)/shard_map/all_gather | solution.py:292
  177.6 2.9 copy-start.1
  177.6 2.9 copy-start.5
  189.8 65.0 %copy-start.2 = (f32[2048]{0:T(1024)S(1)}, f32[2048]{0:T(1024)}, u32[]{:S(2)}) copy-start(f32[2048]{0:T(1024)} %param.23) | copy-start | bytes 24580
  189.8 65.0 %copy-start.3 = (f32[2048]{0:T(1024)S(1)}, f32[2048]{0:T(1024)}, u32[]{:S(2)}) copy-start(f32[2048]{0:T(1024)} %param.22) | copy-start | bytes 24580
  254.0 73.1 %copy-start.6 = (f32[1024]{0:T(1024)S(1)}, f32[1024]{0:T(1024)}, u32[]{:S(2)}) copy-start(f32[1024]{0:T(1024)} %param.25) | copy-start | bytes 12292
  255.9 172.8 %reduce-scatter.2.cloned.1.call-start = ((), (), s32[]{:S(2)}) async-start(), calls=%async_computation.5 | async-start | bytes 4718592 | tf_op jit(solution)/shard_map/reduce_scatter | solution.py:300
  342.3 86.3 %copy-start.4 = (f32[2048]{0:T(1024)S(1)}, f32[2048]{0:T(1024)}, u32[]{:S(2)}) copy-start(f32[2048]{0:T(1024)} %param.27) | copy-start | bytes 24580
Sparse Core Ops, SparseCore 0:
  9.6 101.7 all-gather.2
  256.0 71.0 all-gather.4
  342.5 86.1 reduce-scatter.1

commit v9 on v7

--- a/solution.py
+++ b/solution.py
@@ -256,14 +256,20 @@
     prefix_dev = cache_kv.shape[1]
     local_kv = jnp.concatenate([cache_kv, new_kv], axis=1)
     gathered = [lax.all_gather(local_kv[0], "tok", axis=0, tiled=True)]
-    gathered[0], pick, ids_in = lax.optimization_barrier((gathered[0], pick, ids_in))
+    scals = [
+        jnp.stack([own_prefix[r], live_count[r], base]).astype(jnp.int32)
+        for r in range(req_dev)
+    ]
+    gathered[0], pick, ids_in, q_flat, scals = lax.optimization_barrier(
+        (gathered[0], pick, ids_in, q_flat, scals)
+    )
     for r in range(1, req_dev):
         mine, gathered[-1] = lax.optimization_barrier((local_kv[r], gathered[-1]))
         gathered.append(lax.all_gather(mine, "tok", axis=0, tiled=True))
     outs = []
     for r in range(req_dev):
         both = gathered[r].reshape(n_member, prefix_dev + slot_dev, local_kv.shape[-1])
-        scal = jnp.stack([own_prefix[r], live_count[r], base]).astype(jnp.int32)
+        scal = scals[r]
         attended = flash_attention(
             q_flat, r, both, scal, heads, tq, tk, prefix_dev, slot_dev
         ).reshape(slot_dev, width)

time: 427 us -> 426 us (level)
  Pallas kernels: 77 us -> 52.1 us
  blocking collectives: 51.8 us -> 68.2 us
  waiting for transfers between devices: 208 us -> 214 us
    pallas_call x2, Pallas kernels: 77 us -> 52.1 us  [flash_attention(): pl.pallas_call(kernel, grid_spec=grid_spec, out_shape=jax.ShapeDtypeStruc...]
    all_to_all x1, blocking collectives: 51.8 us -> 68.2 us  [per_device(): lax.all_to_all(send_rows.reshape(devices, capacity, width), ('req', 'tok'...]
    all_gather x1, waiting for transfers between devices: 0.01 us -> 15.1 us  [per_device(): gathered.append(lax.all_gather(mine, 'tok', axis=0, tiled=True))]
    all_to_all x1, waiting for transfers between devices: 6.14 us -> 0.01 us  [per_device(): lax.all_to_all(row_ids.reshape(devices, capacity), ('req', 'tok'), split_...]
  transfers between devices with their start and end apart: 5 -> 5, of which waited for: 4 -> 4; matrix products, arithmetic and copies ran while one was open for 7% -> 7% of each run, Pallas kernels for 9% -> 8%
where the time goes in v9:
time: 426 us; the launch traced here: 419 us
  waiting for transfers between devices  214 us (50%)
  blocking collectives  68.2 us (16%)
  Pallas kernels  52.1 us (12%)
  matrix products  32.1 us (8%)
  local copies, waits for them, and re-layouts  20.5 us (5%)
  between operations  13.7 us (3%)
  other arithmetic  10.3 us (2%)
  starting transfers between devices  7.42 us (2%)
    reduce_scatter x1, waiting for transfers between devices, per_device(): lax.psum_scatter(terms.astype(jnp.bfloat16), 'tok', scatter_dimension=0,...  86.3 us
    all_gather x1, waiting for transfers between devices, per_device(): lax.all_gather(normed, 'tok', axis=0, tiled=True)  71.2 us
    all_to_all x1, blocking collectives, per_device(): lax.all_to_all(send_rows.reshape(devices, capacity, width), ('req', 'tok'...  68.2 us
    pallas_call x2, Pallas kernels, flash_attention(): pl.pallas_call(kernel, grid_spec=grid_spec, out_shape=jax.ShapeDtypeStruc...  52.1 us
    all_gather x1, waiting for transfers between devices, per_device(): gathered = [lax.all_gather(local_kv[0], 'tok', axis=0, tiled=True)]  41.7 us
    dot_general x2, matrix products, per_device(): jnp.dot(pick[:, r * slot_dev:(r + 1) * slot_dev], hidden_r, preferred_ele...  16.3 us
    dot_general x1, matrix products, per_device(): jnp.dot(units.astype(jnp.bfloat16), w_down, preferred_element_type=jnp.fl...  15.3 us
    all_gather x1, waiting for transfers between devices, per_device(): gathered.append(lax.all_gather(mine, 'tok', axis=0, tiled=True))  15.1 us
  transfers between devices with their start and end apart: 5, of which 4 were waited for; matrix products, arithmetic and copies ran while one was open for 7% of the time, Pallas kernels for 8%

profile of v9, /device:TPU:0, one launch (start us, length us, event | category | flops | bytes accessed | tf_op | source)
XLA Modules:
  0.0 418.8 jit_solution(9275362684626383619)
XLA Ops:
  6.5 1.2 constant_dynamic-update-slice_fusion.1
  7.8 1.0 constant_dynamic-update-slice_fusion
  11.1 1.2 reduce-window.6
  13.6 7.3 %all-to-all-start = ((s32[32,1,16]{2,1,0:T(1,128)}), s32[32,1,16]{2,1,0:T(1,128)S(1)}, u32[]{:S(2)}, u32[]{:S(2)}) async-start(s32[32,1,16]{2,1,0:T(1,128)} %bitcast.2), calls=%async_computation | async-start | bytes 32768 | tf_op jit(solution)/shard_map/all_to_all | solution.py:249
  24.6 3.1 add_add_fusion
  27.8 2.4 reshape.189.q_ref
  31.4 41.7 %all-gather.9.cloned.1.call-done = bf16[1,6144,256]{2,1,0:T(8,128)(2,1)} async-done(((bf16[1,768,256]{2,1,0:T(8,128)(2,1)}), bf16[1,6144,256]{2,1,0:T(8,128)(2,1)}) %all-gather.9.cloned.1.call-update) | async-done | bytes 3145744 | tf_op jit(solution)/shard_map/all_gather | solution.py:258
  73.2 1.5 slice.59
  75.4 1.3 concatenate.10.cv_ref.nv_ref
  76.7 32.5 %shard_map.136 = bf16[1,4096,128]{2,1,0:T(8,128)(2,1)} custom-call(s32[3]{0:T(128)} %get-tuple-element.15.scal_ref, bf16[2,4096,128]{2,1,0:T(8,128)(2,1)} %reshape.189.q_ref, bf16[8,768,256]{2,1,0:T(8,128)(2,1)} %bitcast.48, bf16[8,136,768]{2,1,0:T(8,128)(2,1)} %concatenate.10.cv_ref.nv_ref, bf16[8,768,256]{2,1,0:T(8,128)(2,1)} %bitcast.49, ...), custom_call_target="tpu_custom_call" | custom-call | tf_op jit(solution)/shard_map/pallas_call | solution.py:190
  109.3 1.5 reshape.191
  110.8 8.5 %fusion.19 = f32[512,2048]{1,0:T(8,128)} fusion(bf16[256,2048]{1,0:T(8,128)(2,1)S(1)} %reshape.191, bf16[2048,2048]{1,0:T(8,128)(2,1)} %param.20, f32[2048]{0:T(1024)S(1)} %copy-done.5, bf16[2,256,2048]{2,1,0:T(8,128)(2,1)} %param.17, bf16[512,512]{1,0:T(8,128)(2,1)S(1)} %copy-done.1), kind=kOutput, calls=%fused_computation.24 | convolution fusion | flops 2686451712 | bytes 14950400 | tf_op jit(solution)/shard_map/dot_general | solution.py:282
  119.3 15.1 %all-gather.5.cloned.1.call-done = bf16[6144,256]{1,0:T(8,128)(2,1)} async-done(((bf16[768,256]{1,0:T(8,128)(2,1)}), bf16[6144,256]{1,0:T(8,128)(2,1)}) %all-gather.5.cloned.1.call-update) | async-done | bytes 3145744 | tf_op jit(solution)/shard_map/all_gather | solution.py:268
  134.4 1.5 slice.60
  136.7 1.3 concatenate.11.cv_ref.nv_ref
  138.0 19.6 %shard_map.137 = bf16[1,4096,128]{2,1,0:T(8,128)(2,1)} custom-call(s32[3]{0:T(128)} %get-tuple-element.19.scal_ref, bf16[2,4096,128]{2,1,0:T(8,128)(2,1)} %reshape.189.q_ref, bf16[8,768,256]{2,1,0:T(8,128)(2,1)} %bitcast.51, bf16[8,136,768]{2,1,0:T(8,128)(2,1)} %concatenate.11.cv_ref.nv_ref, bf16[8,768,256]{2,1,0:T(8,128)(2,1)} %bitcast.52, ...), custom_call_target="tpu_custom_call" | custom-call | tf_op jit(solution)/shard_map/pallas_call | solution.py:190
  157.5 1.5 reshape.193
  159.0 7.9 %add_convert_fusion = bf16[512,2048]{1,0:T(8,128)(2,1)S(1)} fusion(f32[512,2048]{1,0:T(8,128)} %fusion.19, bf16[256,2048]{1,0:T(8,128)(2,1)S(1)} %reshape.193, bf16[2048,2048]{1,0:T(8,128)(2,1)} %param.20, bf16[2,256,2048]{2,1,0:T(8,128)(2,1)} %param.17, f32[2048]{0:T(1024)S(1)} %copy-done.5, bf16[512,512]{1,0:T(8,128)(2,1)} %fusion.25), kind=kOutput, calls=%fused_computation.9 | convolution fusion | flops 2688548864 | bytes 17047552 | tf_op jit(solution)/shard_map/dot_general | solution.py:282
  166.9 68.2 %all_to_all.11 = bf16[32,16,2048]{2,1,0:T(8,128)(2,1)S(1)} all-to-all(bf16[32,16,2048]{2,1,0:T(8,128)(2,1)S(1)} %bitcast.56), channel_id=1, replica_groups=mesh['req'=4,'tok'=8] {'req','tok'}, dimensions={0} | all-to-all | bytes 4194304 | tf_op jit(solution)/shard_map/all_to_all | solution.py:289
  236.0 1.0 add_convert_fusion.2
  237.1 71.2 %all-gather.7.cloned.1.call-done = bf16[1024,2048]{1,0:T(8,128)(2,1)} async-done(((bf16[128,2048]{1,0:T(8,128)(2,1)}), bf16[1024,2048]{1,0:T(8,128)(2,1)}) %all-gather.7.cloned.1.call-update) | async-done | bytes 4194320 | tf_op jit(solution)/shard_map/all_gather | solution.py:309
  308.3 15.3 %convolution_convert_fusion = bf16[1024,2048]{1,0:T(8,128)(2,1)} fusion(bf16[1024,2048]{1,0:T(8,128)(2,1)} %param.26, f32[1024]{0:T(1024)S(1)} %copy-done.6, bf16[1024,2048]{1,0:T(8,128)(2,1)} %all-gather.7.cloned.1.call-done, bf16[2048,1024]{1,0:T(8,128)(2,1)} %param.24), kind=kOutput, calls=%fused_computation.10 | convolution fusion | flops 8602517504 | bytes 16781312 | tf_op jit(solution)/shard_map/dot_general | solution.py:316
  323.5 86.3 %reduce-scatter.2.cloned.1.call-done = bf16[128,2048]{1,0:T(8,128)(2,1)} async-done(((bf16[1024,2048]{1,0:T(8,128)(2,1)}), bf16[128,2048]{1,0:T(8,128)(2,1)}) %reduce-scatter.2.cloned.1.call-update) | async-done | bytes 524304 | tf_op jit(solution)/shard_map/reduce_scatter | solution.py:317
  409.9 2.0 add_convert_fusion.1
  (51 shorter events, 10.9 us)
Async XLA Ops:
  6.5 21.3 %copy-start = (bf16[2,256,2048]{2,1,0:T(8,128)(2,1)S(1)}, bf16[2,256,2048]{2,1,0:T(8,128)(2,1)}, u32[]{:S(2)}) copy-start(bf16[2,256,2048]{2,1,0:T(8,128)(2,1)} %param.14) | copy-start | bytes 6291460
  6.5 66.6 %all-gather.9.cloned.1.call-start = ((), (), s32[]{:S(2)}) async-start(), calls=%async_computation.6 | async-start | bytes 3538944 | tf_op jit(solution)/shard_map/all_gather | solution.py:258
  13.6 16.6 %all-to-all-start = ((s32[32,1,16]{2,1,0:T(1,128)}), s32[32,1,16]{2,1,0:T(1,128)S(1)}, u32[]{:S(2)}, u32[]{:S(2)}) async-start(s32[32,1,16]{2,1,0:T(1,128)} %bitcast.2), calls=%async_computation | async-start | bytes 32768 | tf_op jit(solution)/shard_map/all_to_all | solution.py:249
  20.9 113.5 %all-gather.5.cloned.1.call-start = ((), (), s32[]{:S(2)}) async-start(), calls=%async_computation.3 | async-start | bytes 3538944 | tf_op jit(solution)/shard_map/all_gather | solution.py:268
  73.2 235.1 %all-gather.7.cloned.1.call-start = ((), (), s32[]{:S(2)}) async-start(), calls=%async_computation.4 | async-start | bytes 4718592 | tf_op jit(solution)/shard_map/all_gather | solution.py:309
  76.7 34.1 %copy-start.1 = (bf16[512,512]{1,0:T(8,128)(2,1)S(1)}, bf16[512,512]{1,0:T(8,128)(2,1)}, u32[]{:S(2)}) copy-start(bf16[512,512]{1,0:T(8,128)(2,1)} %fusion.25) | copy-start | bytes 1572868
  76.7 34.1 %copy-start.5 = (f32[2048]{0:T(1024)S(1)}, f32[2048]{0:T(1024)}, u32[]{:S(2)}) copy-start(f32[2048]{0:T(1024)} %param.21) | copy-start | bytes 24580
  166.9 69.0 %copy-start.2 = (f32[2048]{0:T(1024)S(1)}, f32[2048]{0:T(1024)}, u32[]{:S(2)}) copy-start(f32[2048]{0:T(1024)} %param.23) | copy-start | bytes 24580
  166.9 69.0 %copy-start.3 = (f32[2048]{0:T(1024)S(1)}, f32[2048]{0:T(1024)}, u32[]{:S(2)}) copy-start(f32[2048]{0:T(1024)} %param.22) | copy-start | bytes 24580
  235.1 73.1 %copy-start.6 = (f32[1024]{0:T(1024)S(1)}, f32[1024]{0:T(1024)}, u32[]{:S(2)}) copy-start(f32[1024]{0:T(1024)} %param.25) | copy-start | bytes 12292
  237.0 172.8 %reduce-scatter.2.cloned.1.call-start = ((), (), s32[]{:S(2)}) async-start(), calls=%async_computation.5 | async-start | bytes 4718592 | tf_op jit(solution)/shard_map/reduce_scatter | solution.py:317
  323.5 86.3 %copy-start.4 = (f32[2048]{0:T(1024)S(1)}, f32[2048]{0:T(1024)}, u32[]{:S(2)}) copy-start(f32[2048]{0:T(1024)} %param.27) | copy-start | bytes 24580
Sparse Core Ops, SparseCore 0:
  9.9 63.2 all-gather.8
  75.3 59.0 all-gather.4
  237.1 71.0 all-gather.6
  323.7 86.1 reduce-scatter.1
